TPU v7x, 256 devices: a whole 4x4x8 slice. The times are simulated.
256 devices in a mesh: row: 16 (over x_lo, z), col: 16 (over x_hi, y, core).
Axes of the slice: x: 4 (x_hi: 2, x_lo: 2; x = x_hi * 2 + x_lo), y: 4, z: 8, core: 2. Of those that a mesh axis runs over, the one named last changes fastest.
Arguments:
- sp2_branch: int32 [3], replicated, may hold values from 0 to 1, as said below
- p0_occupancy: int32 [32, 32], replicated, may hold values from 0 to 1, as said below
- p1_occupancy: int32 [32, 32], replicated, may hold values from 0 to 1, as said below
- p0_columns: bfloat16 [73728, 512], P('col'), as said below
- p1_tiles: bfloat16 [3, 8192, 8192], P(None, 'row', 'col'), may hold values from -6 to 6, as said below
Outputs:
- p1_next: bfloat16 [3, 8192, 8192], P(None, 'row', 'col')
Inputs may be any that keep to these rules, and one draw needn't show every extreme that they name: `sp2_branch`: both values occur among the displacements. `p0_occupancy`: symmetric; every diagonal block is 1; blocks more than 8 apart around the circle of 32 blocks are 0. `p1_occupancy`: symmetric. `p0_columns`: the strips describe one symmetric matrix: a stored entry at row u and column v equals the stored entry at row v and column u; blocks more than 8 apart around the circle are zero. `p1_tiles`: each displacement's matrix is symmetric.
All inputs are finite; a program needn't handle non-finite values.
Results may differ from a plain program's by a relative error of at most 0.001.
Values may be sent and summed in bfloat16 or wider, within the bound.
No kernel may reach another device: no remote copies, remote signals or barrier semaphores. Data moves between devices by JAX's collectives and lax.ppermute only.
A program may use at most 192 MiB of HBM per device.

v0:
```python
import jax
import jax.numpy as jnp
from jax import lax
from jax.sharding import PartitionSpec as P

BLK = 256


def from_behind(array, axis, by):
    length = lax.axis_size(axis)
    return lax.ppermute(array, axis, [(i, (i + by) % length) for i in range(length)])


def broadcast(array, axis, root):
    mine = lax.axis_index(axis) == root
    return lax.psum(jnp.where(mine, array, jnp.zeros_like(array)), axis)


def mask_blocks(values, occupancy):
    leading = values.shape[:-2]
    row_blocks = values.shape[-2] // BLK
    col_blocks = values.shape[-1] // BLK
    shaped = values.reshape(leading + (row_blocks, BLK, col_blocks, BLK))
    weight = occupancy.astype(values.dtype)[:, None, :, None]
    return (shaped * weight).reshape(values.shape)


def right_product(left_op, right_op):
    return jnp.einsum("drc,ck->drk", left_op, right_op, preferred_element_type=jnp.float32)


def left_product(left_op, right_op):
    return jnp.einsum("kr,dkc->drc", left_op, right_op, preferred_element_type=jnp.float32)


def column_term(summed, incoming, factor):
    return summed + right_product(incoming, factor)


def row_term(summed, incoming, factor):
    return summed + left_product(factor, incoming)


def col_move(values, distance):
    return from_behind(values, "col", distance)


def row_move(values, distance):
    return from_behind(values, "row", distance)


def body(sp2_branch, p0_occupancy, p1_occupancy, p0_columns, p1_tiles):
    col_count = lax.axis_size("col")
    col_width = p0_columns.shape[1]
    row_height = p1_tiles.shape[1]
    col_blocks = col_width // BLK
    row_blocks = row_height // BLK
    strip_blocks = p0_columns.shape[0] // BLK
    band_half = (strip_blocks - col_blocks) // 2
    all_blocks = col_blocks * col_count
    col_span = band_half // col_blocks
    row_span = band_half // row_blocks
    row_at = lax.axis_index("row")
    col_at = lax.axis_index("col")
    own_occ = lax.dynamic_slice(
        p1_occupancy, (row_at * row_blocks, col_at * col_blocks), (row_blocks, col_blocks)
    )
    p1_local = mask_blocks(p1_tiles, own_occ)
    tripled = jnp.concatenate([p0_occupancy, p0_occupancy, p0_occupancy], axis=0)
    strip_occ = lax.dynamic_slice(
        tripled,
        (col_at * col_blocks - band_half + all_blocks, col_at * col_blocks),
        (strip_blocks, col_blocks),
    )
    strip_local = mask_blocks(p0_columns, strip_occ)

    def col_add(summed, incoming, distance):
        factor = strip_local[
            (distance + col_span) * col_width : (distance + col_span + 1) * col_width, :
        ]
        return column_term(summed, incoming, factor)

    summed_col = jnp.zeros(p1_local.shape, jnp.float32)
    summed_col = col_add(summed_col, p1_local, 0)
    moving = p1_local
    for distance in range(1, col_span + 1):
        moving = col_move(moving, 1)
        summed_col = col_add(summed_col, moving, -distance)
    moving = from_behind(moving, "col", -2 * col_span)
    summed_col = col_add(summed_col, moving, col_span)
    for distance in range(col_span - 1, 0, -1):
        moving = col_move(moving, 1)
        summed_col = col_add(summed_col, moving, distance)
    owner_col = row_at * row_blocks // col_blocks
    shared = broadcast(strip_local, "col", owner_col)

    def row_add(summed, incoming, distance):
        factor = shared[
            (distance + row_span) * row_height : (distance + row_span + 1) * row_height, :
        ]
        return row_term(summed, incoming, factor)

    summed_row = jnp.zeros(p1_local.shape, jnp.float32)
    summed_row = row_add(summed_row, p1_local, 0)
    moving = p1_local
    for distance in range(1, row_span + 1):
        moving = row_move(moving, 1)
        summed_row = row_add(summed_row, moving, -distance)
    moving = from_behind(moving, "row", -2 * row_span)
    summed_row = row_add(summed_row, moving, row_span)
    for distance in range(row_span - 1, 0, -1):
        moving = row_move(moving, 1)
        summed_row = row_add(summed_row, moving, distance)
    bracket = summed_col + summed_row
    squared = (sp2_branch == 1)[:, None, None]
    chosen = jnp.where(squared, bracket, 2.0 * p1_local.astype(jnp.float32) - bracket)
    return mask_blocks(chosen, own_occ).astype(jnp.bfloat16)


def solution(mesh):
    in_specs = (P(), P(), P(), P("col", None), P(None, "row", "col"))
    out_specs = P(None, "row", "col")
    return jax.shard_map(body, mesh=mesh, in_specs=in_specs, out_specs=out_specs, check_vma=False)
```

profile of v0, /device:TPU:2, one launch (start us, length us, event | category | flops | bytes accessed | tf_op | source)
XLA Modules:
  0.0 573.2 jit_solution(15829006812120409035)
XLA Ops:
  6.5 0.8 dynamic-slice_convert_fusion
  7.3 0.3 mul.56
  7.7 0.1 copy.64
  7.8 1.6 broadcast_multiply_fusion.1
  9.4 2.0 collective-permute-start.8
  11.4 38.3 %collective-permute-done.8 = bf16[3,512,512]{2,1,0:T(8,128)(2,1)S(1)} collective-permute-done((bf16[3,512,512]{2,1,0:T(8,128)(2,1)S(1)}, bf16[3,512,512]{2,1,0:T(8,128)(2,1)S(1)}, u32[]{:S(2)}, u32[]{:S(2)}) %collective-permute-start.8) | collective-permute-done | bytes 1572896 | tf_op jit(solution)/shard_map/ppermute | solution.py:11
  49.7 52.7 %collective-permute-done = bf16[3,512,512]{2,1,0:T(8,128)(2,1)} collective-permute-done((bf16[3,512,512]{2,1,0:T(8,128)(2,1)S(1)}, bf16[3,512,512]{2,1,0:T(8,128)(2,1)}, u32[]{:S(2)}, u32[]{:S(2)}) %collective-permute-start) | collective-permute-done | bytes 1572896 | tf_op jit(solution)/shard_map/ppermute | solution.py:11
  102.3 0.0 collective-permute-start.1
  102.3 0.1 copy.24
  102.4 0.1 fusion.12
  102.5 0.1 copy.27
  102.6 2.5 mul.60
  105.1 0.0 slice-start
  105.1 0.0 slice-start.1
  105.2 1.0 copy.65
  106.1 0.1 collective-permute-start.10
  106.2 53.6 %collective-permute-done.1 = bf16[3,512,512]{2,1,0:T(8,128)(2,1)} collective-permute-done((bf16[3,512,512]{2,1,0:T(8,128)(2,1)}, bf16[3,512,512]{2,1,0:T(8,128)(2,1)}, u32[]{:S(2)}, u32[]{:S(2)}) %collective-permute-start.1) | collective-permute-done | bytes 1572896 | tf_op jit(solution)/shard_map/ppermute | solution.py:11
  159.8 2.7 multiply_select_fusion
  162.5 0.0 all-reduce.2.cloned.1.call-update
  162.5 0.1 collective-permute-start.11
  162.6 63.5 %collective-permute-done.2 = bf16[3,512,512]{2,1,0:T(8,128)(2,1)S(1)} collective-permute-done((bf16[3,512,512]{2,1,0:T(8,128)(2,1)}, bf16[3,512,512]{2,1,0:T(8,128)(2,1)S(1)}, u32[]{:S(2)}, u32[]{:S(2)}) %collective-permute-start.2) | collective-permute-done | bytes 1572896 | tf_op jit(solution)/shard_map/ppermute | solution.py:11
  226.1 0.0 collective-permute-start.3
  226.1 8.0 %reshape.24 = bf16[18,256,2,256]{3,2,1,0:T(2,128)(2,1)} reshape(bf16[4608,512]{1,0:T(8,128)(2,1)} %param.8) | data formatting | bytes 9437184 | tf_op jit(solution)/shard_map/reshape | solution.py:23
  234.1 0.5 collective-permute-start.12
  234.6 41.9 %collective-permute-done.3 = bf16[3,512,512]{2,1,0:T(8,128)(2,1)} collective-permute-done((bf16[3,512,512]{2,1,0:T(8,128)(2,1)S(1)}, bf16[3,512,512]{2,1,0:T(8,128)(2,1)}, u32[]{:S(2)}, u32[]{:S(2)}) %collective-permute-start.3) | collective-permute-done | bytes 1572896 | tf_op jit(solution)/shard_map/ppermute | solution.py:11
  276.5 2.7 collective-permute-start.4
  279.1 8.6 %broadcast_multiply_fusion = bf16[18,256,2,256]{3,2,1,0:T(2,128)(2,1)} fusion(bf16[18,256,2,256]{3,2,1,0:T(2,128)(2,1)} %reshape.24, bf16[18,2]{1,0:T(8,128)(2,1)S(1)} %copy.27), kind=kLoop, calls=%fused_computation.5 | loop fusion | flops 2359296 | bytes 9437256 | tf_op jit(solution)/shard_map/mul | solution.py:25
  287.8 0.3 mul.66
  288.1 0.1 copy.66
  288.2 6.1 %fusion.13 = (bf16[2,256,2,256]{3,2,1,0:T(2,128)(2,1)S(1)}, bf16[2,256,2,256]{3,2,1,0:T(2,128)(2,1)}, bf16[2,256,2,256]{3,2,1,0:T(2,128)(2,1)}, bf16[2,256,2,256...) fusion(bf16[18,256,2,256]{3,2,1,0:T(2,128)(2,1)} %broadcast_mul, ...), kind=kLoop, calls=%fused_computation.33 | loop fusion | bytes 9437184 | tf_op jit(solution)/shard_map/slice | solution.py:78
  294.3 1.1 reshape.26
  295.4 1.4 reshape.33
  296.8 2.2 reshape.32
  299.0 2.2 reshape.31
  301.2 2.2 reshape.30
  303.3 2.2 reshape.29
  305.5 2.2 reshape.28
  307.7 2.2 reshape.27
  309.9 2.2 reshape.25
  312.1 3.8 fusion.14
  315.8 7.7 %collective-permute-done.4 = bf16[3,512,512]{2,1,0:T(8,128)(2,1)} collective-permute-done((bf16[3,512,512]{2,1,0:T(8,128)(2,1)}, bf16[3,512,512]{2,1,0:T(8,128)(2,1)}, u32[]{:S(2)}, u32[]{:S(2)}) %collective-permute-start.4) | collective-permute-done | bytes 1572896 | tf_op jit(solution)/shard_map/ppermute | solution.py:11
  323.5 0.0 collective-permute-start.5
  323.5 4.0 fusion.15
  327.5 0.2 collective-permute-start.13
  327.7 4.0 fusion.16
  331.8 82.2 %all-reduce.2.cloned.1.call-done = bf16[4608,512]{1,0:T(8,128)(2,1)} async-done(((bf16[4608,512]{1,0:T(8,128)(2,1)}), bf16[4608,512]{1,0:T(8,128)(2,1)}) %all-reduce.2.cloned.1.call-update) | async-done | bytes 4718608 | tf_op jit(solution)/shard_map/psum | solution.py:16
  414.0 4.3 fusion.6
  418.3 4.3 fusion.7
  422.6 2.7 fusion.8
  425.3 2.7 fusion.9
  428.0 2.6 fusion.17
  430.7 4.2 fusion.5
  434.8 4.1 fusion.18
  438.9 4.1 fusion.4
  443.0 39.6 %collective-permute-done.6 = bf16[3,512,512]{2,1,0:T(8,128)(2,1)S(1)} collective-permute-done((bf16[3,512,512]{2,1,0:T(8,128)(2,1)}, bf16[3,512,512]{2,1,0:T(8,128)(2,1)S(1)}, u32[]{:S(2)}, u32[]{:S(2)}) %collective-permute-start.6) | collective-permute-done | bytes 1572896 | tf_op jit(solution)/shard_map/ppermute | solution.py:11
  482.6 4.0 fusion.19
  486.7 0.2 collective-permute-start.15
  486.9 4.2 fusion.3
  491.1 4.1 fusion.20
  495.2 2.7 fusion.2
  497.9 2.6 fusion.21
  500.5 39.3 %collective-permute-done.7 = bf16[3,512,512]{2,1,0:T(8,128)(2,1)S(1)} collective-permute-done((bf16[3,512,512]{2,1,0:T(8,128)(2,1)S(1)}, bf16[3,512,512]{2,1,0:T(8,128)(2,1)S(1)}, u32[]{:S(2)}, u32[]{:S(2)}) %collective-permute-start.7) | collective-permute-done | bytes 1572896 | tf_op jit(solution)/shard_map/ppermute | solution.py:11
  539.8 2.6 fusion.22
  542.4 23.7 %fusion.1 = bf16[3,512,512]{2,1,0:T(8,128)(2,1)} fusion(f32[3,512,512]{1,2,0:T(8,128)} %fusion.2, f32[3,512,512]{1,2,0:T(8,128)} %fusion.3, f32[3,512,512]{1,2,0:T(8,128)} %fusion.4, bf16[3,512,512]{2,1,0:T(8,128)(2,1)S(1)} %broadcast_multiply_fusion.1, f32[3,512,512]{1,2,0:T(8,128)} %fusion.5, f32[3,512,512]{1,2,0:T(8,128)} %fusion.6, ...), kind=kOutput, calls=%fused_computation.3 | convolution fusion | flops 823394304 | bytes 59768836 | tf_op jit(solution)/shard_map/kr,dkc->drc/dot_general | solution.py:33
  (47 shorter events, 0.1 us)
Async XLA Ops:
  6.5 95.8 %copy-start.12 = (s32[32,32]{1,0:T(8,128)S(1)}, s32[32,32]{1,0:T(8,128)}, u32[]{:S(2)}) copy-start(s32[32,32]{1,0:T(8,128)} %param.6) | copy-start | bytes 12292
  6.5 407.4 %all-reduce.2.cloned.1.call-start = ((), (), s32[]{:S(2)}) async-start(), calls=%async_computation | async-start | bytes 9437184 | tf_op jit(solution)/shard_map/psum | solution.py:16
  9.4 40.3 %collective-permute-start.8 = (bf16[3,512,512]{2,1,0:T(8,128)(2,1)S(1)}, bf16[3,512,512]{2,1,0:T(8,128)(2,1)S(1)}, u32[]{:S(2)}, u32[]{:S(2)}) collective-permute-start(bf16[3,512,512]{2,1,0:T(8,128)(2,1)S(1)} %broadcast_multiply_fusion.1), channel_id=1, source_target_pairs={{0,16},{16,32},{32,48},{48,64},{64,80},{80,96},{96,112},{112,128},... | collective-permute-start | bytes 4718600 | tf_op jit(solution)/shard_map/ppermute | solution.py:11
  11.4 91.0 %collective-permute-start = (bf16[3,512,512]{2,1,0:T(8,128)(2,1)S(1)}, bf16[3,512,512]{2,1,0:T(8,128)(2,1)}, u32[]{:S(2)}, u32[]{:S(2)}) collective-permute-start(bf16[3,512,512]{2,1,0:T(8,128)(2,1)S(1)} %broadcast_multiply_fusion.1), channel_id=1, source_target_pairs={{0,1},{1,2},{2,3},{3,4},{4,5},{5,6},{6,7},{7,8},{8,9},{9,10},{10,1... | collective-permute-start | bytes 4718600 | tf_op jit(solution)/shard_map/ppermute | solution.py:11
  49.7 56.5 %copy-start.8 = (bf16[3,512,512]{2,1,0:T(8,128)(2,1)}, bf16[3,512,512]{2,1,0:T(8,128)(2,1)S(1)}, u32[]{:S(2)}) copy-start(bf16[3,512,512]{2,1,0:T(8,128)(2,1)S(1)} %collective-permute-done.8) | copy-start | bytes 4718596
  49.7 56.5 %collective-permute-start.9 = (bf16[3,512,512]{2,1,0:T(8,128)(2,1)S(1)}, bf16[3,512,512]{2,1,0:T(8,128)(2,1)}, u32[]{:S(2)}, u32[]{:S(2)}) collective-permute-start(bf16[3,512,512]{2,1,0:T(8,128)(2,1)S(1)} %collective-permute-done.8), channel_id=1, source_target_pairs={{0,16},{16,32},{32,48},{48,64},{64,80},{80,96},{96,112},{112,128},... | collective-permute-start | bytes 4718600 | tf_op jit(solution)/shard_map/ppermute | solution.py:11
  102.3 57.5 %collective-permute-start.1 = (bf16[3,512,512]{2,1,0:T(8,128)(2,1)}, bf16[3,512,512]{2,1,0:T(8,128)(2,1)}, u32[]{:S(2)}, u32[]{:S(2)}) collective-permute-start(bf16[3,512,512]{2,1,0:T(8,128)(2,1)} %collective-permute-done), channel_id=1, source_target_pairs={{0,1},{1,2},{2,3},{3,4},{4,5},{5,6},{6,7},{7,8},{8,9},{9,10},{10,1... | collective-permute-start | bytes 4718600 | tf_op jit(solution)/shard_map/ppermute | solution.py:11
  105.1 54.7 %slice-start = ((s8[4718592]{0:T(1024)(128)(4,1)}), s8[4194304]{0:T(1024)(128)(4,1)S(1)}, s32[]{:S(2)}) async-start(s8[4718592]{0:T(1024)(128)(4,1)} %bitcast.68), calls=%async_computation.1 | async-start | bytes 8388608
  105.1 54.7 %slice-start.1 = ((s8[4718592]{0:T(1024)(128)(4,1)}), s8[524288]{0:T(1024)(128)(4,1)S(1)}, s32[]{:S(2)}) async-start(s8[4718592]{0:T(1024)(128)(4,1)} %bitcast.68), calls=%async_computation.2 | async-start | bytes 1048576
  106.1 56.4 %collective-permute-start.10 = (bf16[3,512,512]{2,1,0:T(8,128)(2,1)}, bf16[3,512,512]{2,1,0:T(8,128)(2,1)}, u32[]{:S(2)}, u32[]{:S(2)}) collective-permute-start(bf16[3,512,512]{2,1,0:T(8,128)(2,1)} %collective-permute-done.9), channel_id=1, source_target_pairs={{0,16},{16,32},{32,48},{48,64},{64,80},{80,96},{96,112},{112,128},... | collective-permute-start | bytes 4718600 | tf_op jit(solution)/shard_map/ppermute | solution.py:11
  159.8 66.3 %collective-permute-start.2 = (bf16[3,512,512]{2,1,0:T(8,128)(2,1)}, bf16[3,512,512]{2,1,0:T(8,128)(2,1)S(1)}, u32[]{:S(2)}, u32[]{:S(2)}) collective-permute-start(bf16[3,512,512]{2,1,0:T(8,128)(2,1)} %collective-permute-done.1), channel_id=1, source_target_pairs={{0,1},{1,2},{2,3},{3,4},{4,5},{5,6},{6,7},{7,8},{8,9},{9,10},{10,1... | collective-permute-start | bytes 4718600 | tf_op jit(solution)/shard_map/ppermute | solution.py:11
  162.5 71.5 %collective-permute-start.11 = (bf16[3,512,512]{2,1,0:T(8,128)(2,1)}, bf16[3,512,512]{2,1,0:T(8,128)(2,1)}, u32[]{:S(2)}, u32[]{:S(2)}) collective-permute-start(bf16[3,512,512]{2,1,0:T(8,128)(2,1)} %collective-permute-done.10), channel_id=1, source_target_pairs={{0,16},{16,32},{32,48},{48,64},{64,80},{80,96},{96,112},{112,128},... | collective-permute-start | bytes 4718600 | tf_op jit(solution)/shard_map/ppermute | solution.py:11
  226.1 8.0 %copy-start.10 = (bf16[3,512,512]{2,1,0:T(8,128)(2,1)}, bf16[3,512,512]{2,1,0:T(8,128)(2,1)S(1)}, u32[]{:S(2)}) copy-start(bf16[3,512,512]{2,1,0:T(8,128)(2,1)S(1)} %collective-permute-done.2) | copy-start | bytes 4718596
  226.1 50.4 %collective-permute-start.3 = (bf16[3,512,512]{2,1,0:T(8,128)(2,1)S(1)}, bf16[3,512,512]{2,1,0:T(8,128)(2,1)}, u32[]{:S(2)}, u32[]{:S(2)}) collective-permute-start(bf16[3,512,512]{2,1,0:T(8,128)(2,1)S(1)} %collective-permute-done.2), channel_id=1, source_target_pairs={{0,1},{1,2},{2,3},{3,4},{4,5},{5,6},{6,7},{7,8},{8,9},{9,10},{10,1... | collective-permute-start | bytes 4718600 | tf_op jit(solution)/shard_map/ppermute | solution.py:11
  234.1 93.5 %collective-permute-start.12 = (bf16[3,512,512]{2,1,0:T(8,128)(2,1)}, bf16[3,512,512]{2,1,0:T(8,128)(2,1)}, u32[]{:S(2)}, u32[]{:S(2)}) collective-permute-start(bf16[3,512,512]{2,1,0:T(8,128)(2,1)} %collective-permute-done.11), channel_id=1, source_target_pairs={{0,128},{16,144},{32,160},{48,176},{64,192},{80,208},{96,224},{112... | collective-permute-start | bytes 4718600 | tf_op jit(solution)/shard_map/ppermute | solution.py:11
  276.5 47.0 %collective-permute-start.4 = (bf16[3,512,512]{2,1,0:T(8,128)(2,1)}, bf16[3,512,512]{2,1,0:T(8,128)(2,1)}, u32[]{:S(2)}, u32[]{:S(2)}) collective-permute-start(bf16[3,512,512]{2,1,0:T(8,128)(2,1)} %collective-permute-done.3), channel_id=1, source_target_pairs={{0,8},{1,9},{2,10},{3,11},{4,12},{5,13},{6,14},{7,15},{8,0},{9,1},... | collective-permute-start | bytes 4718600 | tf_op jit(solution)/shard_map/ppermute | solution.py:11
  299.0 13.1 %copy-start.13 = (s32[3]{0:T(128)S(1)}, s32[3]{0:T(128)}, u32[]{:S(2)}) copy-start(s32[3]{0:T(128)} %param.5) | copy-start | bytes 40
  312.0 11.5 %copy-start.6 = (bf16[512,512,1]{1,0,2:T(8,128)(2,1)S(1)}, bf16[512,512,1]{1,0,2:T(8,128)(2,1)}, u32[]{:S(2)}) copy-start(bf16[512,512,1]{1,0,2:T(8,128)(2,1)} %reshape.26) | copy-start | bytes 1572868
  315.8 11.9 %copy-start.7 = (bf16[512,512,1]{1,0,2:T(8,128)(2,1)S(1)}, bf16[512,512,1]{1,0,2:T(8,128)(2,1)}, u32[]{:S(2)}) copy-start(bf16[512,512,1]{1,0,2:T(8,128)(2,1)} %reshape.27) | copy-start | bytes 1572868
  323.5 101.8 %collective-permute-start.5 = (bf16[3,512,512]{2,1,0:T(8,128)(2,1)}, bf16[3,512,512]{2,1,0:T(8,128)(2,1)}, u32[]{:S(2)}, u32[]{:S(2)}) collective-permute-start(bf16[3,512,512]{2,1,0:T(8,128)(2,1)} %collective-permute-done.4), channel_id=1, source_target_pairs={{0,1},{1,2},{2,3},{3,4},{4,5},{5,6},{6,7},{7,8},{8,9},{9,10},{10,1... | collective-permute-start | bytes 4718600 | tf_op jit(solution)/shard_map/ppermute | solution.py:11
  327.5 100.5 %collective-permute-start.13 = (bf16[3,512,512]{2,1,0:T(8,128)(2,1)}, bf16[3,512,512]{2,1,0:T(8,128)(2,1)}, u32[]{:S(2)}, u32[]{:S(2)}) collective-permute-start(bf16[3,512,512]{2,1,0:T(8,128)(2,1)} %collective-permute-done.12), channel_id=1, source_target_pairs={{0,16},{16,32},{32,48},{48,64},{64,80},{80,96},{96,112},{112,128},... | collective-permute-start | bytes 4718600 | tf_op jit(solution)/shard_map/ppermute | solution.py:11
  414.0 4.3 copy-start
  418.3 4.3 copy-start.9
  425.3 2.8 copy-start.5
  425.3 2.8 copy-start.11
  425.3 57.4 %collective-permute-start.6 = (bf16[3,512,512]{2,1,0:T(8,128)(2,1)}, bf16[3,512,512]{2,1,0:T(8,128)(2,1)S(1)}, u32[]{:S(2)}, u32[]{:S(2)}) collective-permute-start(bf16[3,512,512]{2,1,0:T(8,128)(2,1)} %collective-permute-done.5), channel_id=1, source_target_pairs={{0,1},{1,2},{2,3},{3,4},{4,5},{5,6},{6,7},{7,8},{8,9},{9,10},{10,1... | collective-permute-start | bytes 4718600 | tf_op jit(solution)/shard_map/ppermute | solution.py:11
  428.0 58.7 %collective-permute-start.14 = (bf16[3,512,512]{2,1,0:T(8,128)(2,1)}, bf16[3,512,512]{2,1,0:T(8,128)(2,1)S(1)}, u32[]{:S(2)}, u32[]{:S(2)}) collective-permute-start(bf16[3,512,512]{2,1,0:T(8,128)(2,1)} %collective-permute-done.13), channel_id=1, source_target_pairs={{0,16},{16,32},{32,48},{48,64},{64,80},{80,96},{96,112},{112,128},... | collective-permute-start | bytes 4718600 | tf_op jit(solution)/shard_map/ppermute | solution.py:11
  430.7 4.2 copy-start.4
  438.9 43.7 %copy-start.3 = (bf16[512,512,1]{1,0,2:T(8,128)(2,1)S(1)}, bf16[512,512,1]{1,0,2:T(8,128)(2,1)}, u32[]{:S(2)}) copy-start(bf16[512,512,1]{1,0,2:T(8,128)(2,1)} %reshape.30) | copy-start | bytes 1572868
  482.6 57.2 %collective-permute-start.7 = (bf16[3,512,512]{2,1,0:T(8,128)(2,1)S(1)}, bf16[3,512,512]{2,1,0:T(8,128)(2,1)S(1)}, u32[]{:S(2)}, u32[]{:S(2)}) collective-permute-start(bf16[3,512,512]{2,1,0:T(8,128)(2,1)S(1)} %collective-permute-done.6), channel_id=1, source_target_pairs={{0,1},{1,2},{2,3},{3,4},{4,5},{5,6},{6,7},{7,8},{8,9},{9,10},{10,1... | collective-permute-start | bytes 4718600 | tf_op jit(solution)/shard_map/ppermute | solution.py:11
  486.7 4.4 copy-start.2
  486.7 55.7 %collective-permute-start.15 = (bf16[3,512,512]{2,1,0:T(8,128)(2,1)S(1)}, bf16[3,512,512]{2,1,0:T(8,128)(2,1)}, u32[]{:S(2)}, u32[]{:S(2)}) collective-permute-start(bf16[3,512,512]{2,1,0:T(8,128)(2,1)S(1)} %collective-permute-done.14), channel_id=1, source_target_pairs={{0,16},{16,32},{32,48},{48,64},{64,80},{80,96},{96,112},{112,128},... | collective-permute-start | bytes 4718600 | tf_op jit(solution)/shard_map/ppermute | solution.py:11
  495.2 2.7 copy-start.1
Sparse Core Ops, SparseCore 0:
  162.7 251.2 all-reduce.1
where the time goes:
time: 583 us; the launch traced here: 573 us
  waiting for transfers between devices  419 us (72%)
  matrix products  84.8 us (15%)
  local copies, waits for them, and re-layouts  36.4 us (6%)
  other arithmetic  13.8 us (2%)
  between operations  13.8 us (2%)
    ppermute x16, waiting for transfers between devices, from_behind(): lax.ppermute(array, axis, [(i, (i + by) % length) for i in range(length)])  336 us
    psum x1, waiting for transfers between devices, broadcast(): return lax.psum(jnp.where(mine, array, jnp.zeros_like(array)), axis)  82.2 us
    dot_general x9, matrix products, left_product(): jnp.einsum('kr,dkc->drc', left_op, right_op, preferred_element_type=jnp.f...  52.9 us
    dot_general x9, matrix products, right_product(): jnp.einsum('drc,ck->drk', left_op, right_op, preferred_element_type=jnp.f...  31.9 us
    slice x10, local copies, waits for them, and re-layouts, col_add(): strip_local[(distance + col_span) * col_width:(distance + col_span + 1) *...  23.8 us
  transfers between devices with their start and end apart: 17, of which 9 were waited for; matrix products, arithmetic and copies ran while one was open for 19% of the time, Pallas kernels for 0%

commit v1 on v0

v1 whole, which is shorter than its diff:
```python
import jax
import jax.numpy as jnp
from jax import lax
from jax.sharding import PartitionSpec as P

BLK = 256


def shifted(array, axis, by):
    length = lax.axis_size(axis)
    return lax.ppermute(array, axis, [(i, (i + by) % length) for i in range(length)])


def mask_blocks(values, occupancy):
    leading = values.shape[:-2]
    row_blocks = values.shape[-2] // BLK
    col_blocks = values.shape[-1] // BLK
    shaped = values.reshape(leading + (row_blocks, BLK, col_blocks, BLK))
    weight = occupancy.astype(values.dtype)[:, None, :, None]
    return (shaped * weight).reshape(values.shape)


def body(sp2_branch, p0_occupancy, p1_occupancy, p0_columns, p1_tiles):
    col_count = lax.axis_size("col")
    row_count = lax.axis_size("row")
    col_width = p0_columns.shape[1]
    row_height = p1_tiles.shape[1]
    col_blocks = col_width // BLK
    row_blocks = row_height // BLK
    strip_blocks = p0_columns.shape[0] // BLK
    band_half = (strip_blocks - col_blocks) // 2
    all_blocks = col_blocks * col_count
    col_span = band_half // col_blocks
    row_at = lax.axis_index("row")
    col_at = lax.axis_index("col")
    own_occ = lax.dynamic_slice(
        p1_occupancy, (row_at * row_blocks, col_at * col_blocks), (row_blocks, col_blocks)
    )
    p1_local = mask_blocks(p1_tiles, own_occ)
    tripled = jnp.concatenate([p0_occupancy, p0_occupancy, p0_occupancy], axis=0)
    strip_occ = lax.dynamic_slice(
        tripled,
        (col_at * col_blocks - band_half + all_blocks, col_at * col_blocks),
        (strip_blocks, col_blocks),
    )
    strip_local = mask_blocks(p0_columns, strip_occ)

    tiles = []
    for e in range(-col_span, col_span + 1):
        tiles.append(p1_local if e == 0 else shifted(p1_local, "col", -e))

    pairs = [(i * col_count + j, j * col_count + i) for i in range(row_count) for j in range(col_count)]
    squared = sp2_branch == 1
    outs = []
    for d in range(p1_tiles.shape[0]):
        summed = jnp.zeros((row_height, col_width), jnp.float32)
        for k, tile in enumerate(tiles):
            factor = strip_local[k * col_width : (k + 1) * col_width, :]
            summed = summed + jnp.dot(tile[d], factor, preferred_element_type=jnp.float32)
        mirrored = lax.ppermute(summed, ("row", "col"), pairs).T
        bracket = summed + mirrored
        chosen = jnp.where(squared[d], bracket, 2.0 * p1_local[d].astype(jnp.float32) - bracket)
        outs.append(chosen)
    chosen = jnp.stack(outs)
    return mask_blocks(chosen, own_occ).astype(jnp.bfloat16)


def solution(mesh):
    in_specs = (P(), P(), P(), P("col", None), P(None, "row", "col"))
    out_specs = P(None, "row", "col")
    return jax.shard_map(body, mesh=mesh, in_specs=in_specs, out_specs=out_specs, check_vma=False)
```

time: 583 us -> 488 us (0.84)
  the two profiles are of different devices: /device:TPU:2 before, /device:TPU:67 now
where the time goes in v1:
time: 488 us; the launch traced here: 485 us
  waiting for transfers between devices  373 us (76%)
  local copies, waits for them, and re-layouts  33.9 us (7%)
  matrix products  32.9 us (7%)
  starting transfers between devices  23.4 us (5%)
  other arithmetic  20.7 us (4%)
    ppermute x3, waiting for transfers between devices, body(): mirrored = lax.ppermute(summed, ('row', 'col'), pairs).T  235 us
    ppermute x8, waiting for transfers between devices, shifted(): lax.ppermute(array, axis, [(i, (i + by) % length) for i in range(length)])  138 us
    dot_general x27, matrix products, body(): jnp.dot(tile[d], factor, preferred_element_type=jnp.float32)  32.9 us
    ppermute x8, starting transfers between devices, shifted(): lax.ppermute(array, axis, [(i, (i + by) % length) for i in range(length)])  13.4 us
    mul x3, other arithmetic, mask_blocks(): return (shaped * weight).reshape(values.shape)  11.3 us
    unnamed x83, local copies, waits for them, and re-layouts  10.8 us
    ppermute x3, starting transfers between devices, body(): mirrored = lax.ppermute(summed, ('row', 'col'), pairs).T  10 us
  transfers between devices with their start and end apart: 11, of which 9 were waited for; matrix products, arithmetic and copies ran while one was open for 15% of the time, Pallas kernels for 0%

profile of v1, /device:TPU:67, one launch (start us, length us, event | category | flops | bytes accessed | tf_op | source)
XLA Modules:
  0.0 484.7 jit_solution(14894494244042946240)
XLA Ops:
  0.0 0.9 dynamic-slice_convert_fusion
  1.4 1.3 broadcast_multiply_fusion.2
  2.8 1.9 collective-permute-start.3
  4.6 1.3 collective-permute-start.2
  5.9 1.6 collective-permute-start.1
  7.6 2.8 collective-permute-start.7
  10.3 1.9 collective-permute-start.6
  12.5 7.7 %reshape.42 = bf16[18,256,2,256]{3,2,1,0:T(2,128)(2,1)} reshape(bf16[4608,512]{1,0:T(8,128)(2,1)} %param.8) | data formatting | bytes 9437184 | tf_op jit(solution)/shard_map/reshape | solution.py:18
  20.2 8.5 %broadcast_multiply_fusion = bf16[18,256,2,256]{3,2,1,0:T(2,128)(2,1)} fusion(bf16[18,256,2,256]{3,2,1,0:T(2,128)(2,1)} %reshape.42, bf16[18,2]{1,0:T(8,128)(2,1)S(1)} %copy.30), kind=kLoop, calls=%fused_computation.2 | loop fusion | flops 2359296 | bytes 9437256 | tf_op jit(solution)/shard_map/mul | solution.py:20
  28.7 6.0 %fusion.43 = (bf16[2,256,2,256]{3,2,1,0:T(2,128)(2,1)}, bf16[2,256,2,256]{3,2,1,0:T(2,128)(2,1)}, bf16[2,256,2,256]{3,2,1,0:T(2,128)(2,1)}, bf16[2,256,2,256]{3,...) fusion(bf16[18,256,2,256]{3,2,1,0:T(2,128)(2,1)} %broadcast_mul, ...), kind=kLoop, calls=%fused_computation.89 | loop fusion | bytes 9437184 | tf_op jit(solution)/shard_map/slice | solution.py:58
  35.2 1.2 copy.74
  36.4 1.3 copy.73
  37.9 1.4 broadcast_multiply_fusion.1
  39.3 1.1 fusion.44
  40.7 0.9 copy-done.22
  42.1 0.6 copy-done.19
  43.6 1.5 fusion.47
  45.1 44.0 %collective-permute-done.3 = bf16[3,512,512]{2,1,0:T(8,128)(2,1)} collective-permute-done((bf16[3,512,512]{2,1,0:T(8,128)(2,1)}, bf16[3,512,512]{2,1,0:T(8,128)(2,1)}, u32[]{:S(2)}, u32[]{:S(2)}) %collective-permute-start.3) | collective-permute-done | bytes 1572896 | tf_op jit(solution)/shard_map/ppermute | solution.py:11
  89.2 1.5 fusion.48
  90.6 32.2 %collective-permute-done.2 = bf16[3,512,512]{2,1,0:T(8,128)(2,1)} collective-permute-done((bf16[3,512,512]{2,1,0:T(8,128)(2,1)}, bf16[3,512,512]{2,1,0:T(8,128)(2,1)}, u32[]{:S(2)}, u32[]{:S(2)}) %collective-permute-start.2) | collective-permute-done | bytes 1572896 | tf_op jit(solution)/shard_map/ppermute | solution.py:11
  122.9 3.9 collective-permute-start
  126.8 1.5 fusion.37
  128.3 28.4 %collective-permute-done.1 = bf16[3,512,512]{2,1,0:T(8,128)(2,1)} collective-permute-done((bf16[3,512,512]{2,1,0:T(8,128)(2,1)}, bf16[3,512,512]{2,1,0:T(8,128)(2,1)}, u32[]{:S(2)}, u32[]{:S(2)}) %collective-permute-start.1) | collective-permute-done | bytes 1572896 | tf_op jit(solution)/shard_map/ppermute | solution.py:11
  156.6 1.5 fusion.38
  158.1 1.5 fusion.39
  159.6 1.5 collective-permute-done.7
  161.0 1.5 fusion.34
  162.5 15.7 %collective-permute-done.6 = bf16[3,512,512]{2,1,0:T(8,128)(2,1)} collective-permute-done((bf16[3,512,512]{2,1,0:T(8,128)(2,1)}, bf16[3,512,512]{2,1,0:T(8,128)(2,1)}, u32[]{:S(2)}, u32[]{:S(2)}) %collective-permute-start.6) | collective-permute-done | bytes 1572896 | tf_op jit(solution)/shard_map/ppermute | solution.py:11
  178.2 1.5 fusion.35
  180.2 0.7 copy-done.30
  181.3 0.7 copy-done.28
  182.0 16.0 %collective-permute-done.4 = bf16[3,512,512]{2,1,0:T(8,128)(2,1)S(1)} collective-permute-done((bf16[3,512,512]{2,1,0:T(8,128)(2,1)}, bf16[3,512,512]{2,1,0:T(8,128)(2,1)S(1)}, u32[]{:S(2)}, u32[]{:S(2)}) %collective-permute-start.4) | collective-permute-done | bytes 1572896 | tf_op jit(solution)/shard_map/ppermute | solution.py:11
  198.0 1.1 copy-done.26
  199.7 1.3 copy.31
  201.0 2.4 collective-permute-start.8
  203.4 1.7 fusion.31
  205.1 1.5 fusion.32
  206.7 1.5 fusion.33
  208.2 1.7 fusion.28
  209.9 1.7 fusion.29
  212.1 0.7 copy-done.16
  212.8 0.5 fusion.12
  213.4 0.9 copy-done.27
  214.2 1.5 fusion.9
  215.8 5.0 %collective-permute-start.9 = (f32[512,512]{0,1:T(8,128)}, f32[512,512]{0,1:T(8,128)}, u32[]{:S(2)}, u32[]{:S(2)}) collective-permute-start(f32[512,512]{0,1:T(8,128)} %fusion.9), channel_id=1, source_target_pairs={{0,0},{1,16},{2,32},{3,48},{4,64},{5,80},{6,96},{7,112},{8,128},{9... | collective-permute-start | bytes 3145736 | tf_op jit(solution)/shard_map/ppermute | solution.py:60
  220.8 1.5 fusion.25
  222.3 1.5 fusion.26
  223.9 1.5 fusion.27
  225.4 1.5 fusion.23
  227.4 0.7 copy-done.15
  228.1 0.5 fusion.6
  228.7 1.5 fusion.22
  230.2 1.5 fusion.3
  231.7 2.6 collective-permute-start.10
  234.9 0.7 fusion.45
  235.6 2.5 copy.41
  238.1 2.6 copy.51
  240.8 195.1 %collective-permute-done.8 = f32[512,512]{0,1:T(8,128)} collective-permute-done((f32[512,512]{0,1:T(8,128)}, f32[512,512]{0,1:T(8,128)}, u32[]{:S(2)}, u32[]{:S(2)}) %collective-permute-start.8) | collective-permute-done | bytes 1048608 | tf_op jit(solution)/shard_map/ppermute | solution.py:60
  435.8 2.3 fusion.19
  438.1 20.2 %collective-permute-done.9 = f32[512,512]{0,1:T(8,128)} collective-permute-done((f32[512,512]{0,1:T(8,128)}, f32[512,512]{0,1:T(8,128)}, u32[]{:S(2)}, u32[]{:S(2)}) %collective-permute-start.9) | collective-permute-done | bytes 1048608 | tf_op jit(solution)/shard_map/ppermute | solution.py:60
  458.3 2.3 fusion.20
  460.6 20.2 %collective-permute-done.10 = f32[512,512]{0,1:T(8,128)} collective-permute-done((f32[512,512]{0,1:T(8,128)}, f32[512,512]{0,1:T(8,128)}, u32[]{:S(2)}, u32[]{:S(2)}) %collective-permute-start.10) | collective-permute-done | bytes 1048608 | tf_op jit(solution)/shard_map/ppermute | solution.py:60
  480.8 2.2 fusion.21
  483.0 1.7 fusion
  (89 shorter events, 6.1 us)
Async XLA Ops:
  0.0 1.4 copy-start.8
  1.4 10.8 %copy-start.32 = (s32[32,32]{1,0:T(8,128)S(1)}, s32[32,32]{1,0:T(8,128)}, u32[]{:S(2)}) copy-start(s32[32,32]{1,0:T(8,128)} %param.6) | copy-start | bytes 12292
  2.8 86.4 %collective-permute-start.3 = (bf16[3,512,512]{2,1,0:T(8,128)(2,1)}, bf16[3,512,512]{2,1,0:T(8,128)(2,1)}, u32[]{:S(2)}, u32[]{:S(2)}) collective-permute-start(bf16[3,512,512]{2,1,0:T(8,128)(2,1)} %broadcast_multiply_fusion.2), channel_id=1, source_target_pairs={{0,1},{1,2},{2,3},{3,4},{4,5},{5,6},{6,7},{7,8},{8,9},{9,10},{10,1... | collective-permute-start | bytes 4718600 | tf_op jit(solution)/shard_map/ppermute | solution.py:11
  4.6 118.2 %collective-permute-start.2 = (bf16[3,512,512]{2,1,0:T(8,128)(2,1)}, bf16[3,512,512]{2,1,0:T(8,128)(2,1)}, u32[]{:S(2)}, u32[]{:S(2)}) collective-permute-start(bf16[3,512,512]{2,1,0:T(8,128)(2,1)} %broadcast_multiply_fusion.2), channel_id=1, source_target_pairs={{0,2},{1,3},{2,4},{3,5},{4,6},{5,7},{6,8},{7,9},{8,10},{9,11},{10,... | collective-permute-start | bytes 4718600 | tf_op jit(solution)/shard_map/ppermute | solution.py:11
  5.9 150.7 %collective-permute-start.1 = (bf16[3,512,512]{2,1,0:T(8,128)(2,1)}, bf16[3,512,512]{2,1,0:T(8,128)(2,1)}, u32[]{:S(2)}, u32[]{:S(2)}) collective-permute-start(bf16[3,512,512]{2,1,0:T(8,128)(2,1)} %broadcast_multiply_fusion.2), channel_id=1, source_target_pairs={{0,3},{1,4},{2,5},{3,6},{4,7},{5,8},{6,9},{7,10},{8,11},{9,12},{10... | collective-permute-start | bytes 4718600 | tf_op jit(solution)/shard_map/ppermute | solution.py:11
  7.6 153.5 %collective-permute-start.7 = (bf16[3,512,512]{2,1,0:T(8,128)(2,1)}, bf16[3,512,512]{2,1,0:T(8,128)(2,1)}, u32[]{:S(2)}, u32[]{:S(2)}) collective-permute-start(bf16[3,512,512]{2,1,0:T(8,128)(2,1)} %broadcast_multiply_fusion.2), channel_id=1, source_target_pairs={{0,12},{1,13},{2,14},{3,15},{4,0},{5,1},{6,2},{7,3},{8,4},{9,5},{1... | collective-permute-start | bytes 4718600 | tf_op jit(solution)/shard_map/ppermute | solution.py:11
  10.3 167.9 %collective-permute-start.6 = (bf16[3,512,512]{2,1,0:T(8,128)(2,1)}, bf16[3,512,512]{2,1,0:T(8,128)(2,1)}, u32[]{:S(2)}, u32[]{:S(2)}) collective-permute-start(bf16[3,512,512]{2,1,0:T(8,128)(2,1)} %broadcast_multiply_fusion.2), channel_id=1, source_target_pairs={{0,13},{1,14},{2,15},{3,0},{4,1},{5,2},{6,3},{7,4},{8,5},{9,6},{10... | collective-permute-start | bytes 4718600 | tf_op jit(solution)/shard_map/ppermute | solution.py:11
  35.1 2.6 copy-start.25
  35.1 2.7 copy-start.24
  36.4 90.4 %copy-start.2 = (bf16[64,8,2,256]{3,1,2,0:T(8,128)(2,1)}, bf16[64,8,2,256]{3,1,2,0:T(8,128)(2,1)S(1)}, u32[]{:S(2)}) copy-start(bf16[64,8,2,256]{3,1,2,0:T(8,128)(2,1)S(1)} %copy.74) | copy-start | bytes 1572868
  37.7 118.9 %copy-start = (bf16[64,8,2,256]{3,1,2,0:T(8,128)(2,1)}, bf16[64,8,2,256]{3,1,2,0:T(8,128)(2,1)S(1)}, u32[]{:S(2)}) copy-start(bf16[64,8,2,256]{3,1,2,0:T(8,128)(2,1)S(1)} %copy.73) | copy-start | bytes 1572868
  39.3 1.2 copy-start.23
  40.4 1.1 copy-start.22
  40.4 1.4 copy-start.21
  40.5 2.4 copy-start.11
  40.6 1.4 copy-start.20
  41.5 1.1 copy-start.19
  41.9 136.3 %copy-start.4 = (bf16[64,8,2,256]{3,1,2,0:T(8,128)(2,1)}, bf16[64,8,2,256]{3,1,2,0:T(8,128)(2,1)S(1)}, u32[]{:S(2)}) copy-start(bf16[64,8,2,256]{3,1,2,0:T(8,128)(2,1)S(1)} %copy.79) | copy-start | bytes 1572868
  42.1 137.6 %copy-start.6 = (bf16[64,8,2,256]{3,1,2,0:T(8,128)(2,1)}, bf16[64,8,2,256]{3,1,2,0:T(8,128)(2,1)S(1)}, u32[]{:S(2)}) copy-start(bf16[64,8,2,256]{3,1,2,0:T(8,128)(2,1)S(1)} %copy.78) | copy-start | bytes 1572868
  42.9 0.8 copy-start.13
  43.0 46.2 %copy-start.9 = (bf16[64,8,2,256]{3,1,2,0:T(8,128)(2,1)}, bf16[64,8,2,256]{3,1,2,0:T(8,128)(2,1)S(1)}, u32[]{:S(2)}) copy-start(bf16[64,8,2,256]{3,1,2,0:T(8,128)(2,1)S(1)} %copy.82) | copy-start | bytes 1572868
  89.2 90.5 %collective-permute-start.5 = (bf16[3,512,512]{2,1,0:T(8,128)(2,1)}, bf16[3,512,512]{2,1,0:T(8,128)(2,1)S(1)}, u32[]{:S(2)}, u32[]{:S(2)}) collective-permute-start(bf16[3,512,512]{2,1,0:T(8,128)(2,1)} %broadcast_multiply_fusion.2), channel_id=1, source_target_pairs={{0,14},{1,15},{2,0},{3,1},{4,2},{5,3},{6,4},{7,5},{8,6},{9,7},{10,... | collective-permute-start | bytes 4718600 | tf_op jit(solution)/shard_map/ppermute | solution.py:11
  122.9 57.3 %collective-permute-start = (bf16[3,512,512]{2,1,0:T(8,128)(2,1)}, bf16[3,512,512]{2,1,0:T(8,128)(2,1)S(1)}, u32[]{:S(2)}, u32[]{:S(2)}) collective-permute-start(bf16[3,512,512]{2,1,0:T(8,128)(2,1)} %broadcast_multiply_fusion.2), channel_id=1, source_target_pairs={{0,4},{1,5},{2,6},{3,7},{4,8},{5,9},{6,10},{7,11},{8,12},{9,13},{1... | collective-permute-start | bytes 4718600 | tf_op jit(solution)/shard_map/ppermute | solution.py:11
  156.6 41.4 %collective-permute-start.4 = (bf16[3,512,512]{2,1,0:T(8,128)(2,1)}, bf16[3,512,512]{2,1,0:T(8,128)(2,1)S(1)}, u32[]{:S(2)}, u32[]{:S(2)}) collective-permute-start(bf16[3,512,512]{2,1,0:T(8,128)(2,1)} %broadcast_multiply_fusion.2), channel_id=1, source_target_pairs={{0,15},{1,0},{2,1},{3,2},{4,3},{5,4},{6,5},{7,6},{8,7},{9,8},{10,9... | collective-permute-start | bytes 4718600 | tf_op jit(solution)/shard_map/ppermute | solution.py:11
  179.7 1.2 copy-start.30
  180.9 1.2 copy-start.28
  198.0 1.1 copy-start.26
  201.0 4.2 copy-start.1
  201.0 234.8 %collective-permute-start.8 = (f32[512,512]{0,1:T(8,128)}, f32[512,512]{0,1:T(8,128)}, u32[]{:S(2)}, u32[]{:S(2)}) collective-permute-start(f32[512,512]{0,1:T(8,128)} %copy.31), channel_id=1, source_target_pairs={{0,0},{1,16},{2,32},{3,48},{4,64},{5,80},{6,96},{7,112},{8,128},{9... | collective-permute-start | bytes 3145736 | tf_op jit(solution)/shard_map/ppermute | solution.py:60
  208.2 1.7 copy-start.5
  208.2 3.4 copy-start.31
  209.9 1.7 copy-start.7
  209.9 2.2 copy-start.29
  211.6 1.2 copy-start.16
  212.8 1.4 copy-start.27
  214.2 6.6 %copy-start.3 = (bf16[64,8,2,256]{3,1,2,0:T(8,128)(2,1)S(1)}, bf16[64,8,2,256]{3,1,2,0:T(8,128)(2,1)}, u32[]{:S(2)}) copy-start(bf16[64,8,2,256]{3,1,2,0:T(8,128)(2,1)} %copy-done.2) | copy-start | bytes 1572868
  215.8 242.5 %collective-permute-start.9 = (f32[512,512]{0,1:T(8,128)}, f32[512,512]{0,1:T(8,128)}, u32[]{:S(2)}, u32[]{:S(2)}) collective-permute-start(f32[512,512]{0,1:T(8,128)} %fusion.9), channel_id=1, source_target_pairs={{0,0},{1,16},{2,32},{3,48},{4,64},{5,80},{6,96},{7,112},{8,128},{9... | collective-permute-start | bytes 3145736 | tf_op jit(solution)/shard_map/ppermute | solution.py:60
  226.9 1.2 copy-start.15
  231.7 249.1 %collective-permute-start.10 = (f32[512,512]{0,1:T(8,128)}, f32[512,512]{0,1:T(8,128)}, u32[]{:S(2)}, u32[]{:S(2)}) collective-permute-start(f32[512,512]{0,1:T(8,128)} %fusion.3), channel_id=1, source_target_pairs={{0,0},{1,16},{2,32},{3,48},{4,64},{5,80},{6,96},{7,112},{8,128},{9... | collective-permute-start | bytes 3145736 | tf_op jit(solution)/shard_map/ppermute | solution.py:60
  234.3 0.7 copy-start.33
  238.1 197.7 %copy-start.12 = (bf16[64,8,2,256]{3,1,2,0:T(8,128)(2,1)S(1)}, bf16[64,8,2,256]{3,1,2,0:T(8,128)(2,1)}, u32[]{:S(2)}) copy-start(bf16[64,8,2,256]{3,1,2,0:T(8,128)(2,1)} %copy-done.11) | copy-start | bytes 1572868
  435.8 22.5 %copy-start.14 = (bf16[64,8,2,256]{3,1,2,0:T(8,128)(2,1)S(1)}, bf16[64,8,2,256]{3,1,2,0:T(8,128)(2,1)}, u32[]{:S(2)}) copy-start(bf16[64,8,2,256]{3,1,2,0:T(8,128)(2,1)} %copy-done.13) | copy-start | bytes 1572868
  435.8 22.5 %copy-start.18 = (f32[512,512]{1,0:T(8,128)S(1)}, f32[512,512]{1,0:T(8,128)}, u32[]{:S(2)}) copy-start(f32[512,512]{1,0:T(8,128)} %copy.41) | copy-start | bytes 3145732
  458.3 22.5 %copy-start.10 = (bf16[64,8,2,256]{3,1,2,0:T(8,128)(2,1)S(1)}, bf16[64,8,2,256]{3,1,2,0:T(8,128)(2,1)}, u32[]{:S(2)}) copy-start(bf16[64,8,2,256]{3,1,2,0:T(8,128)(2,1)} %copy-done.9) | copy-start | bytes 1572868
  458.3 22.5 %copy-start.17 = (f32[512,512]{1,0:T(8,128)S(1)}, f32[512,512]{1,0:T(8,128)}, u32[]{:S(2)}) copy-start(f32[512,512]{1,0:T(8,128)} %copy.51) | copy-start | bytes 3145732

commit v2 on v1

--- a/solution.py
+++ b/solution.py
@@ -4,11 +4,6 @@
 from jax.sharding import PartitionSpec as P
 
 BLK = 256
-
-
-def shifted(array, axis, by):
-    length = lax.axis_size(axis)
-    return lax.ppermute(array, axis, [(i, (i + by) % length) for i in range(length)])
 
 
 def mask_blocks(values, occupancy):
@@ -45,17 +40,33 @@
     )
     strip_local = mask_blocks(p0_columns, strip_occ)
 
-    tiles = []
-    for e in range(-col_span, col_span + 1):
-        tiles.append(p1_local if e == 0 else shifted(p1_local, "col", -e))
+    sign = jnp.where(col_at % 2 == 0, -1, 1)
+    fetched = []
+    for k in range(col_span):
+        pairs = []
+        for c in range(col_count):
+            src = c - 1 - k if c % 2 == 0 else c + 1 + k
+            pairs.append((src % col_count, c))
+        fetched.append(lax.ppermute(p1_local, "col", pairs))
+    swap = [(c, c ^ 1) for c in range(col_count)]
+    partner_own = lax.ppermute(p1_local, "col", swap)
+    partner_fetched = [lax.ppermute(fetched[j], "col", swap) for j in range(col_span - 1)]
+
+    tiles = [(p1_local, 0)]
+    tiles += [(fetched[k], sign * (k + 1)) for k in range(col_span)]
+    tiles += [(partner_own, -sign)]
+    tiles += [(partner_fetched[j], -sign * (j + 2)) for j in range(col_span - 1)]
+    factors = []
+    for _, offset in tiles:
+        start = (offset + col_span) * col_width
+        factors.append(lax.dynamic_slice_in_dim(strip_local, start, col_width, 0))
 
     pairs = [(i * col_count + j, j * col_count + i) for i in range(row_count) for j in range(col_count)]
     squared = sp2_branch == 1
     outs = []
     for d in range(p1_tiles.shape[0]):
         summed = jnp.zeros((row_height, col_width), jnp.float32)
-        for k, tile in enumerate(tiles):
-            factor = strip_local[k * col_width : (k + 1) * col_width, :]
+        for (tile, _), factor in zip(tiles, factors):
             summed = summed + jnp.dot(tile[d], factor, preferred_element_type=jnp.float32)
         mirrored = lax.ppermute(summed, ("row", "col"), pairs).T
         bracket = summed + mirrored

time: 488 us -> 442 us (0.906)
  the two profiles are of different devices: /device:TPU:67 before, /device:TPU:218 now
where the time goes in v2:
time: 442 us; the launch traced here: 436 us
  waiting for transfers between devices  332 us (75%)
  matrix products  39.3 us (9%)
  local copies, waits for them, and re-layouts  26.5 us (6%)
  starting transfers between devices  20.2 us (5%)
  other arithmetic  18.2 us (4%)
    ppermute x3, waiting for transfers between devices, body(): mirrored = lax.ppermute(summed, ('row', 'col'), pairs).T  242 us
    ppermute x4, waiting for transfers between devices, body(): fetched.append(lax.ppermute(p1_local, 'col', pairs))  89.6 us
    dot_general x27, matrix products, body(): jnp.dot(tile[d], factor, preferred_element_type=jnp.float32)  39.3 us
    ppermute x3, starting transfers between devices, body(): mirrored = lax.ppermute(summed, ('row', 'col'), pairs).T  9.56 us
  transfers between devices with their start and end apart: 11, of which 5 were waited for; matrix products, arithmetic and copies ran while one was open for 17% of the time, Pallas kernels for 0%

profile of v2, /device:TPU:218, one launch (start us, length us, event | category | flops | bytes accessed | tf_op | source)
XLA Modules:
  0.0 436.5 jit_solution(968997875395462176)
XLA Ops:
  0.0 0.9 dynamic-slice_convert_fusion
  0.9 0.3 mul.108
  1.4 1.3 broadcast_multiply_fusion
  3.0 1.7 collective-permute-start.4
  4.7 2.6 collective-permute-start.3
  7.3 1.1 collective-permute-start.2
  8.4 4.4 %collective-permute-start.1 = (bf16[3,512,512]{2,1,0:T(8,128)(2,1)}, bf16[3,512,512]{2,1,0:T(8,128)(2,1)}, u32[]{:S(2)}, u32[]{:S(2)}) collective-permute-start(bf16[3,512,512]{2,1,0:T(8,128)(2,1)} %broadcast_multiply_fusion), channel_id=1, source_target_pairs={{14,0},{3,1},{0,2},{5,3},{2,4},{7,5},{4,6},{9,7},{6,8},{11,9},{8,1... | collective-permute-start | bytes 4718600 | tf_op jit(solution)/shard_map/ppermute | solution.py:50
  13.1 7.7 %reshape.36 = bf16[18,256,2,256]{3,2,1,0:T(2,128)(2,1)} reshape(bf16[4608,512]{1,0:T(8,128)(2,1)} %param.8) | data formatting | bytes 9437184 | tf_op jit(solution)/shard_map/reshape | solution.py:13
  20.8 2.4 slice_multiply_fusion
  23.2 0.4 reshape.35
  23.6 1.1 copy.71
  24.7 1.4 broadcast_multiply_fusion.1
  26.2 1.1 fusion.85
  27.4 2.5 mul.106
  29.9 1.0 copy.73
  30.9 1.2 slice-done.1
  32.1 3.6 mul.113
  35.8 0.4 fusion.87
  36.3 0.5 fusion.88
  36.8 0.5 fusion.89
  37.3 66.4 %collective-permute-done.2 = bf16[3,512,512]{2,1,0:T(8,128)(2,1)} collective-permute-done((bf16[3,512,512]{2,1,0:T(8,128)(2,1)}, bf16[3,512,512]{2,1,0:T(8,128)(2,1)}, u32[]{:S(2)}, u32[]{:S(2)}) %collective-permute-start.2) | collective-permute-done | bytes 1572896 | tf_op jit(solution)/shard_map/ppermute | solution.py:50
  103.6 23.2 %collective-permute-done.1 = bf16[3,512,512]{2,1,0:T(8,128)(2,1)} collective-permute-done((bf16[3,512,512]{2,1,0:T(8,128)(2,1)}, bf16[3,512,512]{2,1,0:T(8,128)(2,1)}, u32[]{:S(2)}, u32[]{:S(2)}) %collective-permute-start.1) | collective-permute-done | bytes 1572896 | tf_op jit(solution)/shard_map/ppermute | solution.py:50
  126.8 1.5 fusion.31
  128.3 1.5 fusion.26
  129.9 1.5 fusion.32
  131.4 1.5 fusion.27
  132.9 1.5 fusion.33
  134.4 1.5 fusion.28
  135.9 0.6 collective-permute-start.5
  136.5 1.5 convolution_add_fusion.8
  138.0 1.5 convolution_add_fusion.5
  139.5 1.5 fusion.15
  141.1 1.5 fusion.21
  142.6 1.5 fusion.22
  144.1 1.5 fusion.23
  145.7 1.5 convolution_add_fusion.2
  147.2 2.5 fusion.10
  149.8 2.5 fusion.5
  152.3 0.4 fusion.29
  152.8 0.4 fusion.30
  153.5 0.5 copy-done.8
  154.0 1.2 copy-done.10
  155.2 0.5 fusion.12
  155.7 1.4 copy.31
  157.1 3.5 collective-permute-start.8
  160.6 1.8 fusion.24
  162.4 1.6 fusion.25
  164.1 2.5 fusion.7
  166.6 2.5 collective-permute-start.9
  169.1 1.5 fusion.20
  170.6 1.8 fusion.19
  172.4 2.5 fusion.2
  174.9 3.6 collective-permute-start.10
  178.9 1.1 copy.76
  180.0 0.7 fusion.86
  180.7 2.6 copy.41
  183.2 2.5 copy.51
  185.7 224.3 %collective-permute-done.8 = f32[512,512]{0,1:T(8,128)} collective-permute-done((f32[512,512]{0,1:T(8,128)}, f32[512,512]{0,1:T(8,128)}, u32[]{:S(2)}, u32[]{:S(2)}) %collective-permute-start.8) | collective-permute-done | bytes 1048608 | tf_op jit(solution)/shard_map/ppermute | solution.py:71
  410.1 2.2 fusion.16
  412.3 9.0 %collective-permute-done.9 = f32[512,512]{0,1:T(8,128)} collective-permute-done((f32[512,512]{0,1:T(8,128)}, f32[512,512]{0,1:T(8,128)}, u32[]{:S(2)}, u32[]{:S(2)}) %collective-permute-start.9) | collective-permute-done | bytes 1048608 | tf_op jit(solution)/shard_map/ppermute | solution.py:71
  421.3 2.3 fusion.17
  423.6 8.9 %collective-permute-done.10 = f32[512,512]{0,1:T(8,128)} collective-permute-done((f32[512,512]{0,1:T(8,128)}, f32[512,512]{0,1:T(8,128)}, u32[]{:S(2)}, u32[]{:S(2)}) %collective-permute-start.10) | collective-permute-done | bytes 1048608 | tf_op jit(solution)/shard_map/ppermute | solution.py:71
  432.6 2.2 fusion.18
  434.7 1.7 fusion
  (49 shorter events, 1.6 us)
Async XLA Ops:
  0.0 1.4 copy-start.1
  1.4 11.4 %copy-start.12 = (s32[32,32]{1,0:T(8,128)S(1)}, s32[32,32]{1,0:T(8,128)}, u32[]{:S(2)}) copy-start(s32[32,32]{1,0:T(8,128)} %param.6) | copy-start | bytes 12292
  2.8 133.1 %collective-permute-start = (bf16[3,512,512]{2,1,0:T(8,128)(2,1)}, bf16[3,512,512]{2,1,0:T(8,128)(2,1)}, u32[]{:S(2)}, u32[]{:S(2)}) collective-permute-start(bf16[3,512,512]{2,1,0:T(8,128)(2,1)} %broadcast_multiply_fusion), channel_id=1, source_target_pairs={{15,0},{2,1},{1,2},{4,3},{3,4},{6,5},{5,6},{8,7},{7,8},{10,9},{9,1... | collective-permute-start | bytes 4718600 | tf_op jit(solution)/shard_map/ppermute | solution.py:50
  3.0 123.9 %collective-permute-start.4 = (bf16[3,512,512]{2,1,0:T(8,128)(2,1)}, bf16[3,512,512]{2,1,0:T(8,128)(2,1)}, u32[]{:S(2)}, u32[]{:S(2)}) collective-permute-start(bf16[3,512,512]{2,1,0:T(8,128)(2,1)} %broadcast_multiply_fusion), channel_id=1, source_target_pairs={{0,1},{1,0},{2,3},{3,2},{4,5},{5,4},{6,7},{7,6},{8,9},{9,8},{10,11... | collective-permute-start | bytes 4718600 | tf_op jit(solution)/shard_map/ppermute | solution.py:52
  4.7 125.2 %collective-permute-start.3 = (bf16[3,512,512]{2,1,0:T(8,128)(2,1)}, bf16[3,512,512]{2,1,0:T(8,128)(2,1)}, u32[]{:S(2)}, u32[]{:S(2)}) collective-permute-start(bf16[3,512,512]{2,1,0:T(8,128)(2,1)} %broadcast_multiply_fusion), channel_id=1, source_target_pairs={{12,0},{5,1},{14,2},{7,3},{0,4},{9,5},{2,6},{11,7},{4,8},{13,9},{6... | collective-permute-start | bytes 4718600 | tf_op jit(solution)/shard_map/ppermute | solution.py:50
  7.3 96.4 %collective-permute-start.2 = (bf16[3,512,512]{2,1,0:T(8,128)(2,1)}, bf16[3,512,512]{2,1,0:T(8,128)(2,1)}, u32[]{:S(2)}, u32[]{:S(2)}) collective-permute-start(bf16[3,512,512]{2,1,0:T(8,128)(2,1)} %broadcast_multiply_fusion), channel_id=1, source_target_pairs={{13,0},{4,1},{15,2},{6,3},{1,4},{8,5},{3,6},{10,7},{5,8},{12,9},{7... | collective-permute-start | bytes 4718600 | tf_op jit(solution)/shard_map/ppermute | solution.py:50
  8.4 118.4 %collective-permute-start.1 = (bf16[3,512,512]{2,1,0:T(8,128)(2,1)}, bf16[3,512,512]{2,1,0:T(8,128)(2,1)}, u32[]{:S(2)}, u32[]{:S(2)}) collective-permute-start(bf16[3,512,512]{2,1,0:T(8,128)(2,1)} %broadcast_multiply_fusion), channel_id=1, source_target_pairs={{14,0},{3,1},{0,2},{5,3},{2,4},{7,5},{4,6},{9,7},{6,8},{11,9},{8,1... | collective-permute-start | bytes 4718600 | tf_op jit(solution)/shard_map/ppermute | solution.py:50
  27.3 3.5 slice-start
  29.9 2.2 slice-start.1
  35.8 91.0 %copy-start = (bf16[4608,512]{1,0:T(8,128)(2,1)S(1)}, bf16[4608,512]{1,0:T(8,128)(2,1)}, u32[]{:S(2)}) copy-start(bf16[4608,512]{1,0:T(8,128)(2,1)} %mul.113) | copy-start | bytes 14155780
  103.6 48.7 %collective-permute-start.7 = (bf16[3,512,512]{2,1,0:T(8,128)(2,1)}, bf16[3,512,512]{2,1,0:T(8,128)(2,1)S(1)}, u32[]{:S(2)}, u32[]{:S(2)}) collective-permute-start(bf16[3,512,512]{2,1,0:T(8,128)(2,1)} %collective-permute-done.2), channel_id=1, source_target_pairs={{0,1},{1,0},{2,3},{3,2},{4,5},{5,4},{6,7},{7,6},{8,9},{9,8},{10,11... | collective-permute-start | bytes 4718600 | tf_op jit(solution)/shard_map/ppermute | solution.py:53
  126.8 26.0 %collective-permute-start.6 = (bf16[3,512,512]{2,1,0:T(8,128)(2,1)}, bf16[3,512,512]{2,1,0:T(8,128)(2,1)S(1)}, u32[]{:S(2)}, u32[]{:S(2)}) collective-permute-start(bf16[3,512,512]{2,1,0:T(8,128)(2,1)} %collective-permute-done.1), channel_id=1, source_target_pairs={{0,1},{1,0},{2,3},{3,2},{4,5},{5,4},{6,7},{7,6},{8,9},{9,8},{10,11... | collective-permute-start | bytes 4718600 | tf_op jit(solution)/shard_map/ppermute | solution.py:53
  135.9 17.6 %collective-permute-start.5 = (bf16[3,512,512]{2,1,0:T(8,128)(2,1)}, bf16[3,512,512]{2,1,0:T(8,128)(2,1)S(1)}, u32[]{:S(2)}, u32[]{:S(2)}) collective-permute-start(bf16[3,512,512]{2,1,0:T(8,128)(2,1)} %collective-permute-done), channel_id=1, source_target_pairs={{0,1},{1,0},{2,3},{3,2},{4,5},{5,4},{6,7},{7,6},{8,9},{9,8},{10,11... | collective-permute-start | bytes 4718600 | tf_op jit(solution)/shard_map/ppermute | solution.py:53
  152.3 1.1 copy-start.7
  152.8 1.2 copy-start.8
  154.0 1.2 copy-start.10
  157.1 5.3 %copy-start.9 = (bf16[3,512,512]{2,1,0:T(8,128)(2,1)S(1)}, bf16[3,512,512]{2,1,0:T(8,128)(2,1)}, u32[]{:S(2)}) copy-start(bf16[3,512,512]{2,1,0:T(8,128)(2,1)} %copy-done.8) | copy-start | bytes 4718596
  157.1 253.0 %collective-permute-start.8 = (f32[512,512]{0,1:T(8,128)}, f32[512,512]{0,1:T(8,128)}, u32[]{:S(2)}, u32[]{:S(2)}) collective-permute-start(f32[512,512]{0,1:T(8,128)} %copy.31), channel_id=1, source_target_pairs={{0,0},{1,16},{2,32},{3,48},{4,64},{5,80},{6,96},{7,112},{8,128},{9... | collective-permute-start | bytes 3145736 | tf_op jit(solution)/shard_map/ppermute | solution.py:71
  160.6 3.5 copy-start.11
  162.4 1.6 copy-start.3
  166.6 254.7 %collective-permute-start.9 = (f32[512,512]{0,1:T(8,128)}, f32[512,512]{0,1:T(8,128)}, u32[]{:S(2)}, u32[]{:S(2)}) collective-permute-start(f32[512,512]{0,1:T(8,128)} %fusion.7), channel_id=1, source_target_pairs={{0,0},{1,16},{2,32},{3,48},{4,64},{5,80},{6,96},{7,112},{8,128},{9... | collective-permute-start | bytes 3145736 | tf_op jit(solution)/shard_map/ppermute | solution.py:71
  170.6 1.8 copy-start.2
  174.9 257.6 %collective-permute-start.10 = (f32[512,512]{0,1:T(8,128)}, f32[512,512]{0,1:T(8,128)}, u32[]{:S(2)}, u32[]{:S(2)}) collective-permute-start(f32[512,512]{0,1:T(8,128)} %fusion.2), channel_id=1, source_target_pairs={{0,0},{1,16},{2,32},{3,48},{4,64},{5,80},{6,96},{7,112},{8,128},{9... | collective-permute-start | bytes 3145736 | tf_op jit(solution)/shard_map/ppermute | solution.py:71
  178.6 1.4 copy-start.13
  410.1 11.2 %copy-start.6 = (f32[512,512]{1,0:T(8,128)S(1)}, f32[512,512]{1,0:T(8,128)}, u32[]{:S(2)}) copy-start(f32[512,512]{1,0:T(8,128)} %copy.41) | copy-start | bytes 3145732
  421.3 11.2 %copy-start.5 = (f32[512,512]{1,0:T(8,128)S(1)}, f32[512,512]{1,0:T(8,128)}, u32[]{:S(2)}) copy-start(f32[512,512]{1,0:T(8,128)} %copy.51) | copy-start | bytes 3145732
  432.6 2.2 copy-start.4

commit v3 on v2

--- a/solution.py
+++ b/solution.py
@@ -41,36 +41,45 @@
     strip_local = mask_blocks(p0_columns, strip_occ)
 
     sign = jnp.where(col_at % 2 == 0, -1, 1)
-    fetched = []
+    fetch_pairs = []
     for k in range(col_span):
         pairs = []
         for c in range(col_count):
             src = c - 1 - k if c % 2 == 0 else c + 1 + k
             pairs.append((src % col_count, c))
-        fetched.append(lax.ppermute(p1_local, "col", pairs))
+        fetch_pairs.append(pairs)
     swap = [(c, c ^ 1) for c in range(col_count)]
-    partner_own = lax.ppermute(p1_local, "col", swap)
-    partner_fetched = [lax.ppermute(fetched[j], "col", swap) for j in range(col_span - 1)]
-
-    tiles = [(p1_local, 0)]
-    tiles += [(fetched[k], sign * (k + 1)) for k in range(col_span)]
-    tiles += [(partner_own, -sign)]
-    tiles += [(partner_fetched[j], -sign * (j + 2)) for j in range(col_span - 1)]
+    offsets = [0] + [sign * (k + 1) for k in range(col_span)] + [-sign]
+    offsets += [-sign * (j + 2) for j in range(col_span - 1)]
     factors = []
-    for _, offset in tiles:
+    for offset in offsets:
         start = (offset + col_span) * col_width
         factors.append(lax.dynamic_slice_in_dim(strip_local, start, col_width, 0))
 
     pairs = [(i * col_count + j, j * col_count + i) for i in range(row_count) for j in range(col_count)]
     squared = sp2_branch == 1
     outs = []
+    products = []
+    mirrors = []
     for d in range(p1_tiles.shape[0]):
+        own = p1_local[d]
+        if d >= 1:
+            own = lax.optimization_barrier((own, products[d - 1]))[0]
+        if d >= 2:
+            own = lax.optimization_barrier((own, mirrors[d - 2]))[0]
+        fetched = [lax.ppermute(own, "col", fp) for fp in fetch_pairs]
+        partner_own = lax.ppermute(own, "col", swap)
+        partner_fetched = [lax.ppermute(fetched[j], "col", swap) for j in range(col_span - 1)]
+        tiles = [own] + fetched + [partner_own] + partner_fetched
         summed = jnp.zeros((row_height, col_width), jnp.float32)
-        for (tile, _), factor in zip(tiles, factors):
-            summed = summed + jnp.dot(tile[d], factor, preferred_element_type=jnp.float32)
-        mirrored = lax.ppermute(summed, ("row", "col"), pairs).T
+        for tile, factor in zip(tiles, factors):
+            summed = summed + jnp.dot(tile, factor, preferred_element_type=jnp.float32)
+        products.append(summed)
+        mirrored = lax.ppermute(summed, ("row", "col"), pairs)
+        mirrors.append(mirrored)
+        mirrored = mirrored.T
         bracket = summed + mirrored
-        chosen = jnp.where(squared[d], bracket, 2.0 * p1_local[d].astype(jnp.float32) - bracket)
+        chosen = jnp.where(squared[d], bracket, 2.0 * own.astype(jnp.float32) - bracket)
         outs.append(chosen)
     chosen = jnp.stack(outs)
     return mask_blocks(chosen, own_occ).astype(jnp.bfloat16)

time: 442 us -> 428 us (0.968)
  starting transfers between devices: 20.2 us -> 140 us
  waiting for transfers between devices: 332 us -> 217 us
  matrix products: 39.3 us -> 23.6 us
    ppermute x8 -> x18, waiting for transfers between devices: 332 us -> 217 us  [the longest x3 177 us: body(): mirrored = lax.ppermute(summed, ('row', 'col'), pairs)]
    ppermute x8 -> x18, starting transfers between devices: 19.6 us -> 121 us  [the longest x12 72.6 us: body(): fetched = [lax.ppermute(own, 'col', fp) for fp in fetch_pairs]]
    ppermute x3 -> x9, starting transfers between devices: 0.59 us -> 18.8 us  [body(): lax.ppermute(fetched[j], 'col', swap)]
    dot_general x27, matrix products: 39.3 us -> 23.6 us  [body(): summed = summed + jnp.dot(tile, factor, preferred_element_type=jnp.float32)]
  transfers between devices with their start and end apart: 11 -> 27, of which waited for: 5 -> 7; matrix products, arithmetic and copies ran while one was open for 17% -> 13% of each run, Pallas kernels for 0% -> 0%
where the time goes in v3:
time: 428 us; the launch traced here: 425 us
  waiting for transfers between devices  217 us (51%)
  starting transfers between devices  140 us (33%)
  local copies, waits for them, and re-layouts  25.5 us (6%)
  matrix products  23.6 us (6%)
  other arithmetic  19.6 us (5%)
    ppermute x3, waiting for transfers between devices, body(): mirrored = lax.ppermute(summed, ('row', 'col'), pairs)  177 us
    ppermute x12, starting transfers between devices, body(): fetched = [lax.ppermute(own, 'col', fp) for fp in fetch_pairs]  72.6 us
    ppermute x3, starting transfers between devices, body(): partner_own = lax.ppermute(own, 'col', swap)  40.2 us
    ppermute x12, waiting for transfers between devices, body(): fetched = [lax.ppermute(own, 'col', fp) for fp in fetch_pairs]  39.8 us
    dot_general x27, matrix products, body(): summed = summed + jnp.dot(tile, factor, preferred_element_type=jnp.float32)  23.6 us
    ppermute x9, starting transfers between devices, body(): lax.ppermute(fetched[j], 'col', swap)  18.8 us
    reshape x2, local copies, waits for them, and re-layouts, mask_blocks(): shaped = values.reshape(leading + (row_blocks, BLK, col_blocks, BLK))  10.1 us
    another operation x3, other arithmetic, body(): chosen = jnp.stack(outs)  8.89 us
  transfers between devices with their start and end apart: 27, of which 7 were waited for; matrix products, arithmetic and copies ran while one was open for 13% of the time, Pallas kernels for 0%

profile of v3, /device:TPU:218, one launch (start us, length us, event | category | flops | bytes accessed | tf_op | source)
XLA Modules:
  0.0 425.5 jit_solution(10369077393058121152)
XLA Ops:
  0.0 2.4 reshape.34
  2.4 0.8 dynamic-slice_convert_fusion
  3.2 1.4 broadcast_multiply_fusion
  4.6 1.9 fusion.88
  6.8 1.7 collective-permute-start.4
  8.5 2.6 collective-permute-start.3
  11.1 1.1 collective-permute-start.2
  12.2 4.4 %collective-permute-start.1 = (bf16[512,512]{1,0:T(8,128)(2,1)S(1)}, bf16[512,512]{1,0:T(8,128)(2,1)S(1)}, u32[]{:S(2)}, u32[]{:S(2)}) collective-permute-start(bf16[512,512]{1,0:T(8,128)(2,1)S(1)} %bitcast.89), channel_id=1, source_target_pairs={{14,0},{3,1},{0,2},{5,3},{2,4},{7,5},{4,6},{9,7},{6,8},{11,9},{8,1... | collective-permute-start | bytes 1572872 | tf_op jit(solution)/shard_map/ppermute | solution.py:70
  16.9 7.7 %reshape.35 = bf16[18,256,2,256]{3,2,1,0:T(2,128)(2,1)} reshape(bf16[4608,512]{1,0:T(8,128)(2,1)} %param.8) | data formatting | bytes 9437184 | tf_op jit(solution)/shard_map/reshape | solution.py:13
  24.6 1.6 slice_multiply_fusion
  26.3 2.5 mul.97
  28.8 1.0 copy.72
  29.8 1.2 slice-done.3
  31.0 3.6 mul.100
  34.5 0.9 copy.73
  35.9 11.3 %collective-permute-done.2 = bf16[512,512]{1,0:T(8,128)(2,1)S(1)} collective-permute-done((bf16[512,512]{1,0:T(8,128)(2,1)S(1)}, bf16[512,512]{1,0:T(8,128)(2,1)S(1)}, u32[]{:S(2)}, u32[]{:S(2)}) %collective-permute-start.2) | collective-permute-done | bytes 524320 | tf_op jit(solution)/shard_map/ppermute | solution.py:70
  47.2 3.1 collective-permute-done.1
  50.4 0.5 collective-permute-start.5
  50.9 1.5 fusion.51
  52.4 1.6 fusion.39
  54.0 1.5 convolution_add_fusion.7
  55.5 1.5 fusion.45
  57.0 0.5 fusion.16
  58.5 0.5 fusion.13
  59.0 1.8 collective-permute-start.11
  60.9 1.3 copy.31
  62.2 2.5 collective-permute-start.9
  64.6 1.4 collective-permute-start.12
  66.0 3.8 collective-permute-start.10
  69.8 1.6 fusion.91
  71.4 17.9 %collective-permute-done.11 = bf16[512,512]{1,0:T(8,128)(2,1)} collective-permute-done((bf16[512,512]{1,0:T(8,128)(2,1)}, bf16[512,512]{1,0:T(8,128)(2,1)}, u32[]{:S(2)}, u32[]{:S(2)}) %collective-permute-start.11) | collective-permute-done | bytes 524320 | tf_op jit(solution)/shard_map/ppermute | solution.py:70
  89.3 2.9 collective-permute-start.8
  92.2 1.7 fusion.49
  93.9 0.6 collective-permute-start.16
  94.5 5.0 %collective-permute-done.10 = bf16[512,512]{1,0:T(8,128)(2,1)S(1)} collective-permute-done((bf16[512,512]{1,0:T(8,128)(2,1)}, bf16[512,512]{1,0:T(8,128)(2,1)S(1)}, u32[]{:S(2)}, u32[]{:S(2)}) %collective-permute-start.10) | collective-permute-done | bytes 524320 | tf_op jit(solution)/shard_map/ppermute | solution.py:70
  99.6 2.4 collective-permute-done.12
  101.9 1.5 fusion.43
  103.5 1.5 convolution_add_fusion.4
  105.5 0.5 fusion.11
  106.1 0.5 fusion.28
  106.6 0.5 fusion.22
  107.1 1.5 fusion.8
  108.6 70.5 %collective-permute-done.8 = f32[512,512]{0,1:T(8,128)S(1)} collective-permute-done((f32[512,512]{0,1:T(8,128)}, f32[512,512]{0,1:T(8,128)S(1)}, u32[]{:S(2)}, u32[]{:S(2)}) %collective-permute-start.8) | collective-permute-done | bytes 1048608 | tf_op jit(solution)/shard_map/ppermute | solution.py:78
  179.1 2.2 collective-permute-start.17
  181.3 53.2 %collective-permute-start.18 = (bf16[512,512]{1,0:T(8,128)(2,1)S(1)}, bf16[512,512]{1,0:T(8,128)(2,1)S(1)}, u32[]{:S(2)}, u32[]{:S(2)}) collective-permute-start(bf16[512,512]{1,0:T(8,128)(2,1)S(1)} %bitcast.80), channel_id=1, source_target_pairs={{15,0},{2,1},{1,2},{4,3},{3,4},{6,5},{5,6},{8,7},{7,8},{10,9},{9,1... | collective-permute-start | bytes 1572872 | tf_op jit(solution)/shard_map/ppermute | solution.py:70
  234.5 1.6 collective-permute-start.21
  236.1 38.5 %collective-permute-start.22 = (bf16[512,512]{1,0:T(8,128)(2,1)S(1)}, bf16[512,512]{1,0:T(8,128)(2,1)S(1)}, u32[]{:S(2)}, u32[]{:S(2)}) collective-permute-start(bf16[512,512]{1,0:T(8,128)(2,1)S(1)} %bitcast.82), channel_id=1, source_target_pairs={{0,1},{1,0},{2,3},{3,2},{4,5},{5,4},{6,7},{7,6},{8,9},{9,8},{10,11... | collective-permute-start | bytes 1572872 | tf_op jit(solution)/shard_map/ppermute | solution.py:71
  275.2 0.5 fusion.47
  275.7 8.0 %collective-permute-start.25 = (bf16[512,512]{1,0:T(8,128)(2,1)S(1)}, bf16[512,512]{1,0:T(8,128)(2,1)S(1)}, u32[]{:S(2)}, u32[]{:S(2)}) collective-permute-start(bf16[512,512]{1,0:T(8,128)(2,1)S(1)} %collective-permute-done.20), channel_id=1, source_target_pairs={{0,1},{1,0},{2,3},{3,2},{4,5},{5,4},{6,7},{7,6},{8,9},{9,8},{10,11... | collective-permute-start | bytes 1572872 | tf_op jit(solution)/shard_map/ppermute | solution.py:72
  284.2 9.6 %collective-permute-start.23 = (bf16[512,512]{1,0:T(8,128)(2,1)S(1)}, bf16[512,512]{1,0:T(8,128)(2,1)S(1)}, u32[]{:S(2)}, u32[]{:S(2)}) collective-permute-start(bf16[512,512]{1,0:T(8,128)(2,1)S(1)} %collective-permute-done.18), channel_id=1, source_target_pairs={{0,1},{1,0},{2,3},{3,2},{4,5},{5,4},{6,7},{7,6},{8,9},{9,8},{10,11... | collective-permute-start | bytes 1572872 | tf_op jit(solution)/shard_map/ppermute | solution.py:72
  294.3 0.5 fusion.35
  294.8 0.6 fusion.6
  295.9 0.5 fusion.20
  296.4 1.5 fusion.2
  297.9 2.9 collective-permute-start.26
  301.2 1.1 copy.75
  302.3 0.7 fusion.89
  302.9 2.5 copy.41
  305.5 3.1 fusion.17
  308.6 3.7 fusion.18
  312.3 1.6 copy.51
  313.9 106.3 %collective-permute-done.26 = f32[512,512]{0,1:T(8,128)} collective-permute-done((f32[512,512]{0,1:T(8,128)}, f32[512,512]{0,1:T(8,128)}, u32[]{:S(2)}, u32[]{:S(2)}) %collective-permute-start.26) | collective-permute-done | bytes 1048608 | tf_op jit(solution)/shard_map/ppermute | solution.py:78
  420.1 2.1 fusion.19
  422.2 3.3 fusion
  (67 shorter events, 5.1 us)
Async XLA Ops:
  0.0 16.6 %copy-start.4 = (s32[32,32]{1,0:T(8,128)S(1)}, s32[32,32]{1,0:T(8,128)}, u32[]{:S(2)}) copy-start(s32[32,32]{1,0:T(8,128)} %param.6) | copy-start | bytes 12292
  6.5 43.8 %collective-permute-start = (bf16[512,512]{1,0:T(8,128)(2,1)S(1)}, bf16[512,512]{1,0:T(8,128)(2,1)}, u32[]{:S(2)}, u32[]{:S(2)}) collective-permute-start(bf16[512,512]{1,0:T(8,128)(2,1)S(1)} %bitcast.85), channel_id=1, source_target_pairs={{15,0},{2,1},{1,2},{4,3},{3,4},{6,5},{5,6},{8,7},{7,8},{10,9},{9,1... | collective-permute-start | bytes 1572872 | tf_op jit(solution)/shard_map/ppermute | solution.py:70
  6.8 45.6 %collective-permute-start.4 = (bf16[512,512]{1,0:T(8,128)(2,1)S(1)}, bf16[512,512]{1,0:T(8,128)(2,1)}, u32[]{:S(2)}, u32[]{:S(2)}) collective-permute-start(bf16[512,512]{1,0:T(8,128)(2,1)S(1)} %bitcast.86), channel_id=1, source_target_pairs={{0,1},{1,0},{2,3},{3,2},{4,5},{5,4},{6,7},{7,6},{8,9},{9,8},{10,11... | collective-permute-start | bytes 1572872 | tf_op jit(solution)/shard_map/ppermute | solution.py:71
  8.5 47.0 %collective-permute-start.3 = (bf16[512,512]{1,0:T(8,128)(2,1)S(1)}, bf16[512,512]{1,0:T(8,128)(2,1)}, u32[]{:S(2)}, u32[]{:S(2)}) collective-permute-start(bf16[512,512]{1,0:T(8,128)(2,1)S(1)} %bitcast.87), channel_id=1, source_target_pairs={{12,0},{5,1},{14,2},{7,3},{0,4},{9,5},{2,6},{11,7},{4,8},{13,9},{6... | collective-permute-start | bytes 1572872 | tf_op jit(solution)/shard_map/ppermute | solution.py:70
  11.1 36.1 %collective-permute-start.2 = (bf16[512,512]{1,0:T(8,128)(2,1)S(1)}, bf16[512,512]{1,0:T(8,128)(2,1)S(1)}, u32[]{:S(2)}, u32[]{:S(2)}) collective-permute-start(bf16[512,512]{1,0:T(8,128)(2,1)S(1)} %bitcast.88), channel_id=1, source_target_pairs={{13,0},{4,1},{15,2},{6,3},{1,4},{8,5},{3,6},{10,7},{5,8},{12,9},{7... | collective-permute-start | bytes 1572872 | tf_op jit(solution)/shard_map/ppermute | solution.py:70
  12.2 38.2 %collective-permute-start.1 = (bf16[512,512]{1,0:T(8,128)(2,1)S(1)}, bf16[512,512]{1,0:T(8,128)(2,1)S(1)}, u32[]{:S(2)}, u32[]{:S(2)}) collective-permute-start(bf16[512,512]{1,0:T(8,128)(2,1)S(1)} %bitcast.89), channel_id=1, source_target_pairs={{14,0},{3,1},{0,2},{5,3},{2,4},{7,5},{4,6},{9,7},{6,8},{11,9},{8,1... | collective-permute-start | bytes 1572872 | tf_op jit(solution)/shard_map/ppermute | solution.py:70
  26.3 3.5 slice-start.2
  28.8 2.2 slice-start.3
  35.5 18.5 %copy-start = (bf16[4608,512]{1,0:T(8,128)(2,1)S(1)}, bf16[4608,512]{1,0:T(8,128)(2,1)}, u32[]{:S(2)}) copy-start(bf16[4608,512]{1,0:T(8,128)(2,1)} %mul.100) | copy-start | bytes 14155780
  47.2 10.3 %collective-permute-start.7 = (bf16[512,512]{1,0:T(8,128)(2,1)S(1)}, bf16[512,512]{1,0:T(8,128)(2,1)S(1)}, u32[]{:S(2)}, u32[]{:S(2)}) collective-permute-start(bf16[512,512]{1,0:T(8,128)(2,1)S(1)} %collective-permute-done.2), channel_id=1, source_target_pairs={{0,1},{1,0},{2,3},{3,2},{4,5},{5,4},{6,7},{7,6},{8,9},{9,8},{10,11... | collective-permute-start | bytes 1572872 | tf_op jit(solution)/shard_map/ppermute | solution.py:72
  50.4 7.6 %collective-permute-start.6 = (bf16[512,512]{1,0:T(8,128)(2,1)S(1)}, bf16[512,512]{1,0:T(8,128)(2,1)S(1)}, u32[]{:S(2)}, u32[]{:S(2)}) collective-permute-start(bf16[512,512]{1,0:T(8,128)(2,1)S(1)} %collective-permute-done.1), channel_id=1, source_target_pairs={{0,1},{1,0},{2,3},{3,2},{4,5},{5,4},{6,7},{7,6},{8,9},{9,8},{10,11... | collective-permute-start | bytes 1572872 | tf_op jit(solution)/shard_map/ppermute | solution.py:72
  50.4 8.1 %collective-permute-start.5 = (bf16[512,512]{1,0:T(8,128)(2,1)}, bf16[512,512]{1,0:T(8,128)(2,1)S(1)}, u32[]{:S(2)}, u32[]{:S(2)}) collective-permute-start(bf16[512,512]{1,0:T(8,128)(2,1)} %collective-permute-done), channel_id=1, source_target_pairs={{0,1},{1,0},{2,3},{3,2},{4,5},{5,4},{6,7},{7,6},{8,9},{9,8},{10,11... | collective-permute-start | bytes 1572872 | tf_op jit(solution)/shard_map/ppermute | solution.py:72
  57.5 3.2 copy-start.2
  58.5 46.5 %slice-start = ((s8[4718592]{0:T(1024)(128)(4,1)}), s8[524288]{0:T(1024)(128)(4,1)S(1)}, s32[]{:S(2)}) async-start(s8[4718592]{0:T(1024)(128)(4,1)} %bitcast.69), calls=%async_computation | async-start | bytes 1048576
  59.0 30.3 %collective-permute-start.11 = (bf16[512,512]{1,0:T(8,128)(2,1)}, bf16[512,512]{1,0:T(8,128)(2,1)}, u32[]{:S(2)}, u32[]{:S(2)}) collective-permute-start(bf16[512,512]{1,0:T(8,128)(2,1)} %bitcast.20), channel_id=1, source_target_pairs={{13,0},{4,1},{15,2},{6,3},{1,4},{8,5},{3,6},{10,7},{5,8},{12,9},{7... | collective-permute-start | bytes 1572872 | tf_op jit(solution)/shard_map/ppermute | solution.py:70
  62.2 42.9 %slice-start.1 = ((s8[4718592]{0:T(1024)(128)(4,1)}), s8[4194304]{0:T(1024)(128)(4,1)S(1)}, s32[]{:S(2)}) async-start(s8[4718592]{0:T(1024)(128)(4,1)} %bitcast.69), calls=%async_computation.1 | async-start | bytes 8388608
  62.2 31.7 %collective-permute-start.9 = (bf16[512,512]{1,0:T(8,128)(2,1)}, bf16[512,512]{1,0:T(8,128)(2,1)S(1)}, u32[]{:S(2)}, u32[]{:S(2)}) collective-permute-start(bf16[512,512]{1,0:T(8,128)(2,1)} %bitcast.20), channel_id=1, source_target_pairs={{15,0},{2,1},{1,2},{4,3},{3,4},{6,5},{5,6},{8,7},{7,8},{10,9},{9,1... | collective-permute-start | bytes 1572872 | tf_op jit(solution)/shard_map/ppermute | solution.py:70
  64.6 37.3 %collective-permute-start.12 = (bf16[512,512]{1,0:T(8,128)(2,1)}, bf16[512,512]{1,0:T(8,128)(2,1)S(1)}, u32[]{:S(2)}, u32[]{:S(2)}) collective-permute-start(bf16[512,512]{1,0:T(8,128)(2,1)} %bitcast.20), channel_id=1, source_target_pairs={{12,0},{5,1},{14,2},{7,3},{0,4},{9,5},{2,6},{11,7},{4,8},{13,9},{6... | collective-permute-start | bytes 1572872 | tf_op jit(solution)/shard_map/ppermute | solution.py:70
  66.0 39.0 %collective-permute-start.13 = (bf16[512,512]{1,0:T(8,128)(2,1)}, bf16[512,512]{1,0:T(8,128)(2,1)S(1)}, u32[]{:S(2)}, u32[]{:S(2)}) collective-permute-start(bf16[512,512]{1,0:T(8,128)(2,1)} %bitcast.20), channel_id=1, source_target_pairs={{0,1},{1,0},{2,3},{3,2},{4,5},{5,4},{6,7},{7,6},{8,9},{9,8},{10,11... | collective-permute-start | bytes 1572872 | tf_op jit(solution)/shard_map/ppermute | solution.py:71
  66.0 33.5 %collective-permute-start.10 = (bf16[512,512]{1,0:T(8,128)(2,1)}, bf16[512,512]{1,0:T(8,128)(2,1)S(1)}, u32[]{:S(2)}, u32[]{:S(2)}) collective-permute-start(bf16[512,512]{1,0:T(8,128)(2,1)} %bitcast.20), channel_id=1, source_target_pairs={{14,0},{3,1},{0,2},{5,3},{2,4},{7,5},{4,6},{9,7},{6,8},{11,9},{8,1... | collective-permute-start | bytes 1572872 | tf_op jit(solution)/shard_map/ppermute | solution.py:70
  89.3 89.8 %collective-permute-start.8 = (f32[512,512]{0,1:T(8,128)}, f32[512,512]{0,1:T(8,128)S(1)}, u32[]{:S(2)}, u32[]{:S(2)}) collective-permute-start(f32[512,512]{0,1:T(8,128)} %copy.31), channel_id=1, source_target_pairs={{0,0},{1,16},{2,32},{3,48},{4,64},{5,80},{6,96},{7,112},{8,128},{9... | collective-permute-start | bytes 3145736 | tf_op jit(solution)/shard_map/ppermute | solution.py:78
  93.9 12.7 %collective-permute-start.16 = (bf16[512,512]{1,0:T(8,128)(2,1)}, bf16[512,512]{1,0:T(8,128)(2,1)S(1)}, u32[]{:S(2)}, u32[]{:S(2)}) collective-permute-start(bf16[512,512]{1,0:T(8,128)(2,1)} %collective-permute-done.11), channel_id=1, source_target_pairs={{0,1},{1,0},{2,3},{3,2},{4,5},{5,4},{6,7},{7,6},{8,9},{9,8},{10,11... | collective-permute-start | bytes 1572872 | tf_op jit(solution)/shard_map/ppermute | solution.py:72
  99.6 6.5 %collective-permute-start.15 = (bf16[512,512]{1,0:T(8,128)(2,1)S(1)}, bf16[512,512]{1,0:T(8,128)(2,1)S(1)}, u32[]{:S(2)}, u32[]{:S(2)}) collective-permute-start(bf16[512,512]{1,0:T(8,128)(2,1)S(1)} %collective-permute-done.10), channel_id=1, source_target_pairs={{0,1},{1,0},{2,3},{3,2},{4,5},{5,4},{6,7},{7,6},{8,9},{9,8},{10,11... | collective-permute-start | bytes 1572872 | tf_op jit(solution)/shard_map/ppermute | solution.py:72
  101.9 5.2 %collective-permute-start.14 = (bf16[512,512]{1,0:T(8,128)(2,1)S(1)}, bf16[512,512]{1,0:T(8,128)(2,1)S(1)}, u32[]{:S(2)}, u32[]{:S(2)}) collective-permute-start(bf16[512,512]{1,0:T(8,128)(2,1)S(1)} %collective-permute-done.9), channel_id=1, source_target_pairs={{0,1},{1,0},{2,3},{3,2},{4,5},{5,4},{6,7},{7,6},{8,9},{9,8},{10,11... | collective-permute-start | bytes 1572872 | tf_op jit(solution)/shard_map/ppermute | solution.py:72
  179.1 115.2 %copy-start.3 = (f32[512,512]{0,1:T(8,128)}, f32[512,512]{0,1:T(8,128)S(1)}, u32[]{:S(2)}) copy-start(f32[512,512]{0,1:T(8,128)S(1)} %collective-permute-done.8) | copy-start | bytes 3145732
  179.1 57.0 %collective-permute-start.19 = (bf16[512,512]{1,0:T(8,128)(2,1)S(1)}, bf16[512,512]{1,0:T(8,128)(2,1)S(1)}, u32[]{:S(2)}, u32[]{:S(2)}) collective-permute-start(bf16[512,512]{1,0:T(8,128)(2,1)S(1)} %bitcast.78), channel_id=1, source_target_pairs={{14,0},{3,1},{0,2},{5,3},{2,4},{7,5},{4,6},{9,7},{6,8},{11,9},{8,1... | collective-permute-start | bytes 1572872 | tf_op jit(solution)/shard_map/ppermute | solution.py:70
  179.1 96.0 %collective-permute-start.20 = (bf16[512,512]{1,0:T(8,128)(2,1)S(1)}, bf16[512,512]{1,0:T(8,128)(2,1)S(1)}, u32[]{:S(2)}, u32[]{:S(2)}) collective-permute-start(bf16[512,512]{1,0:T(8,128)(2,1)S(1)} %bitcast.79), channel_id=1, source_target_pairs={{13,0},{4,1},{15,2},{6,3},{1,4},{8,5},{3,6},{10,7},{5,8},{12,9},{7... | collective-permute-start | bytes 1572872 | tf_op jit(solution)/shard_map/ppermute | solution.py:70
  179.1 129.5 %collective-permute-start.17 = (f32[512,512]{0,1:T(8,128)}, f32[512,512]{0,1:T(8,128)}, u32[]{:S(2)}, u32[]{:S(2)}) collective-permute-start(f32[512,512]{0,1:T(8,128)} %fusion.8), channel_id=1, source_target_pairs={{0,0},{1,16},{2,32},{3,48},{4,64},{5,80},{6,96},{7,112},{8,128},{9... | collective-permute-start | bytes 3145736 | tf_op jit(solution)/shard_map/ppermute | solution.py:78
  181.3 94.4 %collective-permute-start.18 = (bf16[512,512]{1,0:T(8,128)(2,1)S(1)}, bf16[512,512]{1,0:T(8,128)(2,1)S(1)}, u32[]{:S(2)}, u32[]{:S(2)}) collective-permute-start(bf16[512,512]{1,0:T(8,128)(2,1)S(1)} %bitcast.80), channel_id=1, source_target_pairs={{15,0},{2,1},{1,2},{4,3},{3,4},{6,5},{5,6},{8,7},{7,8},{10,9},{9,1... | collective-permute-start | bytes 1572872 | tf_op jit(solution)/shard_map/ppermute | solution.py:70
  234.5 49.6 %collective-permute-start.21 = (bf16[512,512]{1,0:T(8,128)(2,1)S(1)}, bf16[512,512]{1,0:T(8,128)(2,1)S(1)}, u32[]{:S(2)}, u32[]{:S(2)}) collective-permute-start(bf16[512,512]{1,0:T(8,128)(2,1)S(1)} %bitcast.81), channel_id=1, source_target_pairs={{12,0},{5,1},{14,2},{7,3},{0,4},{9,5},{2,6},{11,7},{4,8},{13,9},{6... | collective-permute-start | bytes 1572872 | tf_op jit(solution)/shard_map/ppermute | solution.py:70
  236.1 58.2 %collective-permute-start.22 = (bf16[512,512]{1,0:T(8,128)(2,1)S(1)}, bf16[512,512]{1,0:T(8,128)(2,1)S(1)}, u32[]{:S(2)}, u32[]{:S(2)}) collective-permute-start(bf16[512,512]{1,0:T(8,128)(2,1)S(1)} %bitcast.82), channel_id=1, source_target_pairs={{0,1},{1,0},{2,3},{3,2},{4,5},{5,4},{6,7},{7,6},{8,9},{9,8},{10,11... | collective-permute-start | bytes 1572872 | tf_op jit(solution)/shard_map/ppermute | solution.py:71
  275.1 20.3 %collective-permute-start.24 = (bf16[512,512]{1,0:T(8,128)(2,1)S(1)}, bf16[512,512]{1,0:T(8,128)(2,1)S(1)}, u32[]{:S(2)}, u32[]{:S(2)}) collective-permute-start(bf16[512,512]{1,0:T(8,128)(2,1)S(1)} %collective-permute-done.19), channel_id=1, source_target_pairs={{0,1},{1,0},{2,3},{3,2},{4,5},{5,4},{6,7},{7,6},{8,9},{9,8},{10,11... | collective-permute-start | bytes 1572872 | tf_op jit(solution)/shard_map/ppermute | solution.py:72
  275.7 20.2 %collective-permute-start.25 = (bf16[512,512]{1,0:T(8,128)(2,1)S(1)}, bf16[512,512]{1,0:T(8,128)(2,1)S(1)}, u32[]{:S(2)}, u32[]{:S(2)}) collective-permute-start(bf16[512,512]{1,0:T(8,128)(2,1)S(1)} %collective-permute-done.20), channel_id=1, source_target_pairs={{0,1},{1,0},{2,3},{3,2},{4,5},{5,4},{6,7},{7,6},{8,9},{9,8},{10,11... | collective-permute-start | bytes 1572872 | tf_op jit(solution)/shard_map/ppermute | solution.py:72
  284.2 12.2 %collective-permute-start.23 = (bf16[512,512]{1,0:T(8,128)(2,1)S(1)}, bf16[512,512]{1,0:T(8,128)(2,1)S(1)}, u32[]{:S(2)}, u32[]{:S(2)}) collective-permute-start(bf16[512,512]{1,0:T(8,128)(2,1)S(1)} %collective-permute-done.18), channel_id=1, source_target_pairs={{0,1},{1,0},{2,3},{3,2},{4,5},{5,4},{6,7},{7,6},{8,9},{9,8},{10,11... | collective-permute-start | bytes 1572872 | tf_op jit(solution)/shard_map/ppermute | solution.py:72
  296.4 5.9 %copy-start.5 = (s32[3]{0:T(128)S(1)}, s32[3]{0:T(128)}, u32[]{:S(2)}) copy-start(s32[3]{0:T(128)} %param.5) | copy-start | bytes 40
  297.9 122.2 %collective-permute-start.26 = (f32[512,512]{0,1:T(8,128)}, f32[512,512]{0,1:T(8,128)}, u32[]{:S(2)}, u32[]{:S(2)}) collective-permute-start(f32[512,512]{0,1:T(8,128)} %fusion.2), channel_id=1, source_target_pairs={{0,0},{1,16},{2,32},{3,48},{4,64},{5,80},{6,96},{7,112},{8,128},{9... | collective-permute-start | bytes 3145736 | tf_op jit(solution)/shard_map/ppermute | solution.py:78
  308.6 113.6 %copy-start.1 = (f32[64,8,2,256]{3,1,2,0:T(8,128)S(1)}, f32[64,8,2,256]{3,1,2,0:T(8,128)}, u32[]{:S(2)}) copy-start(f32[64,8,2,256]{3,1,2,0:T(8,128)} %copy.75) | copy-start | bytes 3145732

commit v4 on v3

--- a/solution.py
+++ b/solution.py
@@ -65,12 +65,12 @@
         own = p1_local[d]
         if d >= 1:
             own = lax.optimization_barrier((own, products[d - 1]))[0]
-        if d >= 2:
-            own = lax.optimization_barrier((own, mirrors[d - 2]))[0]
         fetched = [lax.ppermute(own, "col", fp) for fp in fetch_pairs]
         partner_own = lax.ppermute(own, "col", swap)
         partner_fetched = [lax.ppermute(fetched[j], "col", swap) for j in range(col_span - 1)]
         tiles = [own] + fetched + [partner_own] + partner_fetched
+        if d >= 1:
+            tiles, mirrors[d - 1] = lax.optimization_barrier((tiles, mirrors[d - 1]))
         summed = jnp.zeros((row_height, col_width), jnp.float32)
         for tile, factor in zip(tiles, factors):
             summed = summed + jnp.dot(tile, factor, preferred_element_type=jnp.float32)

time: 428 us -> 411 us (0.960)
  starting transfers between devices: 140 us -> 46.8 us
  waiting for transfers between devices: 217 us -> 287 us
    ppermute x12, waiting for transfers between devices: 39.8 us -> 89.3 us  [body(): fetched = [lax.ppermute(own, 'col', fp) for fp in fetch_pairs]]
    ppermute x12, starting transfers between devices: 72.6 us -> 28.7 us  [body(): fetched = [lax.ppermute(own, 'col', fp) for fp in fetch_pairs]]
    ppermute x3, starting transfers between devices: 40.2 us -> 1.72 us  [body(): partner_own = lax.ppermute(own, 'col', swap)]
    ppermute x3, waiting for transfers between devices: 177 us -> 198 us  [body(): mirrored = lax.ppermute(summed, ('row', 'col'), pairs)]
    ppermute x9, starting transfers between devices: 18.8 us -> 7.95 us  [body(): lax.ppermute(fetched[j], 'col', swap)]
  transfers between devices with their start and end apart: 27 -> 27, of which waited for: 7 -> 11; matrix products, arithmetic and copies ran while one was open for 13% -> 10% of each run, Pallas kernels for 0% -> 0%
where the time goes in v4:
time: 411 us; the launch traced here: 405 us
  waiting for transfers between devices  287 us (70%)
  starting transfers between devices  46.8 us (11%)
  local copies, waits for them, and re-layouts  26.9 us (7%)
  matrix products  23.4 us (6%)
  other arithmetic  19.5 us (5%)
    ppermute x3, waiting for transfers between devices, body(): mirrored = lax.ppermute(summed, ('row', 'col'), pairs)  198 us
    ppermute x12, waiting for transfers between devices, body(): fetched = [lax.ppermute(own, 'col', fp) for fp in fetch_pairs]  89.3 us
    ppermute x12, starting transfers between devices, body(): fetched = [lax.ppermute(own, 'col', fp) for fp in fetch_pairs]  28.7 us
    dot_general x27, matrix products, body(): summed = summed + jnp.dot(tile, factor, preferred_element_type=jnp.float32)  23.4 us
    reshape x2, local copies, waits for them, and re-layouts, mask_blocks(): shaped = values.reshape(leading + (row_blocks, BLK, col_blocks, BLK))  10.1 us
    another operation x3, other arithmetic, body(): chosen = jnp.stack(outs)  8.76 us
    ppermute x3, starting transfers between devices, body(): mirrored = lax.ppermute(summed, ('row', 'col'), pairs)  8.38 us
  transfers between devices with their start and end apart: 27, of which 11 were waited for; matrix products, arithmetic and copies ran while one was open for 10% of the time, Pallas kernels for 0%

profile of v4, /device:TPU:218, one launch (start us, length us, event | category | flops | bytes accessed | tf_op | source)
XLA Modules:
  0.0 404.9 jit_solution(15427568838388786156)
XLA Ops:
  0.0 2.4 reshape.34
  2.4 0.8 dynamic-slice_convert_fusion
  3.2 1.4 broadcast_multiply_fusion
  4.6 1.9 fusion.95
  6.9 1.7 collective-permute-start.4
  8.6 2.6 collective-permute-start.3
  11.2 1.1 collective-permute-start.2
  12.3 4.6 %collective-permute-start.1 = (bf16[512,512]{1,0:T(8,128)(2,1)S(1)}, bf16[512,512]{1,0:T(8,128)(2,1)S(1)}, u32[]{:S(2)}, u32[]{:S(2)}) collective-permute-start(bf16[512,512]{1,0:T(8,128)(2,1)S(1)} %bitcast.96), channel_id=1, source_target_pairs={{14,0},{3,1},{0,2},{5,3},{2,4},{7,5},{4,6},{9,7},{6,8},{11,9},{8,1... | collective-permute-start | bytes 1572872 | tf_op jit(solution)/shard_map/ppermute | solution.py:68
  17.1 7.7 %reshape.35 = bf16[18,256,2,256]{3,2,1,0:T(2,128)(2,1)} reshape(bf16[4608,512]{1,0:T(8,128)(2,1)} %param.8) | data formatting | bytes 9437184 | tf_op jit(solution)/shard_map/reshape | solution.py:13
  24.8 1.6 slice_multiply_fusion
  26.5 2.5 mul.97
  29.0 1.0 copy.72
  30.0 1.2 slice-done.3
  31.2 3.6 mul.100
  35.3 12.1 %collective-permute-done.2 = bf16[512,512]{1,0:T(8,128)(2,1)} collective-permute-done((bf16[512,512]{1,0:T(8,128)(2,1)S(1)}, bf16[512,512]{1,0:T(8,128)(2,1)}, u32[]{:S(2)}, u32[]{:S(2)}) %collective-permute-start.2) | collective-permute-done | bytes 524320 | tf_op jit(solution)/shard_map/ppermute | solution.py:68
  47.4 3.0 collective-permute-done.1
  50.4 0.5 collective-permute-start.5
  50.9 1.6 fusion.56
  52.6 1.6 fusion.44
  54.2 1.5 convolution_add_fusion.4
  55.7 1.5 fusion.50
  57.2 0.5 fusion.15
  58.7 0.5 fusion.12
  59.3 5.2 %collective-permute-start.10 = (bf16[512,512]{1,0:T(8,128)(2,1)S(1)}, bf16[512,512]{1,0:T(8,128)(2,1)}, u32[]{:S(2)}, u32[]{:S(2)}) collective-permute-start(bf16[512,512]{1,0:T(8,128)(2,1)S(1)} %bitcast.79), channel_id=1, source_target_pairs={{14,0},{3,1},{0,2},{5,3},{2,4},{7,5},{4,6},{9,7},{6,8},{11,9},{8,1... | collective-permute-start | bytes 1572872 | tf_op jit(solution)/shard_map/ppermute | solution.py:68
  64.5 1.3 copy.31
  65.9 3.1 collective-permute-start.8
  68.9 3.9 collective-permute-start.12
  72.8 5.3 %collective-permute-done.9 = bf16[512,512]{1,0:T(8,128)(2,1)} collective-permute-done((bf16[512,512]{1,0:T(8,128)(2,1)S(1)}, bf16[512,512]{1,0:T(8,128)(2,1)}, u32[]{:S(2)}, u32[]{:S(2)}) %collective-permute-start.9) | collective-permute-done | bytes 524320 | tf_op jit(solution)/shard_map/ppermute | solution.py:68
  78.1 10.3 %collective-permute-done.10 = bf16[512,512]{1,0:T(8,128)(2,1)} collective-permute-done((bf16[512,512]{1,0:T(8,128)(2,1)S(1)}, bf16[512,512]{1,0:T(8,128)(2,1)}, u32[]{:S(2)}, u32[]{:S(2)}) %collective-permute-start.10) | collective-permute-done | bytes 524320 | tf_op jit(solution)/shard_map/ppermute | solution.py:68
  88.4 11.3 %collective-permute-done.11 = bf16[512,512]{1,0:T(8,128)(2,1)S(1)} collective-permute-done((bf16[512,512]{1,0:T(8,128)(2,1)S(1)}, bf16[512,512]{1,0:T(8,128)(2,1)S(1)}, u32[]{:S(2)}, u32[]{:S(2)}) %collective-permute-start.11) | collective-permute-done | bytes 524320 | tf_op jit(solution)/shard_map/ppermute | solution.py:68
  99.7 1.7 collective-permute-done.12
  101.4 1.3 copy.74
  102.7 75.8 %collective-permute-done.8 = f32[512,512]{0,1:T(8,128)S(1)} collective-permute-done((f32[512,512]{0,1:T(8,128)}, f32[512,512]{0,1:T(8,128)S(1)}, u32[]{:S(2)}, u32[]{:S(2)}) %collective-permute-start.8) | collective-permute-done | bytes 1048608 | tf_op jit(solution)/shard_map/ppermute | solution.py:78
  178.5 1.0 copy-done.5
  179.5 1.7 fusion.65
  181.2 1.7 fusion.60
  182.9 1.5 fusion.54
  184.4 1.5 fusion.48
  186.0 0.5 fusion.42
  186.5 0.5 fusion.37
  187.0 0.5 fusion.31
  187.5 0.5 fusion.25
  188.0 0.8 fusion.17
  188.9 2.9 collective-permute-start.17
  191.9 10.7 %collective-permute-start.21 = (bf16[512,512]{1,0:T(8,128)(2,1)S(1)}, bf16[512,512]{1,0:T(8,128)(2,1)S(1)}, u32[]{:S(2)}, u32[]{:S(2)}) collective-permute-start(bf16[512,512]{1,0:T(8,128)(2,1)S(1)} %bitcast.88), channel_id=1, source_target_pairs={{12,0},{5,1},{14,2},{7,3},{0,4},{9,5},{2,6},{11,7},{4,8},{13,9},{6... | collective-permute-start | bytes 1572872 | tf_op jit(solution)/shard_map/ppermute | solution.py:68
  202.6 21.5 %collective-permute-done.18 = bf16[512,512]{1,0:T(8,128)(2,1)S(1)} collective-permute-done((bf16[512,512]{1,0:T(8,128)(2,1)S(1)}, bf16[512,512]{1,0:T(8,128)(2,1)S(1)}, u32[]{:S(2)}, u32[]{:S(2)}) %collective-permute-start.18) | collective-permute-done | bytes 524320 | tf_op jit(solution)/shard_map/ppermute | solution.py:68
  224.1 5.3 %collective-permute-start.23 = (bf16[512,512]{1,0:T(8,128)(2,1)S(1)}, bf16[512,512]{1,0:T(8,128)(2,1)S(1)}, u32[]{:S(2)}, u32[]{:S(2)}) collective-permute-start(bf16[512,512]{1,0:T(8,128)(2,1)S(1)} %collective-permute-done.18), channel_id=1, source_target_pairs={{0,1},{1,0},{2,3},{3,2},{4,5},{5,4},{6,7},{7,6},{8,9},{9,8},{10,11... | collective-permute-start | bytes 1572872 | tf_op jit(solution)/shard_map/ppermute | solution.py:70
  229.3 24.1 %collective-permute-done.20 = bf16[512,512]{1,0:T(8,128)(2,1)S(1)} collective-permute-done((bf16[512,512]{1,0:T(8,128)(2,1)S(1)}, bf16[512,512]{1,0:T(8,128)(2,1)S(1)}, u32[]{:S(2)}, u32[]{:S(2)}) %collective-permute-start.20) | collective-permute-done | bytes 524320 | tf_op jit(solution)/shard_map/ppermute | solution.py:68
  253.5 2.1 collective-permute-start.25
  255.6 86.9 %collective-permute-done.17 = f32[512,512]{0,1:T(8,128)S(1)} collective-permute-done((f32[512,512]{0,1:T(8,128)S(1)}, f32[512,512]{0,1:T(8,128)S(1)}, u32[]{:S(2)}, u32[]{:S(2)}) %collective-permute-start.17) | collective-permute-done | bytes 1048608 | tf_op jit(solution)/shard_map/ppermute | solution.py:78
  342.5 0.5 fusion.63
  343.0 0.5 fusion.58
  345.0 0.5 fusion.35
  346.5 1.7 fusion.19
  348.2 2.5 collective-permute-start.26
  351.1 1.1 copy.75
  352.1 0.7 fusion.96
  352.8 2.6 copy.41
  355.4 3.1 fusion.20
  358.5 3.5 fusion.21
  362.0 1.6 copy.51
  363.6 35.5 %collective-permute-done.26 = f32[512,512]{0,1:T(8,128)} collective-permute-done((f32[512,512]{0,1:T(8,128)}, f32[512,512]{0,1:T(8,128)}, u32[]{:S(2)}, u32[]{:S(2)}) %collective-permute-start.26) | collective-permute-done | bytes 1048608 | tf_op jit(solution)/shard_map/ppermute | solution.py:78
  399.1 2.1 fusion.22
  401.2 3.3 fusion
  (73 shorter events, 5.4 us)
Async XLA Ops:
  0.0 16.8 %copy-start.7 = (s32[32,32]{1,0:T(8,128)S(1)}, s32[32,32]{1,0:T(8,128)}, u32[]{:S(2)}) copy-start(s32[32,32]{1,0:T(8,128)} %param.6) | copy-start | bytes 12292
  6.6 28.3 %copy-start.1 = (bf16[64,8,2,256]{3,1,2,0:T(8,128)(2,1)}, bf16[64,8,2,256]{3,1,2,0:T(8,128)(2,1)S(1)}, u32[]{:S(2)}) copy-start(bf16[64,8,2,256]{3,1,2,0:T(8,128)(2,1)S(1)} %copy.70) | copy-start | bytes 1572868
  6.6 43.8 %collective-permute-start = (bf16[512,512]{1,0:T(8,128)(2,1)S(1)}, bf16[512,512]{1,0:T(8,128)(2,1)}, u32[]{:S(2)}, u32[]{:S(2)}) collective-permute-start(bf16[512,512]{1,0:T(8,128)(2,1)S(1)} %bitcast.92), channel_id=1, source_target_pairs={{15,0},{2,1},{1,2},{4,3},{3,4},{6,5},{5,6},{8,7},{7,8},{10,9},{9,1... | collective-permute-start | bytes 1572872 | tf_op jit(solution)/shard_map/ppermute | solution.py:68
  6.9 45.7 %collective-permute-start.4 = (bf16[512,512]{1,0:T(8,128)(2,1)S(1)}, bf16[512,512]{1,0:T(8,128)(2,1)}, u32[]{:S(2)}, u32[]{:S(2)}) collective-permute-start(bf16[512,512]{1,0:T(8,128)(2,1)S(1)} %bitcast.93), channel_id=1, source_target_pairs={{0,1},{1,0},{2,3},{3,2},{4,5},{5,4},{6,7},{7,6},{8,9},{9,8},{10,11... | collective-permute-start | bytes 1572872 | tf_op jit(solution)/shard_map/ppermute | solution.py:69
  8.6 47.2 %collective-permute-start.3 = (bf16[512,512]{1,0:T(8,128)(2,1)S(1)}, bf16[512,512]{1,0:T(8,128)(2,1)}, u32[]{:S(2)}, u32[]{:S(2)}) collective-permute-start(bf16[512,512]{1,0:T(8,128)(2,1)S(1)} %bitcast.94), channel_id=1, source_target_pairs={{12,0},{5,1},{14,2},{7,3},{0,4},{9,5},{2,6},{11,7},{4,8},{13,9},{6... | collective-permute-start | bytes 1572872 | tf_op jit(solution)/shard_map/ppermute | solution.py:68
  11.2 36.2 %collective-permute-start.2 = (bf16[512,512]{1,0:T(8,128)(2,1)S(1)}, bf16[512,512]{1,0:T(8,128)(2,1)}, u32[]{:S(2)}, u32[]{:S(2)}) collective-permute-start(bf16[512,512]{1,0:T(8,128)(2,1)S(1)} %bitcast.95), channel_id=1, source_target_pairs={{13,0},{4,1},{15,2},{6,3},{1,4},{8,5},{3,6},{10,7},{5,8},{12,9},{7... | collective-permute-start | bytes 1572872 | tf_op jit(solution)/shard_map/ppermute | solution.py:68
  12.3 38.2 %collective-permute-start.1 = (bf16[512,512]{1,0:T(8,128)(2,1)S(1)}, bf16[512,512]{1,0:T(8,128)(2,1)S(1)}, u32[]{:S(2)}, u32[]{:S(2)}) collective-permute-start(bf16[512,512]{1,0:T(8,128)(2,1)S(1)} %bitcast.96), channel_id=1, source_target_pairs={{14,0},{3,1},{0,2},{5,3},{2,4},{7,5},{4,6},{9,7},{6,8},{11,9},{8,1... | collective-permute-start | bytes 1572872 | tf_op jit(solution)/shard_map/ppermute | solution.py:68
  26.5 3.5 slice-start.2
  29.0 2.2 slice-start.3
  34.8 19.4 %copy-start = (bf16[4608,512]{1,0:T(8,128)(2,1)S(1)}, bf16[4608,512]{1,0:T(8,128)(2,1)}, u32[]{:S(2)}) copy-start(bf16[4608,512]{1,0:T(8,128)(2,1)} %mul.100) | copy-start | bytes 14155780
  47.4 10.4 %collective-permute-start.7 = (bf16[512,512]{1,0:T(8,128)(2,1)}, bf16[512,512]{1,0:T(8,128)(2,1)S(1)}, u32[]{:S(2)}, u32[]{:S(2)}) collective-permute-start(bf16[512,512]{1,0:T(8,128)(2,1)} %collective-permute-done.2), channel_id=1, source_target_pairs={{0,1},{1,0},{2,3},{3,2},{4,5},{5,4},{6,7},{7,6},{8,9},{9,8},{10,11... | collective-permute-start | bytes 1572872 | tf_op jit(solution)/shard_map/ppermute | solution.py:70
  50.4 7.8 %collective-permute-start.6 = (bf16[512,512]{1,0:T(8,128)(2,1)S(1)}, bf16[512,512]{1,0:T(8,128)(2,1)S(1)}, u32[]{:S(2)}, u32[]{:S(2)}) collective-permute-start(bf16[512,512]{1,0:T(8,128)(2,1)S(1)} %collective-permute-done.1), channel_id=1, source_target_pairs={{0,1},{1,0},{2,3},{3,2},{4,5},{5,4},{6,7},{7,6},{8,9},{9,8},{10,11... | collective-permute-start | bytes 1572872 | tf_op jit(solution)/shard_map/ppermute | solution.py:70
  50.4 8.2 %collective-permute-start.5 = (bf16[512,512]{1,0:T(8,128)(2,1)}, bf16[512,512]{1,0:T(8,128)(2,1)S(1)}, u32[]{:S(2)}, u32[]{:S(2)}) collective-permute-start(bf16[512,512]{1,0:T(8,128)(2,1)} %collective-permute-done), channel_id=1, source_target_pairs={{0,1},{1,0},{2,3},{3,2},{4,5},{5,4},{6,7},{7,6},{8,9},{9,8},{10,11... | collective-permute-start | bytes 1572872 | tf_op jit(solution)/shard_map/ppermute | solution.py:70
  58.7 127.3 %slice-start = ((s8[4718592]{0:T(1024)(128)(4,1)}), s8[524288]{0:T(1024)(128)(4,1)S(1)}, s32[]{:S(2)}) async-start(s8[4718592]{0:T(1024)(128)(4,1)} %bitcast.69), calls=%async_computation | async-start | bytes 1048576
  59.2 18.9 %collective-permute-start.9 = (bf16[512,512]{1,0:T(8,128)(2,1)S(1)}, bf16[512,512]{1,0:T(8,128)(2,1)}, u32[]{:S(2)}, u32[]{:S(2)}) collective-permute-start(bf16[512,512]{1,0:T(8,128)(2,1)S(1)} %bitcast.78), channel_id=1, source_target_pairs={{15,0},{2,1},{1,2},{4,3},{3,4},{6,5},{5,6},{8,7},{7,8},{10,9},{9,1... | collective-permute-start | bytes 1572872 | tf_op jit(solution)/shard_map/ppermute | solution.py:68
  59.3 29.1 %collective-permute-start.10 = (bf16[512,512]{1,0:T(8,128)(2,1)S(1)}, bf16[512,512]{1,0:T(8,128)(2,1)}, u32[]{:S(2)}, u32[]{:S(2)}) collective-permute-start(bf16[512,512]{1,0:T(8,128)(2,1)S(1)} %bitcast.79), channel_id=1, source_target_pairs={{14,0},{3,1},{0,2},{5,3},{2,4},{7,5},{4,6},{9,7},{6,8},{11,9},{8,1... | collective-permute-start | bytes 1572872 | tf_op jit(solution)/shard_map/ppermute | solution.py:68
  65.8 33.9 %collective-permute-start.11 = (bf16[512,512]{1,0:T(8,128)(2,1)S(1)}, bf16[512,512]{1,0:T(8,128)(2,1)S(1)}, u32[]{:S(2)}, u32[]{:S(2)}) collective-permute-start(bf16[512,512]{1,0:T(8,128)(2,1)S(1)} %bitcast.80), channel_id=1, source_target_pairs={{13,0},{4,1},{15,2},{6,3},{1,4},{8,5},{3,6},{10,7},{5,8},{12,9},{7... | collective-permute-start | bytes 1572872 | tf_op jit(solution)/shard_map/ppermute | solution.py:68
  65.9 112.6 %collective-permute-start.8 = (f32[512,512]{0,1:T(8,128)}, f32[512,512]{0,1:T(8,128)S(1)}, u32[]{:S(2)}, u32[]{:S(2)}) collective-permute-start(f32[512,512]{0,1:T(8,128)} %copy.31), channel_id=1, source_target_pairs={{0,0},{1,16},{2,32},{3,48},{4,64},{5,80},{6,96},{7,112},{8,128},{9... | collective-permute-start | bytes 3145736 | tf_op jit(solution)/shard_map/ppermute | solution.py:78
  68.9 32.5 %collective-permute-start.12 = (bf16[512,512]{1,0:T(8,128)(2,1)S(1)}, bf16[512,512]{1,0:T(8,128)(2,1)S(1)}, u32[]{:S(2)}, u32[]{:S(2)}) collective-permute-start(bf16[512,512]{1,0:T(8,128)(2,1)S(1)} %bitcast.81), channel_id=1, source_target_pairs={{12,0},{5,1},{14,2},{7,3},{0,4},{9,5},{2,6},{11,7},{4,8},{13,9},{6... | collective-permute-start | bytes 1572872 | tf_op jit(solution)/shard_map/ppermute | solution.py:68
  78.1 24.6 %collective-permute-start.13 = (bf16[512,512]{1,0:T(8,128)(2,1)S(1)}, bf16[512,512]{1,0:T(8,128)(2,1)S(1)}, u32[]{:S(2)}, u32[]{:S(2)}) collective-permute-start(bf16[512,512]{1,0:T(8,128)(2,1)S(1)} %bitcast.82), channel_id=1, source_target_pairs={{0,1},{1,0},{2,3},{3,2},{4,5},{5,4},{6,7},{7,6},{8,9},{9,8},{10,11... | collective-permute-start | bytes 1572872 | tf_op jit(solution)/shard_map/ppermute | solution.py:69
  88.4 90.1 %collective-permute-start.14 = (bf16[512,512]{1,0:T(8,128)(2,1)}, bf16[512,512]{1,0:T(8,128)(2,1)S(1)}, u32[]{:S(2)}, u32[]{:S(2)}) collective-permute-start(bf16[512,512]{1,0:T(8,128)(2,1)} %collective-permute-done.9), channel_id=1, source_target_pairs={{0,1},{1,0},{2,3},{3,2},{4,5},{5,4},{6,7},{7,6},{8,9},{9,8},{10,11... | collective-permute-start | bytes 1572872 | tf_op jit(solution)/shard_map/ppermute | solution.py:70
  99.7 78.8 %collective-permute-start.15 = (bf16[512,512]{1,0:T(8,128)(2,1)}, bf16[512,512]{1,0:T(8,128)(2,1)S(1)}, u32[]{:S(2)}, u32[]{:S(2)}) collective-permute-start(bf16[512,512]{1,0:T(8,128)(2,1)} %collective-permute-done.10), channel_id=1, source_target_pairs={{0,1},{1,0},{2,3},{3,2},{4,5},{5,4},{6,7},{7,6},{8,9},{9,8},{10,11... | collective-permute-start | bytes 1572872 | tf_op jit(solution)/shard_map/ppermute | solution.py:70
  101.4 78.1 %collective-permute-start.16 = (bf16[512,512]{1,0:T(8,128)(2,1)S(1)}, bf16[512,512]{1,0:T(8,128)(2,1)S(1)}, u32[]{:S(2)}, u32[]{:S(2)}) collective-permute-start(bf16[512,512]{1,0:T(8,128)(2,1)S(1)} %collective-permute-done.11), channel_id=1, source_target_pairs={{0,1},{1,0},{2,3},{3,2},{4,5},{5,4},{6,7},{7,6},{8,9},{9,8},{10,11... | collective-permute-start | bytes 1572872 | tf_op jit(solution)/shard_map/ppermute | solution.py:70
  101.4 84.6 %slice-start.1 = ((s8[4718592]{0:T(1024)(128)(4,1)}), s8[4194304]{0:T(1024)(128)(4,1)S(1)}, s32[]{:S(2)}) async-start(s8[4718592]{0:T(1024)(128)(4,1)} %bitcast.69), calls=%async_computation.1 | async-start | bytes 8388608
  178.5 1.0 copy-start.5
  188.7 162.3 %copy-start.3 = (f32[512,512]{0,1:T(8,128)}, f32[512,512]{0,1:T(8,128)S(1)}, u32[]{:S(2)}) copy-start(f32[512,512]{0,1:T(8,128)S(1)} %fusion.17) | copy-start | bytes 3145732
  188.7 35.3 %collective-permute-start.18 = (bf16[512,512]{1,0:T(8,128)(2,1)S(1)}, bf16[512,512]{1,0:T(8,128)(2,1)S(1)}, u32[]{:S(2)}, u32[]{:S(2)}) collective-permute-start(bf16[512,512]{1,0:T(8,128)(2,1)S(1)} %bitcast.85), channel_id=1, source_target_pairs={{15,0},{2,1},{1,2},{4,3},{3,4},{6,5},{5,6},{8,7},{7,8},{10,9},{9,1... | collective-permute-start | bytes 1572872 | tf_op jit(solution)/shard_map/ppermute | solution.py:68
  188.8 35.2 %collective-permute-start.19 = (bf16[512,512]{1,0:T(8,128)(2,1)S(1)}, bf16[512,512]{1,0:T(8,128)(2,1)S(1)}, u32[]{:S(2)}, u32[]{:S(2)}) collective-permute-start(bf16[512,512]{1,0:T(8,128)(2,1)S(1)} %bitcast.86), channel_id=1, source_target_pairs={{14,0},{3,1},{0,2},{5,3},{2,4},{7,5},{4,6},{9,7},{6,8},{11,9},{8,1... | collective-permute-start | bytes 1572872 | tf_op jit(solution)/shard_map/ppermute | solution.py:68
  188.9 153.6 %collective-permute-start.17 = (f32[512,512]{0,1:T(8,128)S(1)}, f32[512,512]{0,1:T(8,128)S(1)}, u32[]{:S(2)}, u32[]{:S(2)}) collective-permute-start(f32[512,512]{0,1:T(8,128)S(1)} %fusion.17), channel_id=1, source_target_pairs={{0,0},{1,16},{2,32},{3,48},{4,64},{5,80},{6,96},{7,112},{8,128},{9... | collective-permute-start | bytes 3145736 | tf_op jit(solution)/shard_map/ppermute | solution.py:78
  191.8 61.7 %collective-permute-start.20 = (bf16[512,512]{1,0:T(8,128)(2,1)S(1)}, bf16[512,512]{1,0:T(8,128)(2,1)S(1)}, u32[]{:S(2)}, u32[]{:S(2)}) collective-permute-start(bf16[512,512]{1,0:T(8,128)(2,1)S(1)} %bitcast.87), channel_id=1, source_target_pairs={{13,0},{4,1},{15,2},{6,3},{1,4},{8,5},{3,6},{10,7},{5,8},{12,9},{7... | collective-permute-start | bytes 1572872 | tf_op jit(solution)/shard_map/ppermute | solution.py:68
  191.9 61.6 %collective-permute-start.21 = (bf16[512,512]{1,0:T(8,128)(2,1)S(1)}, bf16[512,512]{1,0:T(8,128)(2,1)S(1)}, u32[]{:S(2)}, u32[]{:S(2)}) collective-permute-start(bf16[512,512]{1,0:T(8,128)(2,1)S(1)} %bitcast.88), channel_id=1, source_target_pairs={{12,0},{5,1},{14,2},{7,3},{0,4},{9,5},{2,6},{11,7},{4,8},{13,9},{6... | collective-permute-start | bytes 1572872 | tf_op jit(solution)/shard_map/ppermute | solution.py:68
  224.1 31.5 %collective-permute-start.22 = (bf16[512,512]{1,0:T(8,128)(2,1)S(1)}, bf16[512,512]{1,0:T(8,128)(2,1)S(1)}, u32[]{:S(2)}, u32[]{:S(2)}) collective-permute-start(bf16[512,512]{1,0:T(8,128)(2,1)S(1)} %bitcast.89), channel_id=1, source_target_pairs={{0,1},{1,0},{2,3},{3,2},{4,5},{5,4},{6,7},{7,6},{8,9},{9,8},{10,11... | collective-permute-start | bytes 1572872 | tf_op jit(solution)/shard_map/ppermute | solution.py:69
  224.1 118.4 %collective-permute-start.23 = (bf16[512,512]{1,0:T(8,128)(2,1)S(1)}, bf16[512,512]{1,0:T(8,128)(2,1)S(1)}, u32[]{:S(2)}, u32[]{:S(2)}) collective-permute-start(bf16[512,512]{1,0:T(8,128)(2,1)S(1)} %collective-permute-done.18), channel_id=1, source_target_pairs={{0,1},{1,0},{2,3},{3,2},{4,5},{5,4},{6,7},{7,6},{8,9},{9,8},{10,11... | collective-permute-start | bytes 1572872 | tf_op jit(solution)/shard_map/ppermute | solution.py:70
  253.4 89.0 %collective-permute-start.24 = (bf16[512,512]{1,0:T(8,128)(2,1)S(1)}, bf16[512,512]{1,0:T(8,128)(2,1)S(1)}, u32[]{:S(2)}, u32[]{:S(2)}) collective-permute-start(bf16[512,512]{1,0:T(8,128)(2,1)S(1)} %collective-permute-done.19), channel_id=1, source_target_pairs={{0,1},{1,0},{2,3},{3,2},{4,5},{5,4},{6,7},{7,6},{8,9},{9,8},{10,11... | collective-permute-start | bytes 1572872 | tf_op jit(solution)/shard_map/ppermute | solution.py:70
  253.5 89.0 %collective-permute-start.25 = (bf16[512,512]{1,0:T(8,128)(2,1)S(1)}, bf16[512,512]{1,0:T(8,128)(2,1)S(1)}, u32[]{:S(2)}, u32[]{:S(2)}) collective-permute-start(bf16[512,512]{1,0:T(8,128)(2,1)S(1)} %collective-permute-done.20), channel_id=1, source_target_pairs={{0,1},{1,0},{2,3},{3,2},{4,5},{5,4},{6,7},{7,6},{8,9},{9,8},{10,11... | collective-permute-start | bytes 1572872 | tf_op jit(solution)/shard_map/ppermute | solution.py:70
  342.5 2.5 copy-start.6
  346.5 5.7 %copy-start.8 = (s32[3]{0:T(128)S(1)}, s32[3]{0:T(128)}, u32[]{:S(2)}) copy-start(s32[3]{0:T(128)} %param.5) | copy-start | bytes 40
  348.2 7.2 %copy-start.2 = (bf16[64,8,2,256]{3,1,2,0:T(8,128)(2,1)S(1)}, bf16[64,8,2,256]{3,1,2,0:T(8,128)(2,1)}, u32[]{:S(2)}) copy-start(bf16[64,8,2,256]{3,1,2,0:T(8,128)(2,1)} %copy-done.1) | copy-start | bytes 1572868
  348.2 50.8 %collective-permute-start.26 = (f32[512,512]{0,1:T(8,128)}, f32[512,512]{0,1:T(8,128)}, u32[]{:S(2)}, u32[]{:S(2)}) collective-permute-start(f32[512,512]{0,1:T(8,128)} %fusion.19), channel_id=1, source_target_pairs={{0,0},{1,16},{2,32},{3,48},{4,64},{5,80},{6,96},{7,112},{8,128},{9... | collective-permute-start | bytes 3145736 | tf_op jit(solution)/shard_map/ppermute | solution.py:78
  358.5 42.7 %copy-start.4 = (f32[64,8,2,256]{3,1,2,0:T(8,128)S(1)}, f32[64,8,2,256]{3,1,2,0:T(8,128)}, u32[]{:S(2)}) copy-start(f32[64,8,2,256]{3,1,2,0:T(8,128)} %copy.75) | copy-start | bytes 3145732

commit v5 on v2

--- a/solution.py
+++ b/solution.py
@@ -61,18 +61,31 @@
         start = (offset + col_span) * col_width
         factors.append(lax.dynamic_slice_in_dim(strip_local, start, col_width, 0))
 
-    pairs = [(i * col_count + j, j * col_count + i) for i in range(row_count) for j in range(col_count)]
-    squared = sp2_branch == 1
-    outs = []
-    for d in range(p1_tiles.shape[0]):
-        summed = jnp.zeros((row_height, col_width), jnp.float32)
-        for (tile, _), factor in zip(tiles, factors):
-            summed = summed + jnp.dot(tile[d], factor, preferred_element_type=jnp.float32)
-        mirrored = lax.ppermute(summed, ("row", "col"), pairs).T
-        bracket = summed + mirrored
-        chosen = jnp.where(squared[d], bracket, 2.0 * p1_local[d].astype(jnp.float32) - bracket)
-        outs.append(chosen)
-    chosen = jnp.stack(outs)
+    summed_col = jnp.zeros(p1_local.shape, jnp.float32)
+    for (tile, _), factor in zip(tiles, factors):
+        summed_col = summed_col + jnp.einsum(
+            "drc,ck->drk", tile, factor, preferred_element_type=jnp.float32
+        )
+
+    row_span = band_half // row_blocks
+    owner_col = row_at * row_blocks // col_blocks
+    mine = col_at == owner_col
+    shared = lax.psum(jnp.where(mine, strip_local, jnp.zeros_like(strip_local)), "col")
+    summed_row = jnp.zeros(p1_local.shape, jnp.float32)
+    for e in range(-row_span, row_span + 1):
+        if e == 0:
+            incoming = p1_local
+        else:
+            incoming = lax.ppermute(
+                p1_local, "row", [(r, (r - e) % row_count) for r in range(row_count)]
+            )
+        factor = shared[(e + row_span) * row_height : (e + row_span + 1) * row_height, :]
+        summed_row = summed_row + jnp.einsum(
+            "kr,dkc->drc", factor, incoming, preferred_element_type=jnp.float32
+        )
+    bracket = summed_col + summed_row
+    squared = (sp2_branch == 1)[:, None, None]
+    chosen = jnp.where(squared, bracket, 2.0 * p1_local.astype(jnp.float32) - bracket)
     return mask_blocks(chosen, own_occ).astype(jnp.bfloat16)
 
 

time: 442 us -> 569 us (1.29)
  the two profiles are of different devices: /device:TPU:218 before, /device:TPU:67 now
where the time goes in v5:
time: 569 us; the launch traced here: 568 us
  waiting for transfers between devices  376 us (66%)
  matrix products  83.4 us (15%)
  starting transfers between devices  68.4 us (12%)
  local copies, waits for them, and re-layouts  16.2 us (3%)
  between operations  13.5 us (2%)
  other arithmetic  10.8 us (2%)
    ppermute x8, waiting for transfers between devices, body(): lax.ppermute(p1_local, 'row', [(r, (r - e) % row_count) for r in range(ro...  225 us
    ppermute x4, waiting for transfers between devices, body(): fetched.append(lax.ppermute(p1_local, 'col', pairs))  91.2 us
    psum x1, waiting for transfers between devices, body(): lax.psum(jnp.where(mine, strip_local, jnp.zeros_like(strip_local)), 'col')  59.6 us
    ppermute x8, starting transfers between devices, body(): lax.ppermute(p1_local, 'row', [(r, (r - e) % row_count) for r in range(ro...  55.8 us
    dot_general x9, matrix products, body(): jnp.einsum('drc,ck->drk', tile, factor, preferred_element_type=jnp.float32)  50.8 us
    dot_general x9, matrix products, body(): jnp.einsum('kr,dkc->drc', factor, incoming, preferred_element_type=jnp.fl...  32.6 us
  transfers between devices with their start and end apart: 17, of which 9 were waited for; matrix products, arithmetic and copies ran while one was open for 13% of the time, Pallas kernels for 0%

profile of v5, /device:TPU:67, one launch (start us, length us, event | category | flops | bytes accessed | tf_op | source)
XLA Modules:
  0.0 568.5 jit_solution(9399080054949832968)
XLA Ops:
  6.5 0.8 copy.24
  7.3 0.1 fusion.47
  7.4 0.1 copy.27
  7.5 2.5 mul.102
  10.0 3.1 copy.65
  13.1 8.1 %broadcast_select_fusion = (bf16[4608,512]{1,0:T(8,128)(2,1)}, bf16[4608,512]{1,0:T(8,128)(2,1)}) fusion(pred[]{:T(512)S(6)} %eq.13, bf16[4608,512]{1,0:T(8,128)(2,1)} %param.8, bf16[4608,512]{1,0:T(8,128)(2,1)} %bitcast.86), kind=kLoop, calls=%fused_computation.1 | loop fusion | flops 4718592 | bytes 18874368 | tf_op jit(solution)/shard_map/jit(_where)/select_n | solution.py:73
  21.1 0.0 all-reduce.2.cloned.1.call-update
  21.2 0.9 dynamic-slice_convert_fusion
  22.1 0.3 mul.98
  22.4 0.1 copy.64
  22.5 0.1 copy-done.1
  22.6 0.2 broadcast_multiply_fusion
  22.8 4.4 collective-permute-start.1
  27.1 0.0 collective-permute-start
  27.1 0.9 collective-permute-start.4
  28.0 2.0 collective-permute-start.3
  30.0 2.0 collective-permute-start.2
  32.0 7.7 %reshape.16 = bf16[18,256,2,256]{3,2,1,0:T(2,128)(2,1)} reshape(bf16[4608,512]{1,0:T(8,128)(2,1)} %param.8) | data formatting | bytes 9437184 | tf_op jit(solution)/shard_map/reshape | solution.py:13
  39.7 1.6 slice_multiply_fusion
  41.3 1.1 reshape.17
  42.4 0.3 mul.122
  42.7 0.0 slice-start
  42.7 0.1 copy.66
  42.8 0.0 copy-start.3
  42.8 3.8 fusion.48
  46.6 59.6 %collective-permute-done.1 = bf16[3,512,512]{2,1,0:T(8,128)(2,1)} collective-permute-done((bf16[3,512,512]{2,1,0:T(8,128)(2,1)S(1)}, bf16[3,512,512]{2,1,0:T(8,128)(2,1)}, u32[]{:S(2)}, u32[]{:S(2)}) %collective-permute-start.1) | collective-permute-done | bytes 1572896 | tf_op jit(solution)/shard_map/ppermute | solution.py:50
  106.3 1.7 collective-permute-start.6
  108.0 4.6 collective-permute-done
  112.6 0.0 collective-permute-start.5
  112.6 4.1 fusion.25
  116.7 4.1 fusion.27
  120.8 0.0 collective-permute-done.4
  120.8 5.2 collective-permute-start.8
  126.0 4.1 fusion.19
  130.1 27.0 %collective-permute-done.3 = bf16[3,512,512]{2,1,0:T(8,128)(2,1)} collective-permute-done((bf16[3,512,512]{2,1,0:T(8,128)(2,1)S(1)}, bf16[3,512,512]{2,1,0:T(8,128)(2,1)}, u32[]{:S(2)}, u32[]{:S(2)}) %collective-permute-start.3) | collective-permute-done | bytes 1572896 | tf_op jit(solution)/shard_map/ppermute | solution.py:50
  157.1 3.8 collective-permute-start.14
  160.9 4.1 fusion.21
  165.0 24.9 %collective-permute-start.13 = (bf16[3,512,512]{2,1,0:T(8,128)(2,1)S(1)}, bf16[3,512,512]{2,1,0:T(8,128)(2,1)}, u32[]{:S(2)}, u32[]{:S(2)}) collective-permute-start(bf16[3,512,512]{2,1,0:T(8,128)(2,1)S(1)} %broadcast_multiply_fusion), channel_id=1, source_target_pairs={{0,224},{16,240},{32,0},{48,16},{64,32},{80,48},{96,64},{112,80},{... | collective-permute-start | bytes 4718600 | tf_op jit(solution)/shard_map/ppermute | solution.py:79
  189.9 4.0 fusion.23
  193.9 0.0 collective-permute-done.6
  193.9 0.0 collective-permute-start.12
  194.0 2.6 fusion.15
  196.6 1.5 collective-permute-start.11
  198.0 2.6 fusion.17
  200.7 59.6 %all-reduce.2.cloned.1.call-done = bf16[4608,512]{1,0:T(8,128)(2,1)} async-done(((bf16[4608,512]{1,0:T(8,128)(2,1)}), bf16[4608,512]{1,0:T(8,128)(2,1)}) %all-reduce.2.cloned.1.call-update) | async-done | bytes 4718608 | tf_op jit(solution)/shard_map/psum | solution.py:73
  260.2 3.9 fusion.6
  264.1 3.5 collective-permute-start.10
  267.6 4.2 fusion.10
  271.8 21.1 %collective-permute-done.14 = bf16[3,512,512]{2,1,0:T(8,128)(2,1)} collective-permute-done((bf16[3,512,512]{2,1,0:T(8,128)(2,1)S(1)}, bf16[3,512,512]{2,1,0:T(8,128)(2,1)}, u32[]{:S(2)}, u32[]{:S(2)}) %collective-permute-start.14) | collective-permute-done | bytes 1572896 | tf_op jit(solution)/shard_map/ppermute | solution.py:79
  292.9 15.0 %collective-permute-start.9 = (bf16[3,512,512]{2,1,0:T(8,128)(2,1)S(1)}, bf16[3,512,512]{2,1,0:T(8,128)(2,1)S(1)}, u32[]{:S(2)}, u32[]{:S(2)}) collective-permute-start(bf16[3,512,512]{2,1,0:T(8,128)(2,1)S(1)} %broadcast_multiply_fusion), channel_id=1, source_target_pairs={{0,48},{16,64},{32,80},{48,96},{64,112},{80,128},{96,144},{112,160... | collective-permute-start | bytes 4718600 | tf_op jit(solution)/shard_map/ppermute | solution.py:79
  307.9 4.2 fusion.3
  312.1 56.1 %collective-permute-done.13 = bf16[3,512,512]{2,1,0:T(8,128)(2,1)} collective-permute-done((bf16[3,512,512]{2,1,0:T(8,128)(2,1)S(1)}, bf16[3,512,512]{2,1,0:T(8,128)(2,1)}, u32[]{:S(2)}, u32[]{:S(2)}) %collective-permute-start.13) | collective-permute-done | bytes 1572896 | tf_op jit(solution)/shard_map/ppermute | solution.py:79
  368.2 1.9 collective-permute-start.15
  370.1 4.1 fusion.4
  374.2 24.0 %collective-permute-done.12 = bf16[3,512,512]{2,1,0:T(8,128)(2,1)} collective-permute-done((bf16[3,512,512]{2,1,0:T(8,128)(2,1)S(1)}, bf16[3,512,512]{2,1,0:T(8,128)(2,1)}, u32[]{:S(2)}, u32[]{:S(2)}) %collective-permute-start.12) | collective-permute-done | bytes 1572896 | tf_op jit(solution)/shard_map/ppermute | solution.py:79
  398.2 1.6 collective-permute-start.7
  399.9 4.0 fusion.5
  403.9 4.1 fusion.7
  408.0 2.7 fusion.8
  410.8 26.2 %collective-permute-done.9 = bf16[3,512,512]{2,1,0:T(8,128)(2,1)S(1)} collective-permute-done((bf16[3,512,512]{2,1,0:T(8,128)(2,1)S(1)}, bf16[3,512,512]{2,1,0:T(8,128)(2,1)S(1)}, u32[]{:S(2)}, u32[]{:S(2)}) %collective-permute-start.9) | collective-permute-done | bytes 1572896 | tf_op jit(solution)/shard_map/ppermute | solution.py:79
  437.0 2.7 fusion.9
  439.7 97.9 %collective-permute-done.15 = bf16[3,512,512]{2,1,0:T(8,128)(2,1)S(1)} collective-permute-done((bf16[3,512,512]{2,1,0:T(8,128)(2,1)S(1)}, bf16[3,512,512]{2,1,0:T(8,128)(2,1)S(1)}, u32[]{:S(2)}, u32[]{:S(2)}) %collective-permute-start.15) | collective-permute-done | bytes 1572896 | tf_op jit(solution)/shard_map/ppermute | solution.py:79
  537.6 2.7 fusion.2
  540.2 21.4 %fusion.1 = bf16[3,512,512]{2,1,0:T(8,128)(2,1)} fusion(f32[3,512,512]{1,2,0:T(8,128)} %fusion.2, f32[3,512,512]{1,2,0:T(8,128)} %fusion.3, f32[3,512,512]{1,2,0:T(8,128)} %fusion.4, f32[3,512,512]{1,2,0:T(8,128)} %fusion.5, bf16[3,512,512]{2,1,0:T(8,128)(2,1)S(1)} %broadcast_multiply_fusion, f32[3,512,512]{1,2,0:T(8,128)} %fusion.6, ...), kind=kOutput, calls=%fused_computation.3 | convolution fusion | flops 823394304 | bytes 59768840 | tf_op jit(solution)/shard_map/drc,ck->drk/dot_general | solution.py:66
  (20 shorter events, 0.0 us)
Async XLA Ops:
  6.5 253.7 %all-reduce.2.cloned.1.call-start = ((), (), s32[]{:S(2)}) async-start(), calls=%async_computation | async-start | bytes 9437184 | tf_op jit(solution)/shard_map/psum | solution.py:73
  7.5 24.5 %copy-start.2 = (bf16[18,2]{1,0:T(8,128)(2,1)}, bf16[18,2]{1,0:T(8,128)(2,1)S(1)}, u32[]{:S(2)}) copy-start(bf16[18,2]{1,0:T(8,128)(2,1)S(1)} %copy.27) | copy-start | bytes 220
  21.1 1.4 copy-start.1
  22.8 83.5 %collective-permute-start.1 = (bf16[3,512,512]{2,1,0:T(8,128)(2,1)S(1)}, bf16[3,512,512]{2,1,0:T(8,128)(2,1)}, u32[]{:S(2)}, u32[]{:S(2)}) collective-permute-start(bf16[3,512,512]{2,1,0:T(8,128)(2,1)S(1)} %broadcast_multiply_fusion), channel_id=1, source_target_pairs={{14,0},{3,1},{0,2},{5,3},{2,4},{7,5},{4,6},{9,7},{6,8},{11,9},{8,1... | collective-permute-start | bytes 4718600 | tf_op jit(solution)/shard_map/ppermute | solution.py:50
  27.1 85.5 %collective-permute-start = (bf16[3,512,512]{2,1,0:T(8,128)(2,1)S(1)}, bf16[3,512,512]{2,1,0:T(8,128)(2,1)}, u32[]{:S(2)}, u32[]{:S(2)}) collective-permute-start(bf16[3,512,512]{2,1,0:T(8,128)(2,1)S(1)} %broadcast_multiply_fusion), channel_id=1, source_target_pairs={{15,0},{2,1},{1,2},{4,3},{3,4},{6,5},{5,6},{8,7},{7,8},{10,9},{9,1... | collective-permute-start | bytes 4718600 | tf_op jit(solution)/shard_map/ppermute | solution.py:50
  27.1 93.6 %collective-permute-start.4 = (bf16[3,512,512]{2,1,0:T(8,128)(2,1)S(1)}, bf16[3,512,512]{2,1,0:T(8,128)(2,1)}, u32[]{:S(2)}, u32[]{:S(2)}) collective-permute-start(bf16[3,512,512]{2,1,0:T(8,128)(2,1)S(1)} %broadcast_multiply_fusion), channel_id=1, source_target_pairs={{0,1},{1,0},{2,3},{3,2},{4,5},{5,4},{6,7},{7,6},{8,9},{9,8},{10,11... | collective-permute-start | bytes 4718600 | tf_op jit(solution)/shard_map/ppermute | solution.py:52
  28.0 129.1 %collective-permute-start.3 = (bf16[3,512,512]{2,1,0:T(8,128)(2,1)S(1)}, bf16[3,512,512]{2,1,0:T(8,128)(2,1)}, u32[]{:S(2)}, u32[]{:S(2)}) collective-permute-start(bf16[3,512,512]{2,1,0:T(8,128)(2,1)S(1)} %broadcast_multiply_fusion), channel_id=1, source_target_pairs={{12,0},{5,1},{14,2},{7,3},{0,4},{9,5},{2,6},{11,7},{4,8},{13,9},{6... | collective-permute-start | bytes 4718600 | tf_op jit(solution)/shard_map/ppermute | solution.py:50
  30.0 135.1 %collective-permute-start.2 = (bf16[3,512,512]{2,1,0:T(8,128)(2,1)S(1)}, bf16[3,512,512]{2,1,0:T(8,128)(2,1)}, u32[]{:S(2)}, u32[]{:S(2)}) collective-permute-start(bf16[3,512,512]{2,1,0:T(8,128)(2,1)S(1)} %broadcast_multiply_fusion), channel_id=1, source_target_pairs={{13,0},{4,1},{15,2},{6,3},{1,4},{8,5},{3,6},{10,7},{5,8},{12,9},{7... | collective-permute-start | bytes 4718600 | tf_op jit(solution)/shard_map/ppermute | solution.py:50
  32.0 7.7 %slice-start.2 = ((bf16[18,2]{1,0:T(8,128)(2,1)}), bf16[2,2]{1,0:T(2,128)(2,1)S(1)}, s32[]{:S(2)}) async-start(bf16[18,2]{1,0:T(8,128)(2,1)} %copy-done.2), calls=%async_computation.3 | async-start | bytes 1024 | tf_op jit(solution)/shard_map/dynamic_slice | solution.py:62
  42.7 74.0 %slice-start = ((s8[4718592]{0:T(1024)(128)(4,1)}), s8[524288]{0:T(1024)(128)(4,1)S(1)}, s32[]{:S(2)}) async-start(s8[4718592]{0:T(1024)(128)(4,1)} %bitcast.87), calls=%async_computation.1 | async-start | bytes 1048576
  42.8 3.8 copy-start.3
  42.8 73.9 %slice-start.1 = ((s8[4718592]{0:T(1024)(128)(4,1)}), s8[4194304]{0:T(1024)(128)(4,1)S(1)}, s32[]{:S(2)}) async-start(s8[4718592]{0:T(1024)(128)(4,1)} %bitcast.87), calls=%async_computation.2 | async-start | bytes 8388608
  106.3 87.7 %collective-permute-start.6 = (bf16[3,512,512]{2,1,0:T(8,128)(2,1)}, bf16[3,512,512]{2,1,0:T(8,128)(2,1)S(1)}, u32[]{:S(2)}, u32[]{:S(2)}) collective-permute-start(bf16[3,512,512]{2,1,0:T(8,128)(2,1)} %collective-permute-done.1), channel_id=1, source_target_pairs={{0,1},{1,0},{2,3},{3,2},{4,5},{5,4},{6,7},{7,6},{8,9},{9,8},{10,11... | collective-permute-start | bytes 4718600 | tf_op jit(solution)/shard_map/ppermute | solution.py:53
  112.6 84.0 %collective-permute-start.5 = (bf16[3,512,512]{2,1,0:T(8,128)(2,1)}, bf16[3,512,512]{2,1,0:T(8,128)(2,1)S(1)}, u32[]{:S(2)}, u32[]{:S(2)}) collective-permute-start(bf16[3,512,512]{2,1,0:T(8,128)(2,1)} %collective-permute-done), channel_id=1, source_target_pairs={{0,1},{1,0},{2,3},{3,2},{4,5},{5,4},{6,7},{7,6},{8,9},{9,8},{10,11... | collective-permute-start | bytes 4718600 | tf_op jit(solution)/shard_map/ppermute | solution.py:53
  120.8 143.3 %collective-permute-start.8 = (bf16[3,512,512]{2,1,0:T(8,128)(2,1)S(1)}, bf16[3,512,512]{2,1,0:T(8,128)(2,1)}, u32[]{:S(2)}, u32[]{:S(2)}) collective-permute-start(bf16[3,512,512]{2,1,0:T(8,128)(2,1)S(1)} %broadcast_multiply_fusion), channel_id=1, source_target_pairs={{0,64},{16,80},{32,96},{48,112},{64,128},{80,144},{96,160},{112,17... | collective-permute-start | bytes 4718600 | tf_op jit(solution)/shard_map/ppermute | solution.py:79
  157.1 135.8 %collective-permute-start.14 = (bf16[3,512,512]{2,1,0:T(8,128)(2,1)S(1)}, bf16[3,512,512]{2,1,0:T(8,128)(2,1)}, u32[]{:S(2)}, u32[]{:S(2)}) collective-permute-start(bf16[3,512,512]{2,1,0:T(8,128)(2,1)S(1)} %broadcast_multiply_fusion), channel_id=1, source_target_pairs={{0,208},{16,224},{32,240},{48,0},{64,16},{80,32},{96,48},{112,64},... | collective-permute-start | bytes 4718600 | tf_op jit(solution)/shard_map/ppermute | solution.py:79
  165.0 203.2 %collective-permute-start.13 = (bf16[3,512,512]{2,1,0:T(8,128)(2,1)S(1)}, bf16[3,512,512]{2,1,0:T(8,128)(2,1)}, u32[]{:S(2)}, u32[]{:S(2)}) collective-permute-start(bf16[3,512,512]{2,1,0:T(8,128)(2,1)S(1)} %broadcast_multiply_fusion), channel_id=1, source_target_pairs={{0,224},{16,240},{32,0},{48,16},{64,32},{80,48},{96,64},{112,80},{... | collective-permute-start | bytes 4718600 | tf_op jit(solution)/shard_map/ppermute | solution.py:79
  193.9 204.3 %collective-permute-start.12 = (bf16[3,512,512]{2,1,0:T(8,128)(2,1)S(1)}, bf16[3,512,512]{2,1,0:T(8,128)(2,1)}, u32[]{:S(2)}, u32[]{:S(2)}) collective-permute-start(bf16[3,512,512]{2,1,0:T(8,128)(2,1)S(1)} %broadcast_multiply_fusion), channel_id=1, source_target_pairs={{0,240},{16,0},{32,16},{48,32},{64,48},{80,64},{96,80},{112,96},{1... | collective-permute-start | bytes 4718600 | tf_op jit(solution)/shard_map/ppermute | solution.py:79
  196.6 207.4 %collective-permute-start.11 = (bf16[3,512,512]{2,1,0:T(8,128)(2,1)S(1)}, bf16[3,512,512]{2,1,0:T(8,128)(2,1)}, u32[]{:S(2)}, u32[]{:S(2)}) collective-permute-start(bf16[3,512,512]{2,1,0:T(8,128)(2,1)S(1)} %broadcast_multiply_fusion), channel_id=1, source_target_pairs={{0,16},{16,32},{32,48},{48,64},{64,80},{80,96},{96,112},{112,128},... | collective-permute-start | bytes 4718600 | tf_op jit(solution)/shard_map/ppermute | solution.py:79
  260.2 7.3 %copy-start = (bf16[4608,512]{1,0:T(8,128)(2,1)S(1)}, bf16[4608,512]{1,0:T(8,128)(2,1)}, u32[]{:S(2)}) copy-start(bf16[4608,512]{1,0:T(8,128)(2,1)} %all-reduce.2.cloned.1.call-done) | copy-start | bytes 14155780
  264.1 143.9 %collective-permute-start.10 = (bf16[3,512,512]{2,1,0:T(8,128)(2,1)S(1)}, bf16[3,512,512]{2,1,0:T(8,128)(2,1)S(1)}, u32[]{:S(2)}, u32[]{:S(2)}) collective-permute-start(bf16[3,512,512]{2,1,0:T(8,128)(2,1)S(1)} %broadcast_multiply_fusion), channel_id=1, source_target_pairs={{0,32},{16,48},{32,64},{48,80},{64,96},{80,112},{96,128},{112,144}... | collective-permute-start | bytes 4718600 | tf_op jit(solution)/shard_map/ppermute | solution.py:79
  292.9 144.1 %collective-permute-start.9 = (bf16[3,512,512]{2,1,0:T(8,128)(2,1)S(1)}, bf16[3,512,512]{2,1,0:T(8,128)(2,1)S(1)}, u32[]{:S(2)}, u32[]{:S(2)}) collective-permute-start(bf16[3,512,512]{2,1,0:T(8,128)(2,1)S(1)} %broadcast_multiply_fusion), channel_id=1, source_target_pairs={{0,48},{16,64},{32,80},{48,96},{64,112},{80,128},{96,144},{112,160... | collective-permute-start | bytes 4718600 | tf_op jit(solution)/shard_map/ppermute | solution.py:79
  368.2 169.4 %collective-permute-start.15 = (bf16[3,512,512]{2,1,0:T(8,128)(2,1)S(1)}, bf16[3,512,512]{2,1,0:T(8,128)(2,1)S(1)}, u32[]{:S(2)}, u32[]{:S(2)}) collective-permute-start(bf16[3,512,512]{2,1,0:T(8,128)(2,1)S(1)} %broadcast_multiply_fusion), channel_id=1, source_target_pairs={{0,192},{16,208},{32,224},{48,240},{64,0},{80,16},{96,32},{112,48}... | collective-permute-start | bytes 4718600 | tf_op jit(solution)/shard_map/ppermute | solution.py:79
  398.2 142.0 %collective-permute-start.7 = (bf16[3,512,512]{2,1,0:T(8,128)(2,1)}, bf16[3,512,512]{2,1,0:T(8,128)(2,1)}, u32[]{:S(2)}, u32[]{:S(2)}) collective-permute-start(bf16[3,512,512]{2,1,0:T(8,128)(2,1)} %collective-permute-done.2), channel_id=1, source_target_pairs={{0,1},{1,0},{2,3},{3,2},{4,5},{5,4},{6,7},{7,6},{8,9},{9,8},{10,11... | collective-permute-start | bytes 4718600 | tf_op jit(solution)/shard_map/ppermute | solution.py:53
Sparse Core Ops, SparseCore 0:
  21.3 238.8 all-reduce.1

commit v6 on v4

--- a/solution.py
+++ b/solution.py
@@ -56,11 +56,16 @@
         start = (offset + col_span) * col_width
         factors.append(lax.dynamic_slice_in_dim(strip_local, start, col_width, 0))
 
-    pairs = [(i * col_count + j, j * col_count + i) for i in range(row_count) for j in range(col_count)]
+    up_pairs = [(j * col_count + i, i * col_count + j) for i in range(row_count) for j in range(col_count) if j > i]
+    down_pairs = [(dst, src) for src, dst in up_pairs]
+    is_upper = row_at < col_at
+    is_diag = row_at == col_at
+    is_lower = row_at > col_at
     squared = sp2_branch == 1
     outs = []
     products = []
     mirrors = []
+    returns = []
     for d in range(p1_tiles.shape[0]):
         own = p1_local[d]
         if d >= 1:
@@ -71,18 +76,24 @@
         tiles = [own] + fetched + [partner_own] + partner_fetched
         if d >= 1:
             tiles, mirrors[d - 1] = lax.optimization_barrier((tiles, mirrors[d - 1]))
+        if d >= 2:
+            tiles, returns[d - 2] = lax.optimization_barrier((tiles, returns[d - 2]))
         summed = jnp.zeros((row_height, col_width), jnp.float32)
         for tile, factor in zip(tiles, factors):
             summed = summed + jnp.dot(tile, factor, preferred_element_type=jnp.float32)
         products.append(summed)
-        mirrored = lax.ppermute(summed, ("row", "col"), pairs)
+        mirrored = lax.ppermute(summed, ("row", "col"), up_pairs)
         mirrors.append(mirrored)
-        mirrored = mirrored.T
-        bracket = summed + mirrored
+        if d == p1_tiles.shape[0] - 1 and d >= 1:
+            mirrored, returns[d - 1] = lax.optimization_barrier((mirrored, returns[d - 1]))
+        other = jnp.where(is_diag, summed, mirrored).T
+        bracket = summed + other
         chosen = jnp.where(squared[d], bracket, 2.0 * own.astype(jnp.float32) - bracket)
-        outs.append(chosen)
-    chosen = jnp.stack(outs)
-    return mask_blocks(chosen, own_occ).astype(jnp.bfloat16)
+        result = mask_blocks(chosen, own_occ).astype(jnp.bfloat16)
+        returned = lax.ppermute(result, ("row", "col"), down_pairs)
+        returns.append(returned)
+        outs.append(jnp.where(is_lower, returned.T, result))
+    return jnp.stack(outs)
 
 
 def solution(mesh):

time: 411 us -> 509 us (1.24)
  the two profiles are of different devices: /device:TPU:218 before, /device:TPU:251 now
where the time goes in v6:
time: 509 us; the launch traced here: 503 us
  waiting for transfers between devices  333 us (65%)
  starting transfers between devices  84.6 us (17%)
  matrix products  36.9 us (7%)
  local copies, waits for them, and re-layouts  28.1 us (6%)
  other arithmetic  19.1 us (4%)
    ppermute x3, waiting for transfers between devices, body(): mirrored = lax.ppermute(summed, ('row', 'col'), up_pairs)  177 us
    ppermute x3, waiting for transfers between devices, body(): returned = lax.ppermute(result, ('row', 'col'), down_pairs)  124 us
    ppermute x9, starting transfers between devices, body(): lax.ppermute(fetched[j], 'col', swap)  44.8 us
    dot_general x27, matrix products, body(): summed = summed + jnp.dot(tile, factor, preferred_element_type=jnp.float32)  36.9 us
    ppermute x12, waiting for transfers between devices, body(): fetched = [lax.ppermute(own, 'col', fp) for fp in fetch_pairs]  32.1 us
    ppermute x12, starting transfers between devices, body(): fetched = [lax.ppermute(own, 'col', fp) for fp in fetch_pairs]  25.4 us
  transfers between devices with their start and end apart: 30, of which 8 were waited for; matrix products, arithmetic and copies ran while one was open for 8% of the time, Pallas kernels for 0%

profile of v6, /device:TPU:251, one launch (start us, length us, event | category | flops | bytes accessed | tf_op | source)
XLA Modules:
  0.0 502.8 jit_solution(11181991476345270604)
XLA Ops:
  0.0 2.4 reshape.28
  3.2 1.4 broadcast_multiply_fusion
  4.6 1.9 fusion.99
  6.5 2.1 collective-permute-start
  9.4 3.7 collective-permute-start.2
  14.3 7.7 %reshape.29 = bf16[18,256,2,256]{3,2,1,0:T(2,128)(2,1)} reshape(bf16[4608,512]{1,0:T(8,128)(2,1)} %param.8) | data formatting | bytes 9437184 | tf_op jit(solution)/shard_map/reshape | solution.py:13
  22.0 1.6 slice_multiply_fusion
  23.7 2.5 mul.109
  27.2 1.2 slice-done.1
  28.4 3.6 mul.112
  33.1 15.0 %collective-permute-start.7 = (bf16[512,512]{1,0:T(8,128)(2,1)}, bf16[512,512]{1,0:T(8,128)(2,1)S(1)}, u32[]{:S(2)}, u32[]{:S(2)}) collective-permute-start(bf16[512,512]{1,0:T(8,128)(2,1)} %collective-permute-done.2), channel_id=1, source_target_pairs={{0,1},{1,0},{2,3},{3,2},{4,5},{5,4},{6,7},{7,6},{8,9},{9,8},{10,11... | collective-permute-start | bytes 1572872 | tf_op jit(solution)/shard_map/ppermute | solution.py:75
  48.0 3.0 collective-permute-start.6
  51.1 1.6 fusion.60
  52.7 1.6 fusion.48
  54.4 1.5 convolution_add_fusion.4
  55.9 1.5 fusion.54
  59.3 3.8 collective-permute-start.10
  63.4 1.7 collective-permute-start.12
  65.1 1.8 collective-permute-start.8
  67.0 3.9 collective-permute-start.13
  70.8 7.3 %collective-permute-done.10 = bf16[512,512]{1,0:T(8,128)(2,1)} collective-permute-done((bf16[512,512]{1,0:T(8,128)(2,1)S(1)}, bf16[512,512]{1,0:T(8,128)(2,1)}, u32[]{:S(2)}, u32[]{:S(2)}) %collective-permute-start.10) | collective-permute-done | bytes 524320 | tf_op jit(solution)/shard_map/ppermute | solution.py:73
  78.2 1.5 collective-permute-start.14
  79.6 6.2 %collective-permute-done.11 = bf16[512,512]{1,0:T(8,128)(2,1)} collective-permute-done((bf16[512,512]{1,0:T(8,128)(2,1)S(1)}, bf16[512,512]{1,0:T(8,128)(2,1)}, u32[]{:S(2)}, u32[]{:S(2)}) %collective-permute-start.11) | collective-permute-done | bytes 524320 | tf_op jit(solution)/shard_map/ppermute | solution.py:73
  85.8 4.1 collective-permute-start.15
  89.9 10.4 %collective-permute-start.16 = (bf16[512,512]{1,0:T(8,128)(2,1)}, bf16[512,512]{1,0:T(8,128)(2,1)S(1)}, u32[]{:S(2)}, u32[]{:S(2)}) collective-permute-start(bf16[512,512]{1,0:T(8,128)(2,1)} %collective-permute-done.11), channel_id=1, source_target_pairs={{0,1},{1,0},{2,3},{3,2},{4,5},{5,4},{6,7},{7,6},{8,9},{9,8},{10,11... | collective-permute-start | bytes 1572872 | tf_op jit(solution)/shard_map/ppermute | solution.py:75
  100.8 177.2 %collective-permute-done.8 = f32[512,512]{0,1:T(8,128)S(1)} collective-permute-done((f32[512,512]{0,1:T(8,128)S(1)}, f32[512,512]{0,1:T(8,128)S(1)}, u32[]{:S(2)}, u32[]{:S(2)}) %collective-permute-start.8) | collective-permute-done | bytes 1048608 | tf_op jit(solution)/shard_map/ppermute | solution.py:85
  278.9 1.7 fusion.69
  280.6 1.7 fusion.64
  282.3 1.5 fusion.58
  283.8 1.5 fusion.52
  285.4 1.5 fusion.46
  286.9 1.5 fusion.41
  288.5 1.5 fusion.35
  290.0 1.5 fusion.29
  292.4 4.9 collective-permute-start.18
  298.6 8.7 %collective-permute-start.23 = (bf16[512,512]{1,0:T(8,128)(2,1)}, bf16[512,512]{1,0:T(8,128)(2,1)}, u32[]{:S(2)}, u32[]{:S(2)}) collective-permute-start(bf16[512,512]{1,0:T(8,128)(2,1)} %bitcast.29), channel_id=1, source_target_pairs={{12,0},{5,1},{14,2},{7,3},{0,4},{9,5},{2,6},{11,7},{4,8},{13,9},{6... | collective-permute-start | bytes 1572872 | tf_op jit(solution)/shard_map/ppermute | solution.py:73
  307.9 1.3 copy.39
  309.2 18.0 %collective-permute-done.20 = bf16[512,512]{1,0:T(8,128)(2,1)} collective-permute-done((bf16[512,512]{1,0:T(8,128)(2,1)}, bf16[512,512]{1,0:T(8,128)(2,1)}, u32[]{:S(2)}, u32[]{:S(2)}) %collective-permute-start.20) | collective-permute-done | bytes 524320 | tf_op jit(solution)/shard_map/ppermute | solution.py:73
  327.7 11.1 %collective-permute-start.26 = (bf16[512,512]{1,0:T(8,128)(2,1)}, bf16[512,512]{1,0:T(8,128)(2,1)}, u32[]{:S(2)}, u32[]{:S(2)}) collective-permute-start(bf16[512,512]{1,0:T(8,128)(2,1)} %collective-permute-done.21), channel_id=1, source_target_pairs={{0,1},{1,0},{2,3},{3,2},{4,5},{5,4},{6,7},{7,6},{8,9},{9,8},{10,11... | collective-permute-start | bytes 1572872 | tf_op jit(solution)/shard_map/ppermute | solution.py:75
  339.1 5.5 %fusion.22 = (bf16[512,512]{1,0:T(8,128)(2,1)}, bf16[512,512]{1,0:T(8,128)(2,1)}) fusion(f32[512,512]{1,0:T(8,128)S(1)} %bitcast.82, f32[512,512]{1,0:T(8,128)} %copy.39, bf16[512,512]{1,0:T(8,128)(2,1)} %bitcast.93, f32[512,512]{0,1:T(8,128)S(1)} %fusion.16, f32[512,512]{0,1:T(8,128)} %collective-permute-done.18, pred[]{:T(512)} %bitcast.4, pred[]{:T(512)S(6)} %eq.13, ...), kind=kLoop, calls=%fused_computation.31 | loop fusion | flops 4194304 | bytes 9437187 | tf_op jit(solution)/shard_map/convert_element_type | solution.py:92
  344.6 1.3 copy.29
  345.8 1.3 collective-permute-start.9
  347.2 109.8 %collective-permute-done.9 = bf16[512,512]{0,1:T(8,128)(2,1)} collective-permute-done((bf16[512,512]{0,1:T(8,128)(2,1)S(1)}, bf16[512,512]{0,1:T(8,128)(2,1)}, u32[]{:S(2)}, u32[]{:S(2)}) %collective-permute-start.9) | collective-permute-done | bytes 524320 | tf_op jit(solution)/shard_map/ppermute | solution.py:93
  457.0 1.6 fusion.67
  458.6 1.6 fusion.62
  460.3 1.6 fusion.56
  461.9 1.6 fusion.50
  463.6 1.7 fusion.44
  465.3 1.6 fusion.39
  466.9 1.6 fusion.33
  468.5 1.6 fusion.27
  470.2 1.8 fusion.18
  472.0 2.4 collective-permute-start.28
  474.4 1.0 copy.40
  475.4 1.3 collective-permute-start.19
  476.7 1.3 copy.41
  478.0 7.6 %collective-permute-done.19 = bf16[512,512]{0,1:T(8,128)(2,1)} collective-permute-done((bf16[512,512]{0,1:T(8,128)(2,1)}, bf16[512,512]{0,1:T(8,128)(2,1)}, u32[]{:S(2)}, u32[]{:S(2)}) %collective-permute-start.19) | collective-permute-done | bytes 524320 | tf_op jit(solution)/shard_map/ppermute | solution.py:93
  485.6 2.6 copy.42
  488.2 2.6 fusion.24
  490.8 1.3 collective-permute-start.29
  492.2 1.1 fusion.26
  493.3 1.1 fusion.25
  494.4 6.4 %collective-permute-done.29 = bf16[512,512]{1,0:T(8,128)(2,1)S(1)} collective-permute-done((bf16[512,512]{1,0:T(8,128)(2,1)S(1)}, bf16[512,512]{1,0:T(8,128)(2,1)S(1)}, u32[]{:S(2)}, u32[]{:S(2)}) %collective-permute-start.29) | collective-permute-done | bytes 524320 | tf_op jit(solution)/shard_map/ppermute | solution.py:93
  501.1 1.3 pad_maximum_fusion
  (88 shorter events, 12.3 us)
Async XLA Ops:
  0.0 14.0 %copy-start.11 = (s32[32,32]{1,0:T(8,128)S(1)}, s32[32,32]{1,0:T(8,128)}, u32[]{:S(2)}) copy-start(s32[32,32]{1,0:T(8,128)} %param.6) | copy-start | bytes 12292
  6.5 25.5 %copy-start.6 = (bf16[64,8,2,256]{3,1,2,0:T(8,128)(2,1)}, bf16[64,8,2,256]{3,1,2,0:T(8,128)(2,1)S(1)}, u32[]{:S(2)}) copy-start(bf16[64,8,2,256]{3,1,2,0:T(8,128)(2,1)S(1)} %copy.53) | copy-start | bytes 1572868
  6.5 44.5 %collective-permute-start = (bf16[512,512]{1,0:T(8,128)(2,1)S(1)}, bf16[512,512]{1,0:T(8,128)(2,1)}, u32[]{:S(2)}, u32[]{:S(2)}) collective-permute-start(bf16[512,512]{1,0:T(8,128)(2,1)S(1)} %bitcast.94), channel_id=1, source_target_pairs={{15,0},{2,1},{1,2},{4,3},{3,4},{6,5},{5,6},{8,7},{7,8},{10,9},{9,1... | collective-permute-start | bytes 1572872 | tf_op jit(solution)/shard_map/ppermute | solution.py:73
  8.7 44.0 %collective-permute-start.4 = (bf16[512,512]{1,0:T(8,128)(2,1)S(1)}, bf16[512,512]{1,0:T(8,128)(2,1)}, u32[]{:S(2)}, u32[]{:S(2)}) collective-permute-start(bf16[512,512]{1,0:T(8,128)(2,1)S(1)} %bitcast.95), channel_id=1, source_target_pairs={{0,1},{1,0},{2,3},{3,2},{4,5},{5,4},{6,7},{7,6},{8,9},{9,8},{10,11... | collective-permute-start | bytes 1572872 | tf_op jit(solution)/shard_map/ppermute | solution.py:74
  8.7 47.2 %collective-permute-start.3 = (bf16[512,512]{1,0:T(8,128)(2,1)S(1)}, bf16[512,512]{1,0:T(8,128)(2,1)}, u32[]{:S(2)}, u32[]{:S(2)}) collective-permute-start(bf16[512,512]{1,0:T(8,128)(2,1)S(1)} %bitcast.96), channel_id=1, source_target_pairs={{12,0},{5,1},{14,2},{7,3},{0,4},{9,5},{2,6},{11,7},{4,8},{13,9},{6... | collective-permute-start | bytes 1572872 | tf_op jit(solution)/shard_map/ppermute | solution.py:73
  9.4 23.6 %collective-permute-start.2 = (bf16[512,512]{1,0:T(8,128)(2,1)S(1)}, bf16[512,512]{1,0:T(8,128)(2,1)}, u32[]{:S(2)}, u32[]{:S(2)}) collective-permute-start(bf16[512,512]{1,0:T(8,128)(2,1)S(1)} %bitcast.97), channel_id=1, source_target_pairs={{13,0},{4,1},{15,2},{6,3},{1,4},{8,5},{3,6},{10,7},{5,8},{12,9},{7... | collective-permute-start | bytes 1572872 | tf_op jit(solution)/shard_map/ppermute | solution.py:73
  13.2 34.8 %collective-permute-start.1 = (bf16[512,512]{1,0:T(8,128)(2,1)S(1)}, bf16[512,512]{1,0:T(8,128)(2,1)S(1)}, u32[]{:S(2)}, u32[]{:S(2)}) collective-permute-start(bf16[512,512]{1,0:T(8,128)(2,1)S(1)} %bitcast.98), channel_id=1, source_target_pairs={{14,0},{3,1},{0,2},{5,3},{2,4},{7,5},{4,6},{9,7},{6,8},{11,9},{8,1... | collective-permute-start | bytes 1572872 | tf_op jit(solution)/shard_map/ppermute | solution.py:73
  23.7 267.9 %copy-start.1 = (bf16[64,8,2,256]{3,1,2,0:T(8,128)(2,1)}, bf16[64,8,2,256]{3,1,2,0:T(8,128)(2,1)S(1)}, u32[]{:S(2)}) copy-start(bf16[64,8,2,256]{3,1,2,0:T(8,128)(2,1)S(1)} %copy.54) | copy-start | bytes 1572868
  23.7 3.5 slice-start
  26.2 2.2 slice-start.1
  32.1 259.5 %copy-start.3 = (bf16[64,8,2,256]{3,1,2,0:T(8,128)(2,1)}, bf16[64,8,2,256]{3,1,2,0:T(8,128)(2,1)S(1)}, u32[]{:S(2)}) copy-start(bf16[64,8,2,256]{3,1,2,0:T(8,128)(2,1)S(1)} %copy.57) | copy-start | bytes 1572868
  32.1 22.3 %copy-start = (bf16[4608,512]{1,0:T(8,128)(2,1)S(1)}, bf16[4608,512]{1,0:T(8,128)(2,1)}, u32[]{:S(2)}) copy-start(bf16[4608,512]{1,0:T(8,128)(2,1)} %mul.112) | copy-start | bytes 14155780
  33.1 24.8 %collective-permute-start.7 = (bf16[512,512]{1,0:T(8,128)(2,1)}, bf16[512,512]{1,0:T(8,128)(2,1)S(1)}, u32[]{:S(2)}, u32[]{:S(2)}) collective-permute-start(bf16[512,512]{1,0:T(8,128)(2,1)} %collective-permute-done.2), channel_id=1, source_target_pairs={{0,1},{1,0},{2,3},{3,2},{4,5},{5,4},{6,7},{7,6},{8,9},{9,8},{10,11... | collective-permute-start | bytes 1572872 | tf_op jit(solution)/shard_map/ppermute | solution.py:75
  48.0 10.3 %collective-permute-start.6 = (bf16[512,512]{1,0:T(8,128)(2,1)S(1)}, bf16[512,512]{1,0:T(8,128)(2,1)S(1)}, u32[]{:S(2)}, u32[]{:S(2)}) collective-permute-start(bf16[512,512]{1,0:T(8,128)(2,1)S(1)} %collective-permute-done.1), channel_id=1, source_target_pairs={{0,1},{1,0},{2,3},{3,2},{4,5},{5,4},{6,7},{7,6},{8,9},{9,8},{10,11... | collective-permute-start | bytes 1572872 | tf_op jit(solution)/shard_map/ppermute | solution.py:75
  51.1 7.7 %collective-permute-start.5 = (bf16[512,512]{1,0:T(8,128)(2,1)}, bf16[512,512]{1,0:T(8,128)(2,1)S(1)}, u32[]{:S(2)}, u32[]{:S(2)}) collective-permute-start(bf16[512,512]{1,0:T(8,128)(2,1)} %collective-permute-done), channel_id=1, source_target_pairs={{0,1},{1,0},{2,3},{3,2},{4,5},{5,4},{6,7},{7,6},{8,9},{9,8},{10,11... | collective-permute-start | bytes 1572872 | tf_op jit(solution)/shard_map/ppermute | solution.py:75
  59.3 18.8 %collective-permute-start.10 = (bf16[512,512]{1,0:T(8,128)(2,1)S(1)}, bf16[512,512]{1,0:T(8,128)(2,1)}, u32[]{:S(2)}, u32[]{:S(2)}) collective-permute-start(bf16[512,512]{1,0:T(8,128)(2,1)S(1)} %bitcast.87), channel_id=1, source_target_pairs={{15,0},{2,1},{1,2},{4,3},{3,4},{6,5},{5,6},{8,7},{7,8},{10,9},{9,1... | collective-permute-start | bytes 1572872 | tf_op jit(solution)/shard_map/ppermute | solution.py:73
  63.1 22.7 %collective-permute-start.11 = (bf16[512,512]{1,0:T(8,128)(2,1)S(1)}, bf16[512,512]{1,0:T(8,128)(2,1)}, u32[]{:S(2)}, u32[]{:S(2)}) collective-permute-start(bf16[512,512]{1,0:T(8,128)(2,1)S(1)} %bitcast.88), channel_id=1, source_target_pairs={{14,0},{3,1},{0,2},{5,3},{2,4},{7,5},{4,6},{9,7},{6,8},{11,9},{8,1... | collective-permute-start | bytes 1572872 | tf_op jit(solution)/shard_map/ppermute | solution.py:73
  63.4 223.5 %copy-start.7 = (f32[512,512]{0,1:T(8,128)}, f32[512,512]{0,1:T(8,128)S(1)}, u32[]{:S(2)}) copy-start(f32[512,512]{0,1:T(8,128)S(1)} %copy.28) | copy-start | bytes 3145732
  63.4 26.5 %collective-permute-start.12 = (bf16[512,512]{1,0:T(8,128)(2,1)S(1)}, bf16[512,512]{1,0:T(8,128)(2,1)S(1)}, u32[]{:S(2)}, u32[]{:S(2)}) collective-permute-start(bf16[512,512]{1,0:T(8,128)(2,1)S(1)} %bitcast.89), channel_id=1, source_target_pairs={{13,0},{4,1},{15,2},{6,3},{1,4},{8,5},{3,6},{10,7},{5,8},{12,9},{7... | collective-permute-start | bytes 1572872 | tf_op jit(solution)/shard_map/ppermute | solution.py:73
  65.1 212.8 %collective-permute-start.8 = (f32[512,512]{0,1:T(8,128)S(1)}, f32[512,512]{0,1:T(8,128)S(1)}, u32[]{:S(2)}, u32[]{:S(2)}) collective-permute-start(f32[512,512]{0,1:T(8,128)S(1)} %copy.28), channel_id=1, source_target_pairs={{16,1},{32,2},{48,3},{64,4},{80,5},{96,6},{112,7},{128,8},{144,9},... | collective-permute-start | bytes 3145736 | tf_op jit(solution)/shard_map/ppermute | solution.py:85
  67.0 33.4 %collective-permute-start.13 = (bf16[512,512]{1,0:T(8,128)(2,1)S(1)}, bf16[512,512]{1,0:T(8,128)(2,1)S(1)}, u32[]{:S(2)}, u32[]{:S(2)}) collective-permute-start(bf16[512,512]{1,0:T(8,128)(2,1)S(1)} %bitcast.90), channel_id=1, source_target_pairs={{12,0},{5,1},{14,2},{7,3},{0,4},{9,5},{2,6},{11,7},{4,8},{13,9},{6... | collective-permute-start | bytes 1572872 | tf_op jit(solution)/shard_map/ppermute | solution.py:73
  78.2 22.6 %collective-permute-start.14 = (bf16[512,512]{1,0:T(8,128)(2,1)S(1)}, bf16[512,512]{1,0:T(8,128)(2,1)S(1)}, u32[]{:S(2)}, u32[]{:S(2)}) collective-permute-start(bf16[512,512]{1,0:T(8,128)(2,1)S(1)} %bitcast.91), channel_id=1, source_target_pairs={{0,1},{1,0},{2,3},{3,2},{4,5},{5,4},{6,7},{7,6},{8,9},{9,8},{10,11... | collective-permute-start | bytes 1572872 | tf_op jit(solution)/shard_map/ppermute | solution.py:74
  85.8 192.1 %collective-permute-start.15 = (bf16[512,512]{1,0:T(8,128)(2,1)}, bf16[512,512]{1,0:T(8,128)(2,1)S(1)}, u32[]{:S(2)}, u32[]{:S(2)}) collective-permute-start(bf16[512,512]{1,0:T(8,128)(2,1)} %collective-permute-done.10), channel_id=1, source_target_pairs={{0,1},{1,0},{2,3},{3,2},{4,5},{5,4},{6,7},{7,6},{8,9},{9,8},{10,11... | collective-permute-start | bytes 1572872 | tf_op jit(solution)/shard_map/ppermute | solution.py:75
  89.9 188.0 %collective-permute-start.16 = (bf16[512,512]{1,0:T(8,128)(2,1)}, bf16[512,512]{1,0:T(8,128)(2,1)S(1)}, u32[]{:S(2)}, u32[]{:S(2)}) collective-permute-start(bf16[512,512]{1,0:T(8,128)(2,1)} %collective-permute-done.11), channel_id=1, source_target_pairs={{0,1},{1,0},{2,3},{3,2},{4,5},{5,4},{6,7},{7,6},{8,9},{9,8},{10,11... | collective-permute-start | bytes 1572872 | tf_op jit(solution)/shard_map/ppermute | solution.py:75
  100.4 178.6 %collective-permute-start.17 = (bf16[512,512]{1,0:T(8,128)(2,1)S(1)}, bf16[512,512]{1,0:T(8,128)(2,1)S(1)}, u32[]{:S(2)}, u32[]{:S(2)}) collective-permute-start(bf16[512,512]{1,0:T(8,128)(2,1)S(1)} %collective-permute-done.12), channel_id=1, source_target_pairs={{0,1},{1,0},{2,3},{3,2},{4,5},{5,4},{6,7},{7,6},{8,9},{9,8},{10,11... | collective-permute-start | bytes 1572872 | tf_op jit(solution)/shard_map/ppermute | solution.py:75
  277.9 1.0 copy-start.10
  291.6 5.6 %copy-start.8 = (bf16[1,2,256,2,256]{4,3,2,1,0:T(2,128)(2,1)S(1)}, bf16[1,2,256,2,256]{4,3,2,1,0:T(2,128)(2,1)}, u32[]{:S(2)}) copy-start(bf16[1,2,256,2,256]{4,3,2,1,0:T(2,128)(2,1)} %get-tuple-element.66) | copy-start | bytes 1572868
  291.6 7.0 %copy-start.12 = (s32[3]{0:T(128)S(1)}, s32[3]{0:T(128)}, u32[]{:S(2)}) copy-start(s32[3]{0:T(128)} %param.5) | copy-start | bytes 40
  292.4 46.5 %collective-permute-start.18 = (f32[512,512]{0,1:T(8,128)S(1)}, f32[512,512]{0,1:T(8,128)}, u32[]{:S(2)}, u32[]{:S(2)}) collective-permute-start(f32[512,512]{0,1:T(8,128)S(1)} %fusion.16), channel_id=1, source_target_pairs={{16,1},{32,2},{48,3},{64,4},{80,5},{96,6},{112,7},{128,8},{144,9},... | collective-permute-start | bytes 3145736 | tf_op jit(solution)/shard_map/ppermute | solution.py:85
  298.1 29.1 %collective-permute-start.20 = (bf16[512,512]{1,0:T(8,128)(2,1)}, bf16[512,512]{1,0:T(8,128)(2,1)}, u32[]{:S(2)}, u32[]{:S(2)}) collective-permute-start(bf16[512,512]{1,0:T(8,128)(2,1)} %bitcast.29), channel_id=1, source_target_pairs={{15,0},{2,1},{1,2},{4,3},{3,4},{6,5},{5,6},{8,7},{7,8},{10,9},{9,1... | collective-permute-start | bytes 1572872 | tf_op jit(solution)/shard_map/ppermute | solution.py:73
  298.1 29.1 %collective-permute-start.21 = (bf16[512,512]{1,0:T(8,128)(2,1)}, bf16[512,512]{1,0:T(8,128)(2,1)}, u32[]{:S(2)}, u32[]{:S(2)}) collective-permute-start(bf16[512,512]{1,0:T(8,128)(2,1)} %bitcast.29), channel_id=1, source_target_pairs={{14,0},{3,1},{0,2},{5,3},{2,4},{7,5},{4,6},{9,7},{6,8},{11,9},{8,1... | collective-permute-start | bytes 1572872 | tf_op jit(solution)/shard_map/ppermute | solution.py:73
  298.1 29.6 %collective-permute-start.22 = (bf16[512,512]{1,0:T(8,128)(2,1)}, bf16[512,512]{1,0:T(8,128)(2,1)}, u32[]{:S(2)}, u32[]{:S(2)}) collective-permute-start(bf16[512,512]{1,0:T(8,128)(2,1)} %bitcast.29), channel_id=1, source_target_pairs={{13,0},{4,1},{15,2},{6,3},{1,4},{8,5},{3,6},{10,7},{5,8},{12,9},{7... | collective-permute-start | bytes 1572872 | tf_op jit(solution)/shard_map/ppermute | solution.py:73
  298.6 47.3 %collective-permute-start.23 = (bf16[512,512]{1,0:T(8,128)(2,1)}, bf16[512,512]{1,0:T(8,128)(2,1)}, u32[]{:S(2)}, u32[]{:S(2)}) collective-permute-start(bf16[512,512]{1,0:T(8,128)(2,1)} %bitcast.29), channel_id=1, source_target_pairs={{12,0},{5,1},{14,2},{7,3},{0,4},{9,5},{2,6},{11,7},{4,8},{13,9},{6... | collective-permute-start | bytes 1572872 | tf_op jit(solution)/shard_map/ppermute | solution.py:73
  327.2 20.0 %collective-permute-start.24 = (bf16[512,512]{1,0:T(8,128)(2,1)}, bf16[512,512]{1,0:T(8,128)(2,1)}, u32[]{:S(2)}, u32[]{:S(2)}) collective-permute-start(bf16[512,512]{1,0:T(8,128)(2,1)} %bitcast.29), channel_id=1, source_target_pairs={{0,1},{1,0},{2,3},{3,2},{4,5},{5,4},{6,7},{7,6},{8,9},{9,8},{10,11... | collective-permute-start | bytes 1572872 | tf_op jit(solution)/shard_map/ppermute | solution.py:74
  327.2 20.0 %collective-permute-start.25 = (bf16[512,512]{1,0:T(8,128)(2,1)}, bf16[512,512]{1,0:T(8,128)(2,1)}, u32[]{:S(2)}, u32[]{:S(2)}) collective-permute-start(bf16[512,512]{1,0:T(8,128)(2,1)} %collective-permute-done.20), channel_id=1, source_target_pairs={{0,1},{1,0},{2,3},{3,2},{4,5},{5,4},{6,7},{7,6},{8,9},{9,8},{10,11... | collective-permute-start | bytes 1572872 | tf_op jit(solution)/shard_map/ppermute | solution.py:75
  327.7 19.5 %collective-permute-start.26 = (bf16[512,512]{1,0:T(8,128)(2,1)}, bf16[512,512]{1,0:T(8,128)(2,1)}, u32[]{:S(2)}, u32[]{:S(2)}) collective-permute-start(bf16[512,512]{1,0:T(8,128)(2,1)} %collective-permute-done.21), channel_id=1, source_target_pairs={{0,1},{1,0},{2,3},{3,2},{4,5},{5,4},{6,7},{7,6},{8,9},{9,8},{10,11... | collective-permute-start | bytes 1572872 | tf_op jit(solution)/shard_map/ppermute | solution.py:75
  338.8 8.3 %collective-permute-start.27 = (bf16[512,512]{1,0:T(8,128)(2,1)}, bf16[512,512]{1,0:T(8,128)(2,1)}, u32[]{:S(2)}, u32[]{:S(2)}) collective-permute-start(bf16[512,512]{1,0:T(8,128)(2,1)} %collective-permute-done.22), channel_id=1, source_target_pairs={{0,1},{1,0},{2,3},{3,2},{4,5},{5,4},{6,7},{7,6},{8,9},{9,8},{10,11... | collective-permute-start | bytes 1572872 | tf_op jit(solution)/shard_map/ppermute | solution.py:75
  345.8 111.2 %collective-permute-start.9 = (bf16[512,512]{0,1:T(8,128)(2,1)S(1)}, bf16[512,512]{0,1:T(8,128)(2,1)}, u32[]{:S(2)}, u32[]{:S(2)}) collective-permute-start(bf16[512,512]{0,1:T(8,128)(2,1)S(1)} %copy.29), channel_id=1, source_target_pairs={{1,16},{2,32},{3,48},{4,64},{5,80},{6,96},{7,112},{8,128},{9,144},... | collective-permute-start | bytes 1572872 | tf_op jit(solution)/shard_map/ppermute | solution.py:93
  463.6 6.6 %copy-start.2 = (bf16[64,8,2,256]{3,1,2,0:T(8,128)(2,1)S(1)}, bf16[64,8,2,256]{3,1,2,0:T(8,128)(2,1)}, u32[]{:S(2)}) copy-start(bf16[64,8,2,256]{3,1,2,0:T(8,128)(2,1)} %copy-done.1) | copy-start | bytes 1572868
  470.2 4.2 copy-start.4
  472.0 13.6 %collective-permute-start.28 = (f32[512,512]{1,0:T(8,128)S(1)}, f32[512,512]{1,0:T(8,128)}, u32[]{:S(2)}, u32[]{:S(2)}) collective-permute-start(f32[512,512]{1,0:T(8,128)S(1)} %fusion.18), channel_id=1, source_target_pairs={{16,1},{32,2},{48,3},{64,4},{80,5},{96,6},{112,7},{128,8},{144,9},... | collective-permute-start | bytes 3145736 | tf_op jit(solution)/shard_map/ppermute | solution.py:85
  475.4 10.2 %collective-permute-start.19 = (bf16[512,512]{0,1:T(8,128)(2,1)}, bf16[512,512]{0,1:T(8,128)(2,1)}, u32[]{:S(2)}, u32[]{:S(2)}) collective-permute-start(bf16[512,512]{0,1:T(8,128)(2,1)} %copy.40), channel_id=1, source_target_pairs={{1,16},{2,32},{3,48},{4,64},{5,80},{6,96},{7,112},{8,128},{9,144},... | collective-permute-start | bytes 1572872 | tf_op jit(solution)/shard_map/ppermute | solution.py:93
  476.7 15.4 %copy-start.5 = (bf16[512,512]{1,0:T(8,128)(2,1)S(1)}, bf16[512,512]{1,0:T(8,128)(2,1)}, u32[]{:S(2)}) copy-start(bf16[512,512]{1,0:T(8,128)(2,1)} %get-tuple-element.69) | copy-start | bytes 1572868
  490.8 9.9 %copy-start.9 = (bf16[512,512]{1,0:T(8,128)(2,1)}, bf16[512,512]{1,0:T(8,128)(2,1)S(1)}, u32[]{:S(2)}) copy-start(bf16[512,512]{1,0:T(8,128)(2,1)S(1)} %fusion.24) | copy-start | bytes 1572868
  490.8 9.9 %collective-permute-start.29 = (bf16[512,512]{1,0:T(8,128)(2,1)S(1)}, bf16[512,512]{1,0:T(8,128)(2,1)S(1)}, u32[]{:S(2)}, u32[]{:S(2)}) collective-permute-start(bf16[512,512]{1,0:T(8,128)(2,1)S(1)} %fusion.24), channel_id=1, source_target_pairs={{1,16},{2,32},{3,48},{4,64},{5,80},{6,96},{7,112},{8,128},{9,144},... | collective-permute-start | bytes 1572872 | tf_op jit(solution)/shard_map/ppermute | solution.py:93

commit v7 on v4

--- a/solution.py
+++ b/solution.py
@@ -56,6 +56,8 @@
         start = (offset + col_span) * col_width
         factors.append(lax.dynamic_slice_in_dim(strip_local, start, col_width, 0))
 
+    band_factor = jnp.concatenate(factors, axis=0)
+
     pairs = [(i * col_count + j, j * col_count + i) for i in range(row_count) for j in range(col_count)]
     squared = sp2_branch == 1
     outs = []
@@ -71,9 +73,9 @@
         tiles = [own] + fetched + [partner_own] + partner_fetched
         if d >= 1:
             tiles, mirrors[d - 1] = lax.optimization_barrier((tiles, mirrors[d - 1]))
-        summed = jnp.zeros((row_height, col_width), jnp.float32)
-        for tile, factor in zip(tiles, factors):
-            summed = summed + jnp.dot(tile, factor, preferred_element_type=jnp.float32)
+        summed = jnp.dot(
+            jnp.concatenate(tiles, axis=1), band_factor, preferred_element_type=jnp.float32
+        )
         products.append(summed)
         mirrored = lax.ppermute(summed, ("row", "col"), pairs)
         mirrors.append(mirrored)

time: 411 us -> 415 us (level)
  the two profiles are of different devices: /device:TPU:218 before, /device:TPU:4 now
where the time goes in v7:
time: 415 us; the launch traced here: 413 us
  waiting for transfers between devices  236 us (57%)
  starting transfers between devices  87.7 us (21%)
  local copies, waits for them, and re-layouts  54.4 us (13%)
  other arithmetic  18.2 us (4%)
  matrix products  16.3 us (4%)
    ppermute x3, waiting for transfers between devices, body(): mirrored = lax.ppermute(summed, ('row', 'col'), pairs)  212 us
    ppermute x9, starting transfers between devices, body(): lax.ppermute(fetched[j], 'col', swap)  38.6 us
    unnamed x51, local copies, waits for them, and re-layouts  30.5 us
    ppermute x12, starting transfers between devices, body(): fetched = [lax.ppermute(own, 'col', fp) for fp in fetch_pairs]  30.2 us
    ppermute x12, waiting for transfers between devices, body(): fetched = [lax.ppermute(own, 'col', fp) for fp in fetch_pairs]  24 us
    dot_general x3, matrix products, body(): jnp.dot(jnp.concatenate(tiles, axis=1), band_factor, preferred_element_ty...  16.3 us
    ppermute x3, starting transfers between devices, body(): partner_own = lax.ppermute(own, 'col', swap)  10.5 us
    mul x3, other arithmetic, mask_blocks(): return (shaped * weight).reshape(values.shape)  10.3 us
  transfers between devices with their start and end apart: 27, of which 7 were waited for; matrix products, arithmetic and copies ran while one was open for 14% of the time, Pallas kernels for 0%

profile of v7, /device:TPU:4, one launch (start us, length us, event | category | flops | bytes accessed | tf_op | source)
XLA Modules:
  0.0 413.1 jit_solution(6633501721296611513)
XLA Ops:
  0.0 2.4 reshape.34
  2.4 0.8 dynamic-slice_convert_fusion
  3.1 1.4 broadcast_multiply_fusion
  4.6 1.1 fusion.7
  5.7 2.5 collective-permute-start
  8.2 2.2 collective-permute-start.2
  10.4 4.0 collective-permute-start.3
  14.5 0.9 constant_dynamic-update-slice_fusion.8
  15.5 0.1 copy.12
  15.6 2.5 mul.97
  18.1 3.0 copy.18
  21.1 7.7 %reshape.35 = bf16[18,256,2,256]{3,2,1,0:T(2,128)(2,1)} reshape(bf16[4608,512]{1,0:T(8,128)(2,1)} %param.8) | data formatting | bytes 9437184 | tf_op jit(solution)/shard_map/reshape | solution.py:13
  28.8 7.3 %mul.100 = bf16[4608,512]{1,0:T(8,128)(2,1)} multiply(bf16[4608,512]{1,0:T(8,128)(2,1)} %param.8, bf16[4608,512]{1,0:T(8,128)(2,1)} %bitcast.45) | non-fusion elementwise | flops 2359296 | bytes 14155776 | tf_op jit(solution)/shard_map/mul | solution.py:15
  36.1 1.6 slice_multiply_fusion
  37.8 0.8 constant_dynamic-update-slice_fusion.9
  38.6 1.9 dynamic-slice_dynamic-update-slice_fusion.7
  40.5 1.9 dynamic-slice_dynamic-update-slice_fusion.6
  42.4 1.9 dynamic-slice_dynamic-update-slice_fusion.5
  44.2 1.9 dynamic-slice_dynamic-update-slice_fusion.4
  46.1 1.9 dynamic-slice_dynamic-update-slice_fusion.3
  48.0 1.9 dynamic-slice_dynamic-update-slice_fusion.2
  49.9 1.9 dynamic-slice_dynamic-update-slice_fusion.1
  51.7 1.9 dynamic-slice_dynamic-update-slice_fusion
  53.7 0.6 collective-permute-start.5
  54.3 2.3 constant_dynamic-update-slice_fusion.7
  56.5 0.8 constant_dynamic-update-slice_fusion.6
  57.4 0.5 collective-permute-start.7
  57.9 0.9 constant_dynamic-update-slice_fusion.5
  58.8 1.9 constant_dynamic-update-slice_fusion.4
  60.7 1.9 constant_dynamic-update-slice_fusion.3
  62.6 0.9 constant_dynamic-update-slice_fusion.2
  63.5 0.8 constant_dynamic-update-slice_fusion.1
  64.3 0.9 constant_dynamic-update-slice_fusion
  65.2 4.4 %fusion.9 = f32[512,512]{1,0:T(8,128)S(1)} fusion(bf16[512,4608]{1,0:T(8,128)(2,1)} %constant_dynamic-update-slice_fusion, bf16[4608,512]{1,0:T(8,128)(2,1)S(1)} %copy-done.2), kind=kOutput, calls=%fused_computation.60 | convolution fusion | flops 2415919104 | bytes 10485760 | tf_op jit(solution)/shard_map/dot_general | solution.py:76
  69.7 2.3 collective-permute-start.9
  72.0 1.3 copy.13
  73.3 1.6 collective-permute-start.11
  74.9 3.7 collective-permute-start.8
  78.6 9.7 %collective-permute-start.12 = (bf16[512,512]{1,0:T(8,128)(2,1)S(1)}, bf16[512,512]{1,0:T(8,128)(2,1)S(1)}, u32[]{:S(2)}, u32[]{:S(2)}) collective-permute-start(bf16[512,512]{1,0:T(8,128)(2,1)S(1)} %bitcast.57), channel_id=1, source_target_pairs={{12,0},{5,1},{14,2},{7,3},{0,4},{9,5},{2,6},{11,7},{4,8},{13,9},{6... | collective-permute-start | bytes 1572872 | tf_op jit(solution)/shard_map/ppermute | solution.py:70
  88.3 1.5 collective-permute-done.9
  89.7 10.5 %collective-permute-start.13 = (bf16[512,512]{1,0:T(8,128)(2,1)S(1)}, bf16[512,512]{1,0:T(8,128)(2,1)S(1)}, u32[]{:S(2)}, u32[]{:S(2)}) collective-permute-start(bf16[512,512]{1,0:T(8,128)(2,1)S(1)} %bitcast.58), channel_id=1, source_target_pairs={{0,1},{1,0},{2,3},{3,2},{4,5},{5,4},{6,7},{7,6},{8,9},{9,8},{10,11... | collective-permute-start | bytes 1572872 | tf_op jit(solution)/shard_map/ppermute | solution.py:71
  100.3 10.2 %collective-permute-start.15 = (bf16[512,512]{1,0:T(8,128)(2,1)}, bf16[512,512]{1,0:T(8,128)(2,1)S(1)}, u32[]{:S(2)}, u32[]{:S(2)}) collective-permute-start(bf16[512,512]{1,0:T(8,128)(2,1)} %collective-permute-done.10), channel_id=1, source_target_pairs={{0,1},{1,0},{2,3},{3,2},{4,5},{5,4},{6,7},{7,6},{8,9},{9,8},{10,11... | collective-permute-start | bytes 1572872 | tf_op jit(solution)/shard_map/ppermute | solution.py:72
  110.5 78.6 %collective-permute-done.8 = f32[512,512]{0,1:T(8,128)} collective-permute-done((f32[512,512]{0,1:T(8,128)}, f32[512,512]{0,1:T(8,128)}, u32[]{:S(2)}, u32[]{:S(2)}) %collective-permute-start.8) | collective-permute-done | bytes 1048608 | tf_op jit(solution)/shard_map/ppermute | solution.py:80
  189.2 1.1 constant_dynamic-update-slice_fusion.17
  190.3 1.1 constant_dynamic-update-slice_fusion.16
  191.7 5.9 %fusion.10 = f32[512,512]{1,0:T(8,128)} fusion(bf16[512,4608]{1,0:T(8,128)(2,1)S(1)} %constant_dynamic-update-slice_fusion.10, bf16[4608,512]{1,0:T(8,128)(2,1)} %dynamic-slice_dynamic-update-slice_fusion), kind=kOutput, calls=%fused_computation.61 | convolution fusion | flops 2415919104 | bytes 10485760 | tf_op jit(solution)/shard_map/dot_general | solution.py:76
  197.6 2.5 copy.14
  200.1 2.6 collective-permute-start.17
  202.9 7.9 %collective-permute-start.21 = (bf16[512,512]{1,0:T(8,128)(2,1)S(1)}, bf16[512,512]{1,0:T(8,128)(2,1)S(1)}, u32[]{:S(2)}, u32[]{:S(2)}) collective-permute-start(bf16[512,512]{1,0:T(8,128)(2,1)S(1)} %bitcast.64), channel_id=1, source_target_pairs={{12,0},{5,1},{14,2},{7,3},{0,4},{9,5},{2,6},{11,7},{4,8},{13,9},{6... | collective-permute-start | bytes 1572872 | tf_op jit(solution)/shard_map/ppermute | solution.py:70
  210.7 3.7 collective-permute-done.18
  214.5 14.1 %collective-permute-done.19 = bf16[512,512]{1,0:T(8,128)(2,1)S(1)} collective-permute-done((bf16[512,512]{1,0:T(8,128)(2,1)S(1)}, bf16[512,512]{1,0:T(8,128)(2,1)S(1)}, u32[]{:S(2)}, u32[]{:S(2)}) %collective-permute-start.19) | collective-permute-done | bytes 524320 | tf_op jit(solution)/shard_map/ppermute | solution.py:70
  228.6 27.3 %collective-permute-start.24 = (bf16[512,512]{1,0:T(8,128)(2,1)S(1)}, bf16[512,512]{1,0:T(8,128)(2,1)S(1)}, u32[]{:S(2)}, u32[]{:S(2)}) collective-permute-start(bf16[512,512]{1,0:T(8,128)(2,1)S(1)} %collective-permute-done.19), channel_id=1, source_target_pairs={{0,1},{1,0},{2,3},{3,2},{4,5},{5,4},{6,7},{7,6},{8,9},{9,8},{10,11... | collective-permute-start | bytes 1572872 | tf_op jit(solution)/shard_map/ppermute | solution.py:72
  255.9 4.7 %collective-permute-done.21 = bf16[512,512]{1,0:T(8,128)(2,1)S(1)} collective-permute-done((bf16[512,512]{1,0:T(8,128)(2,1)S(1)}, bf16[512,512]{1,0:T(8,128)(2,1)S(1)}, u32[]{:S(2)}, u32[]{:S(2)}) %collective-permute-start.21) | collective-permute-done | bytes 524320 | tf_op jit(solution)/shard_map/ppermute | solution.py:70
  260.6 123.9 %collective-permute-done.17 = f32[512,512]{0,1:T(8,128)} collective-permute-done((f32[512,512]{0,1:T(8,128)}, f32[512,512]{0,1:T(8,128)}, u32[]{:S(2)}, u32[]{:S(2)}) %collective-permute-start.17) | collective-permute-done | bytes 1048608 | tf_op jit(solution)/shard_map/ppermute | solution.py:80
  384.9 5.9 %fusion.11 = f32[512,512]{1,0:T(8,128)} fusion(bf16[512,4608]{1,0:T(8,128)(2,1)S(1)} %constant_dynamic-update-slice_fusion.19, bf16[4608,512]{1,0:T(8,128)(2,1)} %dynamic-slice_dynamic-update-slice_fusion), kind=kOutput, calls=%fused_computation.62 | convolution fusion | flops 2415919104 | bytes 10485760 | tf_op jit(solution)/shard_map/dot_general | solution.py:76
  390.8 2.5 copy.15
  393.4 2.0 collective-permute-start.26
  395.4 0.3 mul.118
  395.9 0.7 fusion.8
  396.5 2.2 fusion.1
  398.7 2.2 fusion.2
  400.9 9.5 %collective-permute-done.26 = f32[512,512]{0,1:T(8,128)S(1)} collective-permute-done((f32[512,512]{0,1:T(8,128)}, f32[512,512]{0,1:T(8,128)S(1)}, u32[]{:S(2)}, u32[]{:S(2)}) %collective-permute-start.26) | collective-permute-done | bytes 1048608 | tf_op jit(solution)/shard_map/ppermute | solution.py:80
  410.4 0.9 fusion.3
  411.3 1.7 fusion
  (70 shorter events, 1.4 us)
Async XLA Ops:
  2.4 13.0 %copy-start.4 = (s32[32,32]{1,0:T(8,128)S(1)}, s32[32,32]{1,0:T(8,128)}, u32[]{:S(2)}) copy-start(s32[32,32]{1,0:T(8,128)} %param.6) | copy-start | bytes 12292
  5.7 47.9 %collective-permute-start = (bf16[512,512]{1,0:T(8,128)(2,1)S(1)}, bf16[512,512]{1,0:T(8,128)(2,1)}, u32[]{:S(2)}, u32[]{:S(2)}) collective-permute-start(bf16[512,512]{1,0:T(8,128)(2,1)S(1)} %bitcast.47), channel_id=1, source_target_pairs={{15,0},{2,1},{1,2},{4,3},{3,4},{6,5},{5,6},{8,7},{7,8},{10,9},{9,1... | collective-permute-start | bytes 1572872 | tf_op jit(solution)/shard_map/ppermute | solution.py:70
  8.2 48.3 %collective-permute-start.1 = (bf16[512,512]{1,0:T(8,128)(2,1)S(1)}, bf16[512,512]{1,0:T(8,128)(2,1)S(1)}, u32[]{:S(2)}, u32[]{:S(2)}) collective-permute-start(bf16[512,512]{1,0:T(8,128)(2,1)S(1)} %bitcast.48), channel_id=1, source_target_pairs={{14,0},{3,1},{0,2},{5,3},{2,4},{7,5},{4,6},{9,7},{6,8},{11,9},{8,1... | collective-permute-start | bytes 1572872 | tf_op jit(solution)/shard_map/ppermute | solution.py:70
  8.2 49.2 %collective-permute-start.2 = (bf16[512,512]{1,0:T(8,128)(2,1)S(1)}, bf16[512,512]{1,0:T(8,128)(2,1)S(1)}, u32[]{:S(2)}, u32[]{:S(2)}) collective-permute-start(bf16[512,512]{1,0:T(8,128)(2,1)S(1)} %bitcast.49), channel_id=1, source_target_pairs={{13,0},{4,1},{15,2},{6,3},{1,4},{8,5},{3,6},{10,7},{5,8},{12,9},{7... | collective-permute-start | bytes 1572872 | tf_op jit(solution)/shard_map/ppermute | solution.py:70
  10.4 48.3 %collective-permute-start.3 = (bf16[512,512]{1,0:T(8,128)(2,1)S(1)}, bf16[512,512]{1,0:T(8,128)(2,1)}, u32[]{:S(2)}, u32[]{:S(2)}) collective-permute-start(bf16[512,512]{1,0:T(8,128)(2,1)S(1)} %bitcast.50), channel_id=1, source_target_pairs={{12,0},{5,1},{14,2},{7,3},{0,4},{9,5},{2,6},{11,7},{4,8},{13,9},{6... | collective-permute-start | bytes 1572872 | tf_op jit(solution)/shard_map/ppermute | solution.py:70
  14.4 46.2 %collective-permute-start.4 = (bf16[512,512]{1,0:T(8,128)(2,1)S(1)}, bf16[512,512]{1,0:T(8,128)(2,1)}, u32[]{:S(2)}, u32[]{:S(2)}) collective-permute-start(bf16[512,512]{1,0:T(8,128)(2,1)S(1)} %bitcast.51), channel_id=1, source_target_pairs={{0,1},{1,0},{2,3},{3,2},{4,5},{5,4},{6,7},{7,6},{8,9},{9,8},{10,11... | collective-permute-start | bytes 1572872 | tf_op jit(solution)/shard_map/ppermute | solution.py:71
  15.6 5.5 %copy-start.3 = (bf16[18,2]{1,0:T(8,128)(2,1)}, bf16[18,2]{1,0:T(8,128)(2,1)S(1)}, u32[]{:S(2)}) copy-start(bf16[18,2]{1,0:T(8,128)(2,1)S(1)} %copy.12) | copy-start | bytes 220
  28.8 7.3 %slice-start = ((bf16[18,2]{1,0:T(8,128)(2,1)}), bf16[2,2]{1,0:T(2,128)(2,1)S(1)}, s32[]{:S(2)}) async-start(bf16[18,2]{1,0:T(8,128)(2,1)} %copy-done.3), calls=%async_computation | async-start | bytes 1024 | tf_op jit(solution)/shard_map/dynamic_slice | solution.py:57
  53.6 11.6 %copy-start.2 = (bf16[4608,512]{1,0:T(8,128)(2,1)S(1)}, bf16[4608,512]{1,0:T(8,128)(2,1)}, u32[]{:S(2)}) copy-start(bf16[4608,512]{1,0:T(8,128)(2,1)} %dynamic-slice_dynamic-update-slice_fusion) | copy-start | bytes 14155780
  53.7 8.9 %collective-permute-start.5 = (bf16[512,512]{1,0:T(8,128)(2,1)}, bf16[512,512]{1,0:T(8,128)(2,1)S(1)}, u32[]{:S(2)}, u32[]{:S(2)}) collective-permute-start(bf16[512,512]{1,0:T(8,128)(2,1)} %collective-permute-done), channel_id=1, source_target_pairs={{0,1},{1,0},{2,3},{3,2},{4,5},{5,4},{6,7},{7,6},{8,9},{9,8},{10,11... | collective-permute-start | bytes 1572872 | tf_op jit(solution)/shard_map/ppermute | solution.py:72
  56.5 6.9 %collective-permute-start.6 = (bf16[512,512]{1,0:T(8,128)(2,1)S(1)}, bf16[512,512]{1,0:T(8,128)(2,1)S(1)}, u32[]{:S(2)}, u32[]{:S(2)}) collective-permute-start(bf16[512,512]{1,0:T(8,128)(2,1)S(1)} %collective-permute-done.1), channel_id=1, source_target_pairs={{0,1},{1,0},{2,3},{3,2},{4,5},{5,4},{6,7},{7,6},{8,9},{9,8},{10,11... | collective-permute-start | bytes 1572872 | tf_op jit(solution)/shard_map/ppermute | solution.py:72
  57.4 6.9 %collective-permute-start.7 = (bf16[512,512]{1,0:T(8,128)(2,1)S(1)}, bf16[512,512]{1,0:T(8,128)(2,1)S(1)}, u32[]{:S(2)}, u32[]{:S(2)}) collective-permute-start(bf16[512,512]{1,0:T(8,128)(2,1)S(1)} %collective-permute-done.2), channel_id=1, source_target_pairs={{0,1},{1,0},{2,3},{3,2},{4,5},{5,4},{6,7},{7,6},{8,9},{9,8},{10,11... | collective-permute-start | bytes 1572872 | tf_op jit(solution)/shard_map/ppermute | solution.py:72
  69.7 20.1 %collective-permute-start.9 = (bf16[512,512]{1,0:T(8,128)(2,1)S(1)}, bf16[512,512]{1,0:T(8,128)(2,1)}, u32[]{:S(2)}, u32[]{:S(2)}) collective-permute-start(bf16[512,512]{1,0:T(8,128)(2,1)S(1)} %bitcast.54), channel_id=1, source_target_pairs={{15,0},{2,1},{1,2},{4,3},{3,4},{6,5},{5,6},{8,7},{7,8},{10,9},{9,1... | collective-permute-start | bytes 1572872 | tf_op jit(solution)/shard_map/ppermute | solution.py:70
  72.0 28.3 %collective-permute-start.10 = (bf16[512,512]{1,0:T(8,128)(2,1)S(1)}, bf16[512,512]{1,0:T(8,128)(2,1)}, u32[]{:S(2)}, u32[]{:S(2)}) collective-permute-start(bf16[512,512]{1,0:T(8,128)(2,1)S(1)} %bitcast.55), channel_id=1, source_target_pairs={{14,0},{3,1},{0,2},{5,3},{2,4},{7,5},{4,6},{9,7},{6,8},{11,9},{8,1... | collective-permute-start | bytes 1572872 | tf_op jit(solution)/shard_map/ppermute | solution.py:70
  73.3 27.0 %collective-permute-start.11 = (bf16[512,512]{1,0:T(8,128)(2,1)S(1)}, bf16[512,512]{1,0:T(8,128)(2,1)S(1)}, u32[]{:S(2)}, u32[]{:S(2)}) collective-permute-start(bf16[512,512]{1,0:T(8,128)(2,1)S(1)} %bitcast.56), channel_id=1, source_target_pairs={{13,0},{4,1},{15,2},{6,3},{1,4},{8,5},{3,6},{10,7},{5,8},{12,9},{7... | collective-permute-start | bytes 1572872 | tf_op jit(solution)/shard_map/ppermute | solution.py:70
  74.9 114.3 %collective-permute-start.8 = (f32[512,512]{0,1:T(8,128)}, f32[512,512]{0,1:T(8,128)}, u32[]{:S(2)}, u32[]{:S(2)}) collective-permute-start(f32[512,512]{0,1:T(8,128)} %copy.13), channel_id=1, source_target_pairs={{0,0},{1,16},{2,32},{3,48},{4,64},{5,80},{6,96},{7,112},{8,128},{9... | collective-permute-start | bytes 3145736 | tf_op jit(solution)/shard_map/ppermute | solution.py:80
  78.6 31.8 %collective-permute-start.12 = (bf16[512,512]{1,0:T(8,128)(2,1)S(1)}, bf16[512,512]{1,0:T(8,128)(2,1)S(1)}, u32[]{:S(2)}, u32[]{:S(2)}) collective-permute-start(bf16[512,512]{1,0:T(8,128)(2,1)S(1)} %bitcast.57), channel_id=1, source_target_pairs={{12,0},{5,1},{14,2},{7,3},{0,4},{9,5},{2,6},{11,7},{4,8},{13,9},{6... | collective-permute-start | bytes 1572872 | tf_op jit(solution)/shard_map/ppermute | solution.py:70
  89.7 20.8 %collective-permute-start.13 = (bf16[512,512]{1,0:T(8,128)(2,1)S(1)}, bf16[512,512]{1,0:T(8,128)(2,1)S(1)}, u32[]{:S(2)}, u32[]{:S(2)}) collective-permute-start(bf16[512,512]{1,0:T(8,128)(2,1)S(1)} %bitcast.58), channel_id=1, source_target_pairs={{0,1},{1,0},{2,3},{3,2},{4,5},{5,4},{6,7},{7,6},{8,9},{9,8},{10,11... | collective-permute-start | bytes 1572872 | tf_op jit(solution)/shard_map/ppermute | solution.py:71
  100.3 88.9 %collective-permute-start.14 = (bf16[512,512]{1,0:T(8,128)(2,1)}, bf16[512,512]{1,0:T(8,128)(2,1)S(1)}, u32[]{:S(2)}, u32[]{:S(2)}) collective-permute-start(bf16[512,512]{1,0:T(8,128)(2,1)} %collective-permute-done.9), channel_id=1, source_target_pairs={{0,1},{1,0},{2,3},{3,2},{4,5},{5,4},{6,7},{7,6},{8,9},{9,8},{10,11... | collective-permute-start | bytes 1572872 | tf_op jit(solution)/shard_map/ppermute | solution.py:72
  100.3 88.9 %collective-permute-start.15 = (bf16[512,512]{1,0:T(8,128)(2,1)}, bf16[512,512]{1,0:T(8,128)(2,1)S(1)}, u32[]{:S(2)}, u32[]{:S(2)}) collective-permute-start(bf16[512,512]{1,0:T(8,128)(2,1)} %collective-permute-done.10), channel_id=1, source_target_pairs={{0,1},{1,0},{2,3},{3,2},{4,5},{5,4},{6,7},{7,6},{8,9},{9,8},{10,11... | collective-permute-start | bytes 1572872 | tf_op jit(solution)/shard_map/ppermute | solution.py:72
  110.4 78.7 %collective-permute-start.16 = (bf16[512,512]{1,0:T(8,128)(2,1)S(1)}, bf16[512,512]{1,0:T(8,128)(2,1)S(1)}, u32[]{:S(2)}, u32[]{:S(2)}) collective-permute-start(bf16[512,512]{1,0:T(8,128)(2,1)S(1)} %collective-permute-done.11), channel_id=1, source_target_pairs={{0,1},{1,0},{2,3},{3,2},{4,5},{5,4},{6,7},{7,6},{8,9},{9,8},{10,11... | collective-permute-start | bytes 1572872 | tf_op jit(solution)/shard_map/ppermute | solution.py:72
  197.6 16.9 %collective-permute-start.18 = (bf16[512,512]{1,0:T(8,128)(2,1)S(1)}, bf16[512,512]{1,0:T(8,128)(2,1)S(1)}, u32[]{:S(2)}, u32[]{:S(2)}) collective-permute-start(bf16[512,512]{1,0:T(8,128)(2,1)S(1)} %bitcast.61), channel_id=1, source_target_pairs={{15,0},{2,1},{1,2},{4,3},{3,4},{6,5},{5,6},{8,7},{7,8},{10,9},{9,1... | collective-permute-start | bytes 1572872 | tf_op jit(solution)/shard_map/ppermute | solution.py:70
  200.1 28.5 %collective-permute-start.19 = (bf16[512,512]{1,0:T(8,128)(2,1)S(1)}, bf16[512,512]{1,0:T(8,128)(2,1)S(1)}, u32[]{:S(2)}, u32[]{:S(2)}) collective-permute-start(bf16[512,512]{1,0:T(8,128)(2,1)S(1)} %bitcast.62), channel_id=1, source_target_pairs={{14,0},{3,1},{0,2},{5,3},{2,4},{7,5},{4,6},{9,7},{6,8},{11,9},{8,1... | collective-permute-start | bytes 1572872 | tf_op jit(solution)/shard_map/ppermute | solution.py:70
  200.1 184.3 %collective-permute-start.17 = (f32[512,512]{0,1:T(8,128)}, f32[512,512]{0,1:T(8,128)}, u32[]{:S(2)}, u32[]{:S(2)}) collective-permute-start(f32[512,512]{0,1:T(8,128)} %copy.14), channel_id=1, source_target_pairs={{0,0},{1,16},{2,32},{3,48},{4,64},{5,80},{6,96},{7,112},{8,128},{9... | collective-permute-start | bytes 3145736 | tf_op jit(solution)/shard_map/ppermute | solution.py:80
  202.8 25.8 %collective-permute-start.20 = (bf16[512,512]{1,0:T(8,128)(2,1)S(1)}, bf16[512,512]{1,0:T(8,128)(2,1)S(1)}, u32[]{:S(2)}, u32[]{:S(2)}) collective-permute-start(bf16[512,512]{1,0:T(8,128)(2,1)S(1)} %bitcast.63), channel_id=1, source_target_pairs={{13,0},{4,1},{15,2},{6,3},{1,4},{8,5},{3,6},{10,7},{5,8},{12,9},{7... | collective-permute-start | bytes 1572872 | tf_op jit(solution)/shard_map/ppermute | solution.py:70
  202.9 57.7 %collective-permute-start.21 = (bf16[512,512]{1,0:T(8,128)(2,1)S(1)}, bf16[512,512]{1,0:T(8,128)(2,1)S(1)}, u32[]{:S(2)}, u32[]{:S(2)}) collective-permute-start(bf16[512,512]{1,0:T(8,128)(2,1)S(1)} %bitcast.64), channel_id=1, source_target_pairs={{12,0},{5,1},{14,2},{7,3},{0,4},{9,5},{2,6},{11,7},{4,8},{13,9},{6... | collective-permute-start | bytes 1572872 | tf_op jit(solution)/shard_map/ppermute | solution.py:70
  214.5 46.1 %collective-permute-start.22 = (bf16[512,512]{1,0:T(8,128)(2,1)S(1)}, bf16[512,512]{1,0:T(8,128)(2,1)S(1)}, u32[]{:S(2)}, u32[]{:S(2)}) collective-permute-start(bf16[512,512]{1,0:T(8,128)(2,1)S(1)} %bitcast.65), channel_id=1, source_target_pairs={{0,1},{1,0},{2,3},{3,2},{4,5},{5,4},{6,7},{7,6},{8,9},{9,8},{10,11... | collective-permute-start | bytes 1572872 | tf_op jit(solution)/shard_map/ppermute | solution.py:71
  228.6 155.9 %collective-permute-start.23 = (bf16[512,512]{1,0:T(8,128)(2,1)S(1)}, bf16[512,512]{1,0:T(8,128)(2,1)S(1)}, u32[]{:S(2)}, u32[]{:S(2)}) collective-permute-start(bf16[512,512]{1,0:T(8,128)(2,1)S(1)} %collective-permute-done.18), channel_id=1, source_target_pairs={{0,1},{1,0},{2,3},{3,2},{4,5},{5,4},{6,7},{7,6},{8,9},{9,8},{10,11... | collective-permute-start | bytes 1572872 | tf_op jit(solution)/shard_map/ppermute | solution.py:72
  228.6 155.9 %collective-permute-start.24 = (bf16[512,512]{1,0:T(8,128)(2,1)S(1)}, bf16[512,512]{1,0:T(8,128)(2,1)S(1)}, u32[]{:S(2)}, u32[]{:S(2)}) collective-permute-start(bf16[512,512]{1,0:T(8,128)(2,1)S(1)} %collective-permute-done.19), channel_id=1, source_target_pairs={{0,1},{1,0},{2,3},{3,2},{4,5},{5,4},{6,7},{7,6},{8,9},{9,8},{10,11... | collective-permute-start | bytes 1572872 | tf_op jit(solution)/shard_map/ppermute | solution.py:72
  260.6 123.9 %collective-permute-start.25 = (bf16[512,512]{1,0:T(8,128)(2,1)S(1)}, bf16[512,512]{1,0:T(8,128)(2,1)S(1)}, u32[]{:S(2)}, u32[]{:S(2)}) collective-permute-start(bf16[512,512]{1,0:T(8,128)(2,1)S(1)} %collective-permute-done.20), channel_id=1, source_target_pairs={{0,1},{1,0},{2,3},{3,2},{4,5},{5,4},{6,7},{7,6},{8,9},{9,8},{10,11... | collective-permute-start | bytes 1572872 | tf_op jit(solution)/shard_map/ppermute | solution.py:72
  390.8 5.0 %copy-start.5 = (s32[3]{0:T(128)S(1)}, s32[3]{0:T(128)}, u32[]{:S(2)}) copy-start(s32[3]{0:T(128)} %param.5) | copy-start | bytes 40
  393.4 5.3 %copy-start = (f32[512,512]{1,0:T(8,128)S(1)}, f32[512,512]{1,0:T(8,128)}, u32[]{:S(2)}) copy-start(f32[512,512]{1,0:T(8,128)} %fusion.10) | copy-start | bytes 3145732
  393.4 17.0 %collective-permute-start.26 = (f32[512,512]{0,1:T(8,128)}, f32[512,512]{0,1:T(8,128)S(1)}, u32[]{:S(2)}, u32[]{:S(2)}) collective-permute-start(f32[512,512]{0,1:T(8,128)} %copy.15), channel_id=1, source_target_pairs={{0,0},{1,16},{2,32},{3,48},{4,64},{5,80},{6,96},{7,112},{8,128},{9... | collective-permute-start | bytes 3145736 | tf_op jit(solution)/shard_map/ppermute | solution.py:80
  395.8 14.6 %copy-start.1 = (f32[512,512]{1,0:T(8,128)S(1)}, f32[512,512]{1,0:T(8,128)}, u32[]{:S(2)}) copy-start(f32[512,512]{1,0:T(8,128)} %fusion.11) | copy-start | bytes 3145732

commit v8 on v4

--- a/solution.py
+++ b/solution.py
@@ -64,7 +64,7 @@
     for d in range(p1_tiles.shape[0]):
         own = p1_local[d]
         if d >= 1:
-            own = lax.optimization_barrier((own, products[d - 1]))[0]
+            own = lax.optimization_barrier((own, products[0]))[0]
         fetched = [lax.ppermute(own, "col", fp) for fp in fetch_pairs]
         partner_own = lax.ppermute(own, "col", swap)
         partner_fetched = [lax.ppermute(fetched[j], "col", swap) for j in range(col_span - 1)]

time: 411 us -> 413 us (level)
  starting transfers between devices: 46.8 us -> 92.1 us
  waiting for transfers between devices: 287 us -> 247 us
    ppermute x3, starting transfers between devices: 1.72 us -> 47.1 us  [body(): partner_own = lax.ppermute(own, 'col', swap)]
    ppermute x12, waiting for transfers between devices: 89.3 us -> 46.3 us  [body(): fetched = [lax.ppermute(own, 'col', fp) for fp in fetch_pairs]]
    ppermute x12, starting transfers between devices: 28.7 us -> 17.4 us  [body(): fetched = [lax.ppermute(own, 'col', fp) for fp in fetch_pairs]]
    ppermute x9, starting transfers between devices: 7.95 us -> 18.2 us  [body(): lax.ppermute(fetched[j], 'col', swap)]
  transfers between devices with their start and end apart: 27 -> 27, of which waited for: 11 -> 11; matrix products, arithmetic and copies ran while one was open for 10% -> 12% of each run, Pallas kernels for 0% -> 0%
where the time goes in v8:
time: 413 us; the launch traced here: 407 us
  waiting for transfers between devices  247 us (60%)
  starting transfers between devices  92.1 us (22%)
  local copies, waits for them, and re-layouts  26.8 us (6%)
  matrix products  23.2 us (6%)
  other arithmetic  16.8 us (4%)
    ppermute x3, waiting for transfers between devices, body(): mirrored = lax.ppermute(summed, ('row', 'col'), pairs)  197 us
    ppermute x3, starting transfers between devices, body(): partner_own = lax.ppermute(own, 'col', swap)  47.1 us
    ppermute x12, waiting for transfers between devices, body(): fetched = [lax.ppermute(own, 'col', fp) for fp in fetch_pairs]  46.3 us
    dot_general x27, matrix products, body(): summed = summed + jnp.dot(tile, factor, preferred_element_type=jnp.float32)  23.2 us
    ppermute x9, starting transfers between devices, body(): lax.ppermute(fetched[j], 'col', swap)  18.2 us
    ppermute x12, starting transfers between devices, body(): fetched = [lax.ppermute(own, 'col', fp) for fp in fetch_pairs]  17.4 us
    reshape x2, local copies, waits for them, and re-layouts, mask_blocks(): shaped = values.reshape(leading + (row_blocks, BLK, col_blocks, BLK))  10.1 us
    ppermute x3, starting transfers between devices, body(): mirrored = lax.ppermute(summed, ('row', 'col'), pairs)  9.45 us
  transfers between devices with their start and end apart: 27, of which 11 were waited for; matrix products, arithmetic and copies ran while one was open for 12% of the time, Pallas kernels for 0%

profile of v8, /device:TPU:218, one launch (start us, length us, event | category | flops | bytes accessed | tf_op | source)
XLA Modules:
  0.0 406.6 jit_solution(847568245032610805)
XLA Ops:
  0.0 2.4 reshape.34
  2.4 0.8 dynamic-slice_convert_fusion
  3.2 1.4 broadcast_multiply_fusion
  4.6 1.9 fusion.95
  6.9 1.7 collective-permute-start.4
  8.6 2.6 collective-permute-start.3
  11.2 1.1 collective-permute-start.2
  12.3 4.6 %collective-permute-start.1 = (bf16[512,512]{1,0:T(8,128)(2,1)S(1)}, bf16[512,512]{1,0:T(8,128)(2,1)S(1)}, u32[]{:S(2)}, u32[]{:S(2)}) collective-permute-start(bf16[512,512]{1,0:T(8,128)(2,1)S(1)} %bitcast.96), channel_id=1, source_target_pairs={{14,0},{3,1},{0,2},{5,3},{2,4},{7,5},{4,6},{9,7},{6,8},{11,9},{8,1... | collective-permute-start | bytes 1572872 | tf_op jit(solution)/shard_map/ppermute | solution.py:68
  17.1 7.7 %reshape.35 = bf16[18,256,2,256]{3,2,1,0:T(2,128)(2,1)} reshape(bf16[4608,512]{1,0:T(8,128)(2,1)} %param.8) | data formatting | bytes 9437184 | tf_op jit(solution)/shard_map/reshape | solution.py:13
  24.8 1.6 slice_multiply_fusion
  26.5 2.5 mul.97
  29.0 1.0 copy.72
  30.0 1.2 slice-done.3
  31.2 3.6 mul.100
  35.3 12.1 %collective-permute-done.2 = bf16[512,512]{1,0:T(8,128)(2,1)} collective-permute-done((bf16[512,512]{1,0:T(8,128)(2,1)S(1)}, bf16[512,512]{1,0:T(8,128)(2,1)}, u32[]{:S(2)}, u32[]{:S(2)}) %collective-permute-start.2) | collective-permute-done | bytes 524320 | tf_op jit(solution)/shard_map/ppermute | solution.py:68
  47.4 3.0 collective-permute-done.1
  50.4 0.5 collective-permute-start.5
  50.9 1.6 fusion.56
  52.6 1.6 fusion.44
  54.2 1.5 convolution_add_fusion.4
  55.7 1.5 fusion.50
  57.2 0.5 fusion.15
  58.7 0.5 fusion.12
  59.3 1.3 copy.31
  60.6 3.1 collective-permute-start.8
  63.7 4.2 %collective-permute-start.10 = (bf16[512,512]{1,0:T(8,128)(2,1)S(1)}, bf16[512,512]{1,0:T(8,128)(2,1)S(1)}, u32[]{:S(2)}, u32[]{:S(2)}) collective-permute-start(bf16[512,512]{1,0:T(8,128)(2,1)S(1)} %bitcast.79), channel_id=1, source_target_pairs={{14,0},{3,1},{0,2},{5,3},{2,4},{7,5},{4,6},{9,7},{6,8},{11,9},{8,1... | collective-permute-start | bytes 1572872 | tf_op jit(solution)/shard_map/ppermute | solution.py:68
  67.8 4.3 %collective-permute-start.12 = (bf16[512,512]{1,0:T(8,128)(2,1)S(1)}, bf16[512,512]{1,0:T(8,128)(2,1)S(1)}, u32[]{:S(2)}, u32[]{:S(2)}) collective-permute-start(bf16[512,512]{1,0:T(8,128)(2,1)S(1)} %bitcast.81), channel_id=1, source_target_pairs={{12,0},{5,1},{14,2},{7,3},{0,4},{9,5},{2,6},{11,7},{4,8},{13,9},{6... | collective-permute-start | bytes 1572872 | tf_op jit(solution)/shard_map/ppermute | solution.py:68
  72.2 16.5 %collective-permute-done.10 = bf16[512,512]{1,0:T(8,128)(2,1)S(1)} collective-permute-done((bf16[512,512]{1,0:T(8,128)(2,1)S(1)}, bf16[512,512]{1,0:T(8,128)(2,1)S(1)}, u32[]{:S(2)}, u32[]{:S(2)}) %collective-permute-start.10) | collective-permute-done | bytes 524320 | tf_op jit(solution)/shard_map/ppermute | solution.py:68
  88.7 1.5 collective-permute-start.14
  90.2 14.7 %collective-permute-done.11 = bf16[512,512]{1,0:T(8,128)(2,1)S(1)} collective-permute-done((bf16[512,512]{1,0:T(8,128)(2,1)S(1)}, bf16[512,512]{1,0:T(8,128)(2,1)S(1)}, u32[]{:S(2)}, u32[]{:S(2)}) %collective-permute-start.11) | collective-permute-done | bytes 524320 | tf_op jit(solution)/shard_map/ppermute | solution.py:68
  104.9 15.3 %collective-permute-start.16 = (bf16[512,512]{1,0:T(8,128)(2,1)S(1)}, bf16[512,512]{1,0:T(8,128)(2,1)S(1)}, u32[]{:S(2)}, u32[]{:S(2)}) collective-permute-start(bf16[512,512]{1,0:T(8,128)(2,1)S(1)} %collective-permute-done.11), channel_id=1, source_target_pairs={{0,1},{1,0},{2,3},{3,2},{4,5},{5,4},{6,7},{7,6},{8,9},{9,8},{10,11... | collective-permute-start | bytes 1572872 | tf_op jit(solution)/shard_map/ppermute | solution.py:70
  120.2 1.3 copy.74
  121.6 78.8 %collective-permute-done.8 = f32[512,512]{0,1:T(8,128)S(1)} collective-permute-done((f32[512,512]{0,1:T(8,128)}, f32[512,512]{0,1:T(8,128)S(1)}, u32[]{:S(2)}, u32[]{:S(2)}) %collective-permute-start.8) | collective-permute-done | bytes 1048608 | tf_op jit(solution)/shard_map/ppermute | solution.py:78
  200.6 0.8 copy-done.6
  201.4 1.7 fusion.65
  203.0 1.5 fusion.60
  204.6 1.5 fusion.54
  206.1 1.5 fusion.48
  207.7 0.5 fusion.42
  209.6 0.8 fusion.17
  210.4 3.1 collective-permute-start.17
  213.6 45.4 %collective-permute-start.22 = (bf16[512,512]{1,0:T(8,128)(2,1)S(1)}, bf16[512,512]{1,0:T(8,128)(2,1)S(1)}, u32[]{:S(2)}, u32[]{:S(2)}) collective-permute-start(bf16[512,512]{1,0:T(8,128)(2,1)S(1)} %bitcast.89), channel_id=1, source_target_pairs={{0,1},{1,0},{2,3},{3,2},{4,5},{5,4},{6,7},{7,6},{8,9},{9,8},{10,11... | collective-permute-start | bytes 1572872 | tf_op jit(solution)/shard_map/ppermute | solution.py:69
  259.9 0.7 collective-permute-done.22
  260.5 0.7 collective-permute-done.23
  261.3 0.7 collective-permute-done.24
  262.0 0.7 collective-permute-done.25
  262.8 87.9 %collective-permute-done.17 = f32[512,512]{0,1:T(8,128)S(1)} collective-permute-done((f32[512,512]{0,1:T(8,128)S(1)}, f32[512,512]{0,1:T(8,128)S(1)}, u32[]{:S(2)}, u32[]{:S(2)}) %collective-permute-start.17) | collective-permute-done | bytes 1048608 | tf_op jit(solution)/shard_map/ppermute | solution.py:78
  350.7 0.5 fusion.63
  351.2 0.5 fusion.58
  351.7 0.5 fusion.52
  352.2 0.5 fusion.46
  352.7 0.5 fusion.40
  353.2 0.5 fusion.35
  354.7 1.7 fusion.19
  356.4 3.3 collective-permute-start.26
  360.0 1.1 copy.75
  361.1 0.6 fusion.96
  361.8 2.6 copy.41
  364.3 3.0 fusion.20
  367.4 1.6 copy.51
  369.0 2.5 fusion.21
  371.6 30.7 %collective-permute-done.26 = f32[512,512]{0,1:T(8,128)} collective-permute-done((f32[512,512]{0,1:T(8,128)}, f32[512,512]{0,1:T(8,128)}, u32[]{:S(2)}, u32[]{:S(2)}) %collective-permute-start.26) | collective-permute-done | bytes 1048608 | tf_op jit(solution)/shard_map/ppermute | solution.py:78
  402.3 2.1 fusion.22
  404.4 1.7 fusion
  (75 shorter events, 6.2 us)
Async XLA Ops:
  0.0 16.8 %copy-start.8 = (s32[32,32]{1,0:T(8,128)S(1)}, s32[32,32]{1,0:T(8,128)}, u32[]{:S(2)}) copy-start(s32[32,32]{1,0:T(8,128)} %param.6) | copy-start | bytes 12292
  6.6 28.3 %copy-start.1 = (bf16[64,8,2,256]{3,1,2,0:T(8,128)(2,1)}, bf16[64,8,2,256]{3,1,2,0:T(8,128)(2,1)S(1)}, u32[]{:S(2)}) copy-start(bf16[64,8,2,256]{3,1,2,0:T(8,128)(2,1)S(1)} %copy.70) | copy-start | bytes 1572868
  6.6 43.8 %collective-permute-start = (bf16[512,512]{1,0:T(8,128)(2,1)S(1)}, bf16[512,512]{1,0:T(8,128)(2,1)}, u32[]{:S(2)}, u32[]{:S(2)}) collective-permute-start(bf16[512,512]{1,0:T(8,128)(2,1)S(1)} %bitcast.92), channel_id=1, source_target_pairs={{15,0},{2,1},{1,2},{4,3},{3,4},{6,5},{5,6},{8,7},{7,8},{10,9},{9,1... | collective-permute-start | bytes 1572872 | tf_op jit(solution)/shard_map/ppermute | solution.py:68
  6.9 45.7 %collective-permute-start.4 = (bf16[512,512]{1,0:T(8,128)(2,1)S(1)}, bf16[512,512]{1,0:T(8,128)(2,1)}, u32[]{:S(2)}, u32[]{:S(2)}) collective-permute-start(bf16[512,512]{1,0:T(8,128)(2,1)S(1)} %bitcast.93), channel_id=1, source_target_pairs={{0,1},{1,0},{2,3},{3,2},{4,5},{5,4},{6,7},{7,6},{8,9},{9,8},{10,11... | collective-permute-start | bytes 1572872 | tf_op jit(solution)/shard_map/ppermute | solution.py:69
  8.6 47.2 %collective-permute-start.3 = (bf16[512,512]{1,0:T(8,128)(2,1)S(1)}, bf16[512,512]{1,0:T(8,128)(2,1)}, u32[]{:S(2)}, u32[]{:S(2)}) collective-permute-start(bf16[512,512]{1,0:T(8,128)(2,1)S(1)} %bitcast.94), channel_id=1, source_target_pairs={{12,0},{5,1},{14,2},{7,3},{0,4},{9,5},{2,6},{11,7},{4,8},{13,9},{6... | collective-permute-start | bytes 1572872 | tf_op jit(solution)/shard_map/ppermute | solution.py:68
  11.2 36.2 %collective-permute-start.2 = (bf16[512,512]{1,0:T(8,128)(2,1)S(1)}, bf16[512,512]{1,0:T(8,128)(2,1)}, u32[]{:S(2)}, u32[]{:S(2)}) collective-permute-start(bf16[512,512]{1,0:T(8,128)(2,1)S(1)} %bitcast.95), channel_id=1, source_target_pairs={{13,0},{4,1},{15,2},{6,3},{1,4},{8,5},{3,6},{10,7},{5,8},{12,9},{7... | collective-permute-start | bytes 1572872 | tf_op jit(solution)/shard_map/ppermute | solution.py:68
  12.3 38.2 %collective-permute-start.1 = (bf16[512,512]{1,0:T(8,128)(2,1)S(1)}, bf16[512,512]{1,0:T(8,128)(2,1)S(1)}, u32[]{:S(2)}, u32[]{:S(2)}) collective-permute-start(bf16[512,512]{1,0:T(8,128)(2,1)S(1)} %bitcast.96), channel_id=1, source_target_pairs={{14,0},{3,1},{0,2},{5,3},{2,4},{7,5},{4,6},{9,7},{6,8},{11,9},{8,1... | collective-permute-start | bytes 1572872 | tf_op jit(solution)/shard_map/ppermute | solution.py:68
  26.5 3.5 slice-start.2
  29.0 2.2 slice-start.3
  34.9 19.4 %copy-start = (bf16[4608,512]{1,0:T(8,128)(2,1)S(1)}, bf16[4608,512]{1,0:T(8,128)(2,1)}, u32[]{:S(2)}) copy-start(bf16[4608,512]{1,0:T(8,128)(2,1)} %mul.100) | copy-start | bytes 14155780
  47.4 10.4 %collective-permute-start.7 = (bf16[512,512]{1,0:T(8,128)(2,1)}, bf16[512,512]{1,0:T(8,128)(2,1)S(1)}, u32[]{:S(2)}, u32[]{:S(2)}) collective-permute-start(bf16[512,512]{1,0:T(8,128)(2,1)} %collective-permute-done.2), channel_id=1, source_target_pairs={{0,1},{1,0},{2,3},{3,2},{4,5},{5,4},{6,7},{7,6},{8,9},{9,8},{10,11... | collective-permute-start | bytes 1572872 | tf_op jit(solution)/shard_map/ppermute | solution.py:70
  50.4 7.8 %collective-permute-start.6 = (bf16[512,512]{1,0:T(8,128)(2,1)S(1)}, bf16[512,512]{1,0:T(8,128)(2,1)S(1)}, u32[]{:S(2)}, u32[]{:S(2)}) collective-permute-start(bf16[512,512]{1,0:T(8,128)(2,1)S(1)} %collective-permute-done.1), channel_id=1, source_target_pairs={{0,1},{1,0},{2,3},{3,2},{4,5},{5,4},{6,7},{7,6},{8,9},{9,8},{10,11... | collective-permute-start | bytes 1572872 | tf_op jit(solution)/shard_map/ppermute | solution.py:70
  50.4 8.2 %collective-permute-start.5 = (bf16[512,512]{1,0:T(8,128)(2,1)}, bf16[512,512]{1,0:T(8,128)(2,1)S(1)}, u32[]{:S(2)}, u32[]{:S(2)}) collective-permute-start(bf16[512,512]{1,0:T(8,128)(2,1)} %collective-permute-done), channel_id=1, source_target_pairs={{0,1},{1,0},{2,3},{3,2},{4,5},{5,4},{6,7},{7,6},{8,9},{9,8},{10,11... | collective-permute-start | bytes 1572872 | tf_op jit(solution)/shard_map/ppermute | solution.py:70
  58.7 149.0 %slice-start = ((s8[4718592]{0:T(1024)(128)(4,1)}), s8[524288]{0:T(1024)(128)(4,1)S(1)}, s32[]{:S(2)}) async-start(s8[4718592]{0:T(1024)(128)(4,1)} %bitcast.69), calls=%async_computation | async-start | bytes 1048576
  59.2 13.0 %collective-permute-start.9 = (bf16[512,512]{1,0:T(8,128)(2,1)S(1)}, bf16[512,512]{1,0:T(8,128)(2,1)}, u32[]{:S(2)}, u32[]{:S(2)}) collective-permute-start(bf16[512,512]{1,0:T(8,128)(2,1)S(1)} %bitcast.78), channel_id=1, source_target_pairs={{15,0},{2,1},{1,2},{4,3},{3,4},{6,5},{5,6},{8,7},{7,8},{10,9},{9,1... | collective-permute-start | bytes 1572872 | tf_op jit(solution)/shard_map/ppermute | solution.py:68
  60.6 139.7 %collective-permute-start.8 = (f32[512,512]{0,1:T(8,128)}, f32[512,512]{0,1:T(8,128)S(1)}, u32[]{:S(2)}, u32[]{:S(2)}) collective-permute-start(f32[512,512]{0,1:T(8,128)} %copy.31), channel_id=1, source_target_pairs={{0,0},{1,16},{2,32},{3,48},{4,64},{5,80},{6,96},{7,112},{8,128},{9... | collective-permute-start | bytes 3145736 | tf_op jit(solution)/shard_map/ppermute | solution.py:78
  63.7 25.0 %collective-permute-start.10 = (bf16[512,512]{1,0:T(8,128)(2,1)S(1)}, bf16[512,512]{1,0:T(8,128)(2,1)S(1)}, u32[]{:S(2)}, u32[]{:S(2)}) collective-permute-start(bf16[512,512]{1,0:T(8,128)(2,1)S(1)} %bitcast.79), channel_id=1, source_target_pairs={{14,0},{3,1},{0,2},{5,3},{2,4},{7,5},{4,6},{9,7},{6,8},{11,9},{8,1... | collective-permute-start | bytes 1572872 | tf_op jit(solution)/shard_map/ppermute | solution.py:68
  67.8 37.0 %collective-permute-start.11 = (bf16[512,512]{1,0:T(8,128)(2,1)S(1)}, bf16[512,512]{1,0:T(8,128)(2,1)S(1)}, u32[]{:S(2)}, u32[]{:S(2)}) collective-permute-start(bf16[512,512]{1,0:T(8,128)(2,1)S(1)} %bitcast.80), channel_id=1, source_target_pairs={{13,0},{4,1},{15,2},{6,3},{1,4},{8,5},{3,6},{10,7},{5,8},{12,9},{7... | collective-permute-start | bytes 1572872 | tf_op jit(solution)/shard_map/ppermute | solution.py:68
  67.8 37.0 %collective-permute-start.12 = (bf16[512,512]{1,0:T(8,128)(2,1)S(1)}, bf16[512,512]{1,0:T(8,128)(2,1)S(1)}, u32[]{:S(2)}, u32[]{:S(2)}) collective-permute-start(bf16[512,512]{1,0:T(8,128)(2,1)S(1)} %bitcast.81), channel_id=1, source_target_pairs={{12,0},{5,1},{14,2},{7,3},{0,4},{9,5},{2,6},{11,7},{4,8},{13,9},{6... | collective-permute-start | bytes 1572872 | tf_op jit(solution)/shard_map/ppermute | solution.py:68
  72.2 49.3 %collective-permute-start.13 = (bf16[512,512]{1,0:T(8,128)(2,1)S(1)}, bf16[512,512]{1,0:T(8,128)(2,1)S(1)}, u32[]{:S(2)}, u32[]{:S(2)}) collective-permute-start(bf16[512,512]{1,0:T(8,128)(2,1)S(1)} %bitcast.82), channel_id=1, source_target_pairs={{0,1},{1,0},{2,3},{3,2},{4,5},{5,4},{6,7},{7,6},{8,9},{9,8},{10,11... | collective-permute-start | bytes 1572872 | tf_op jit(solution)/shard_map/ppermute | solution.py:69
  88.7 111.7 %collective-permute-start.14 = (bf16[512,512]{1,0:T(8,128)(2,1)}, bf16[512,512]{1,0:T(8,128)(2,1)S(1)}, u32[]{:S(2)}, u32[]{:S(2)}) collective-permute-start(bf16[512,512]{1,0:T(8,128)(2,1)} %collective-permute-done.9), channel_id=1, source_target_pairs={{0,1},{1,0},{2,3},{3,2},{4,5},{5,4},{6,7},{7,6},{8,9},{9,8},{10,11... | collective-permute-start | bytes 1572872 | tf_op jit(solution)/shard_map/ppermute | solution.py:70
  104.9 95.6 %collective-permute-start.15 = (bf16[512,512]{1,0:T(8,128)(2,1)S(1)}, bf16[512,512]{1,0:T(8,128)(2,1)S(1)}, u32[]{:S(2)}, u32[]{:S(2)}) collective-permute-start(bf16[512,512]{1,0:T(8,128)(2,1)S(1)} %collective-permute-done.10), channel_id=1, source_target_pairs={{0,1},{1,0},{2,3},{3,2},{4,5},{5,4},{6,7},{7,6},{8,9},{9,8},{10,11... | collective-permute-start | bytes 1572872 | tf_op jit(solution)/shard_map/ppermute | solution.py:70
  104.9 96.5 %collective-permute-start.16 = (bf16[512,512]{1,0:T(8,128)(2,1)S(1)}, bf16[512,512]{1,0:T(8,128)(2,1)S(1)}, u32[]{:S(2)}, u32[]{:S(2)}) collective-permute-start(bf16[512,512]{1,0:T(8,128)(2,1)S(1)} %collective-permute-done.11), channel_id=1, source_target_pairs={{0,1},{1,0},{2,3},{3,2},{4,5},{5,4},{6,7},{7,6},{8,9},{9,8},{10,11... | collective-permute-start | bytes 1572872 | tf_op jit(solution)/shard_map/ppermute | solution.py:70
  120.2 87.5 %slice-start.1 = ((s8[4718592]{0:T(1024)(128)(4,1)}), s8[4194304]{0:T(1024)(128)(4,1)S(1)}, s32[]{:S(2)}) async-start(s8[4718592]{0:T(1024)(128)(4,1)} %bitcast.69), calls=%async_computation.1 | async-start | bytes 8388608
  121.5 92.1 %collective-permute-start.18 = (bf16[512,512]{1,0:T(8,128)(2,1)S(1)}, bf16[512,512]{1,0:T(8,128)(2,1)S(1)}, u32[]{:S(2)}, u32[]{:S(2)}) collective-permute-start(bf16[512,512]{1,0:T(8,128)(2,1)S(1)} %bitcast.85), channel_id=1, source_target_pairs={{15,0},{2,1},{1,2},{4,3},{3,4},{6,5},{5,6},{8,7},{7,8},{10,9},{9,1... | collective-permute-start | bytes 1572872 | tf_op jit(solution)/shard_map/ppermute | solution.py:68
  200.3 1.0 copy-start.6
  200.3 58.7 %collective-permute-start.19 = (bf16[512,512]{1,0:T(8,128)(2,1)S(1)}, bf16[512,512]{1,0:T(8,128)(2,1)S(1)}, u32[]{:S(2)}, u32[]{:S(2)}) collective-permute-start(bf16[512,512]{1,0:T(8,128)(2,1)S(1)} %bitcast.86), channel_id=1, source_target_pairs={{14,0},{3,1},{0,2},{5,3},{2,4},{7,5},{4,6},{9,7},{6,8},{11,9},{8,1... | collective-permute-start | bytes 1572872 | tf_op jit(solution)/shard_map/ppermute | solution.py:68
  200.4 58.8 %collective-permute-start.20 = (bf16[512,512]{1,0:T(8,128)(2,1)S(1)}, bf16[512,512]{1,0:T(8,128)(2,1)S(1)}, u32[]{:S(2)}, u32[]{:S(2)}) collective-permute-start(bf16[512,512]{1,0:T(8,128)(2,1)S(1)} %bitcast.87), channel_id=1, source_target_pairs={{13,0},{4,1},{15,2},{6,3},{1,4},{8,5},{3,6},{10,7},{5,8},{12,9},{7... | collective-permute-start | bytes 1572872 | tf_op jit(solution)/shard_map/ppermute | solution.py:68
  200.5 59.1 %collective-permute-start.21 = (bf16[512,512]{1,0:T(8,128)(2,1)S(1)}, bf16[512,512]{1,0:T(8,128)(2,1)S(1)}, u32[]{:S(2)}, u32[]{:S(2)}) collective-permute-start(bf16[512,512]{1,0:T(8,128)(2,1)S(1)} %bitcast.88), channel_id=1, source_target_pairs={{12,0},{5,1},{14,2},{7,3},{0,4},{9,5},{2,6},{11,7},{4,8},{13,9},{6... | collective-permute-start | bytes 1572872 | tf_op jit(solution)/shard_map/ppermute | solution.py:68
  210.4 149.6 %copy-start.3 = (f32[512,512]{0,1:T(8,128)}, f32[512,512]{0,1:T(8,128)S(1)}, u32[]{:S(2)}) copy-start(f32[512,512]{0,1:T(8,128)S(1)} %fusion.17) | copy-start | bytes 3145732
  210.4 140.3 %collective-permute-start.17 = (f32[512,512]{0,1:T(8,128)S(1)}, f32[512,512]{0,1:T(8,128)S(1)}, u32[]{:S(2)}, u32[]{:S(2)}) collective-permute-start(f32[512,512]{0,1:T(8,128)S(1)} %fusion.17), channel_id=1, source_target_pairs={{0,0},{1,16},{2,32},{3,48},{4,64},{5,80},{6,96},{7,112},{8,128},{9... | collective-permute-start | bytes 3145736 | tf_op jit(solution)/shard_map/ppermute | solution.py:78
  213.6 47.0 %collective-permute-start.22 = (bf16[512,512]{1,0:T(8,128)(2,1)S(1)}, bf16[512,512]{1,0:T(8,128)(2,1)S(1)}, u32[]{:S(2)}, u32[]{:S(2)}) collective-permute-start(bf16[512,512]{1,0:T(8,128)(2,1)S(1)} %bitcast.89), channel_id=1, source_target_pairs={{0,1},{1,0},{2,3},{3,2},{4,5},{5,4},{6,7},{7,6},{8,9},{9,8},{10,11... | collective-permute-start | bytes 1572872 | tf_op jit(solution)/shard_map/ppermute | solution.py:69
  259.0 2.3 collective-permute-start.23
  259.1 2.9 collective-permute-start.24
  259.5 3.3 collective-permute-start.25
  350.7 2.5 copy-start.7
  354.7 6.4 %copy-start.9 = (s32[3]{0:T(128)S(1)}, s32[3]{0:T(128)}, u32[]{:S(2)}) copy-start(s32[3]{0:T(128)} %param.5) | copy-start | bytes 40
  356.4 7.9 %copy-start.2 = (bf16[64,8,2,256]{3,1,2,0:T(8,128)(2,1)S(1)}, bf16[64,8,2,256]{3,1,2,0:T(8,128)(2,1)}, u32[]{:S(2)}) copy-start(bf16[64,8,2,256]{3,1,2,0:T(8,128)(2,1)} %copy-done.1) | copy-start | bytes 1572868
  356.4 45.9 %collective-permute-start.26 = (f32[512,512]{0,1:T(8,128)}, f32[512,512]{0,1:T(8,128)}, u32[]{:S(2)}, u32[]{:S(2)}) collective-permute-start(f32[512,512]{0,1:T(8,128)} %fusion.19), channel_id=1, source_target_pairs={{0,0},{1,16},{2,32},{3,48},{4,64},{5,80},{6,96},{7,112},{8,128},{9... | collective-permute-start | bytes 3145736 | tf_op jit(solution)/shard_map/ppermute | solution.py:78
  367.4 37.0 %copy-start.4 = (f32[64,8,2,256]{3,1,2,0:T(8,128)S(1)}, f32[64,8,2,256]{3,1,2,0:T(8,128)}, u32[]{:S(2)}) copy-start(f32[64,8,2,256]{3,1,2,0:T(8,128)} %copy.75) | copy-start | bytes 3145732
  369.0 35.4 %copy-start.5 = (f32[1,512,512]{2,1,0:T(8,128)S(1)}, f32[1,512,512]{2,1,0:T(8,128)}, u32[]{:S(2)}) copy-start(f32[1,512,512]{2,1,0:T(8,128)} %fusion.20) | copy-start | bytes 3145732

commit v9 on v4

--- a/solution.py
+++ b/solution.py
@@ -61,14 +61,20 @@
     outs = []
     products = []
     mirrors = []
+    def tile_occ(offset):
+        src_col = (col_at + offset) % col_count
+        return lax.dynamic_slice(p1_occupancy, (row_at * row_blocks, src_col * col_blocks), (row_blocks, col_blocks))
+
+    occs = [tile_occ(offset) for offset in offsets]
     for d in range(p1_tiles.shape[0]):
-        own = p1_local[d]
+        own = p1_tiles[d]
         if d >= 1:
             own = lax.optimization_barrier((own, products[d - 1]))[0]
         fetched = [lax.ppermute(own, "col", fp) for fp in fetch_pairs]
         partner_own = lax.ppermute(own, "col", swap)
         partner_fetched = [lax.ppermute(fetched[j], "col", swap) for j in range(col_span - 1)]
         tiles = [own] + fetched + [partner_own] + partner_fetched
+        tiles = [mask_blocks(tile, occ) for tile, occ in zip(tiles, occs)]
         if d >= 1:
             tiles, mirrors[d - 1] = lax.optimization_barrier((tiles, mirrors[d - 1]))
         summed = jnp.zeros((row_height, col_width), jnp.float32)
@@ -77,9 +83,9 @@
         products.append(summed)
         mirrored = lax.ppermute(summed, ("row", "col"), pairs)
         mirrors.append(mirrored)
-        mirrored = mirrored.T
-        bracket = summed + mirrored
-        chosen = jnp.where(squared[d], bracket, 2.0 * own.astype(jnp.float32) - bracket)
+        ahead = jnp.where(squared[d], summed, 2.0 * p1_local[d].astype(jnp.float32) - summed)
+        sgn = jnp.where(squared[d], 1.0, -1.0).astype(jnp.float32)
+        chosen = ahead + sgn * mirrored.T
         outs.append(chosen)
     chosen = jnp.stack(outs)
     return mask_blocks(chosen, own_occ).astype(jnp.bfloat16)

time: 411 us -> 411 us (level)
  waiting for transfers between devices: 287 us -> 272 us
  local copies, waits for them, and re-layouts: 26.9 us -> 40.1 us
  other arithmetic: 19.5 us -> 24.7 us
    ppermute x12, waiting for transfers between devices: 89.3 us -> 74.2 us  [body(): fetched = [lax.ppermute(own, 'col', fp) for fp in fetch_pairs]]
    mul x3 -> x21, other arithmetic: 6.57 us -> 13.8 us  [mask_blocks(): return (shaped * weight).reshape(values.shape)]
    unnamed x33 -> x74, local copies, waits for them, and re-layouts: 5.9 us -> 11.2 us
    mul x2 -> x12, local copies, waits for them, and re-layouts: 2.83 us -> 6.99 us  [mask_blocks(): return (shaped * weight).reshape(values.shape)]
  transfers between devices with their start and end apart: 27 -> 27, of which waited for: 11 -> 11; matrix products, arithmetic and copies ran while one was open for 10% -> 16% of each run, Pallas kernels for 0% -> 0%
where the time goes in v9:
time: 411 us; the launch traced here: 406 us
  waiting for transfers between devices  272 us (66%)
  starting transfers between devices  43 us (10%)
  local copies, waits for them, and re-layouts  40.1 us (10%)
  other arithmetic  24.7 us (6%)
  matrix products  23.3 us (6%)
    ppermute x3, waiting for transfers between devices, body(): mirrored = lax.ppermute(summed, ('row', 'col'), pairs)  198 us
    ppermute x12, waiting for transfers between devices, body(): fetched = [lax.ppermute(own, 'col', fp) for fp in fetch_pairs]  74.2 us
    ppermute x12, starting transfers between devices, body(): fetched = [lax.ppermute(own, 'col', fp) for fp in fetch_pairs]  25.5 us
    dot_general x27, matrix products, body(): summed = summed + jnp.dot(tile, factor, preferred_element_type=jnp.float32)  23.3 us
    mul x21, other arithmetic, mask_blocks(): return (shaped * weight).reshape(values.shape)  13.8 us
    unnamed x74, local copies, waits for them, and re-layouts  11.2 us
    reshape x2, local copies, waits for them, and re-layouts, mask_blocks(): shaped = values.reshape(leading + (row_blocks, BLK, col_blocks, BLK))  9.58 us
  transfers between devices with their start and end apart: 27, of which 11 were waited for; matrix products, arithmetic and copies ran while one was open for 16% of the time, Pallas kernels for 0%

profile of v9, /device:TPU:218, one launch (start us, length us, event | category | flops | bytes accessed | tf_op | source)
XLA Modules:
  0.0 406.3 jit_solution(12204734116456473469)
XLA Ops:
  0.0 2.6 slice_bitcast_fusion.2
  2.8 1.7 collective-permute-start.4
  4.5 2.6 collective-permute-start.3
  7.1 1.1 collective-permute-start.2
  8.2 4.9 %collective-permute-start.1 = (bf16[512,512]{1,0:T(8,128)(2,1)}, bf16[512,512]{1,0:T(8,128)(2,1)}, u32[]{:S(2)}, u32[]{:S(2)}) collective-permute-start(bf16[512,512]{1,0:T(8,128)(2,1)} %get-tuple-element.48), channel_id=1, source_target_pairs={{14,0},{3,1},{0,2},{5,3},{2,4},{7,5},{4,6},{9,7},{6,8},{11,9},{8,1... | collective-permute-start | bytes 1572872 | tf_op jit(solution)/shard_map/ppermute | solution.py:73
  13.1 1.1 dynamic-slice_convert_fusion.9
  14.6 1.1 mul.398
  16.0 7.7 %reshape.135 = bf16[18,256,2,256]{3,2,1,0:T(2,128)(2,1)} reshape(bf16[4608,512]{1,0:T(8,128)(2,1)} %param.8) | data formatting | bytes 9437184 | tf_op jit(solution)/shard_map/reshape | solution.py:13
  23.7 1.6 slice_multiply_fusion
  25.7 0.9 copy.52
  26.6 2.5 mul.402
  29.1 1.0 copy.53
  30.1 1.2 slice-done.5
  31.3 3.6 mul.409
  35.2 0.9 copy.57
  36.5 0.9 copy.56
  37.7 0.9 copy.55
  38.9 0.9 copy.54
  40.2 0.9 copy.60
  41.5 0.9 copy.59
  42.8 1.6 fusion.24
  44.5 2.1 collective-permute-done.1
  47.3 1.8 fusion.35
  49.1 1.7 fusion.31
  50.9 1.5 convolution_add_fusion.4
  52.4 1.5 fusion.33
  54.0 1.6 fusion.15
  56.5 1.5 fusion.12
  58.0 5.3 %collective-permute-start.10 = (bf16[512,512]{1,0:T(8,128)(2,1)}, bf16[512,512]{1,0:T(8,128)(2,1)}, u32[]{:S(2)}, u32[]{:S(2)}) collective-permute-start(bf16[512,512]{1,0:T(8,128)(2,1)} %get-tuple-element.25), channel_id=1, source_target_pairs={{14,0},{3,1},{0,2},{5,3},{2,4},{7,5},{4,6},{9,7},{6,8},{11,9},{8,1... | collective-permute-start | bytes 1572872 | tf_op jit(solution)/shard_map/ppermute | solution.py:73
  63.2 4.0 collective-permute-start.12
  67.2 2.1 collective-permute-start.8
  69.3 1.9 reshape.136
  71.1 1.1 copy.62
  72.3 1.6 copy_multiply_fusion
  73.9 4.8 %collective-permute-done.9 = bf16[512,512]{1,0:T(8,128)(2,1)} collective-permute-done((bf16[512,512]{1,0:T(8,128)(2,1)}, bf16[512,512]{1,0:T(8,128)(2,1)}, u32[]{:S(2)}, u32[]{:S(2)}) %collective-permute-start.9) | collective-permute-done | bytes 524320 | tf_op jit(solution)/shard_map/ppermute | solution.py:73
  78.8 6.9 %collective-permute-done.10 = bf16[512,512]{1,0:T(8,128)(2,1)} collective-permute-done((bf16[512,512]{1,0:T(8,128)(2,1)}, bf16[512,512]{1,0:T(8,128)(2,1)}, u32[]{:S(2)}, u32[]{:S(2)}) %collective-permute-start.10) | collective-permute-done | bytes 524320 | tf_op jit(solution)/shard_map/ppermute | solution.py:73
  85.6 13.0 %collective-permute-done.11 = bf16[512,512]{1,0:T(8,128)(2,1)S(1)} collective-permute-done((bf16[512,512]{1,0:T(8,128)(2,1)}, bf16[512,512]{1,0:T(8,128)(2,1)S(1)}, u32[]{:S(2)}, u32[]{:S(2)}) %collective-permute-start.11) | collective-permute-done | bytes 524320 | tf_op jit(solution)/shard_map/ppermute | solution.py:73
  98.6 2.5 collective-permute-done.12
  101.3 1.2 convert_multiply_fusion.2
  102.5 0.8 copy.43
  104.0 1.3 mul.460
  105.5 1.2 mul.462
  106.8 1.2 mul.461
  108.0 1.2 mul.464
  109.9 69.1 %collective-permute-done.8 = f32[512,512]{1,0:T(8,128)} collective-permute-done((f32[512,512]{1,0:T(8,128)}, f32[512,512]{1,0:T(8,128)}, u32[]{:S(2)}, u32[]{:S(2)}) %collective-permute-start.8) | collective-permute-done | bytes 1048608 | tf_op jit(solution)/shard_map/ppermute | solution.py:84
  182.5 1.4 subtract_select_fusion.1
  184.3 7.2 %collective-permute-start.21 = (bf16[512,512]{1,0:T(8,128)(2,1)S(1)}, bf16[512,512]{1,0:T(8,128)(2,1)S(1)}, u32[]{:S(2)}, u32[]{:S(2)}) collective-permute-start(bf16[512,512]{1,0:T(8,128)(2,1)S(1)} %copy-done.18), channel_id=1, source_target_pairs={{12,0},{5,1},{14,2},{7,3},{0,4},{9,5},{2,6},{11,7},{4,8},{13,9},{6... | collective-permute-start | bytes 1572872 | tf_op jit(solution)/shard_map/ppermute | solution.py:73
  191.5 3.0 collective-permute-start.17
  194.5 10.9 %collective-permute-done.18 = bf16[512,512]{1,0:T(8,128)(2,1)S(1)} collective-permute-done((bf16[512,512]{1,0:T(8,128)(2,1)S(1)}, bf16[512,512]{1,0:T(8,128)(2,1)S(1)}, u32[]{:S(2)}, u32[]{:S(2)}) %collective-permute-start.18) | collective-permute-done | bytes 524320 | tf_op jit(solution)/shard_map/ppermute | solution.py:73
  206.0 33.4 %collective-permute-done.20 = bf16[512,512]{1,0:T(8,128)(2,1)S(1)} collective-permute-done((bf16[512,512]{1,0:T(8,128)(2,1)S(1)}, bf16[512,512]{1,0:T(8,128)(2,1)S(1)}, u32[]{:S(2)}, u32[]{:S(2)}) %collective-permute-start.20) | collective-permute-done | bytes 524320 | tf_op jit(solution)/shard_map/ppermute | solution.py:73
  239.4 6.9 %collective-permute-start.25 = (bf16[512,512]{1,0:T(8,128)(2,1)S(1)}, bf16[512,512]{1,0:T(8,128)(2,1)S(1)}, u32[]{:S(2)}, u32[]{:S(2)}) collective-permute-start(bf16[512,512]{1,0:T(8,128)(2,1)S(1)} %collective-permute-done.20), channel_id=1, source_target_pairs={{0,1},{1,0},{2,3},{3,2},{4,5},{5,4},{6,7},{7,6},{8,9},{9,8},{10,11... | collective-permute-start | bytes 1572872 | tf_op jit(solution)/shard_map/ppermute | solution.py:75
  248.5 95.7 %collective-permute-done.17 = f32[512,512]{1,0:T(8,128)S(1)} collective-permute-done((f32[512,512]{1,0:T(8,128)S(1)}, f32[512,512]{1,0:T(8,128)S(1)}, u32[]{:S(2)}, u32[]{:S(2)}) %collective-permute-start.17) | collective-permute-done | bytes 1048608 | tf_op jit(solution)/shard_map/ppermute | solution.py:84
  347.8 2.7 subtract_select_fusion
  350.5 2.9 collective-permute-start.26
  354.6 1.6 copy.49
  357.3 1.1 copy.65
  358.4 2.6 copy.42
  361.0 1.3 copy.44
  362.3 3.7 fusion.21
  366.0 1.2 fusion.23
  367.5 33.3 %collective-permute-done.26 = f32[512,512]{1,0:T(8,128)} collective-permute-done((f32[512,512]{1,0:T(8,128)}, f32[512,512]{1,0:T(8,128)}, u32[]{:S(2)}, u32[]{:S(2)}) %collective-permute-start.26) | collective-permute-done | bytes 1048608 | tf_op jit(solution)/shard_map/ppermute | solution.py:84
  400.9 1.4 fusion.22
  402.3 2.1 fusion
  404.5 1.6 copy.48
  (149 shorter events, 17.9 us)
Async XLA Ops:
  0.0 15.7 %copy-start.21 = (s32[32,32]{1,0:T(8,128)S(1)}, s32[32,32]{1,0:T(8,128)}, u32[]{:S(2)}) copy-start(s32[32,32]{1,0:T(8,128)} %param.6) | copy-start | bytes 12292
  2.6 44.1 %collective-permute-start = (bf16[512,512]{1,0:T(8,128)(2,1)}, bf16[512,512]{1,0:T(8,128)(2,1)}, u32[]{:S(2)}, u32[]{:S(2)}) collective-permute-start(bf16[512,512]{1,0:T(8,128)(2,1)} %get-tuple-element.48), channel_id=1, source_target_pairs={{15,0},{2,1},{1,2},{4,3},{3,4},{6,5},{5,6},{8,7},{7,8},{10,9},{9,1... | collective-permute-start | bytes 1572872 | tf_op jit(solution)/shard_map/ppermute | solution.py:73
  2.8 46.4 %collective-permute-start.4 = (bf16[512,512]{1,0:T(8,128)(2,1)}, bf16[512,512]{1,0:T(8,128)(2,1)}, u32[]{:S(2)}, u32[]{:S(2)}) collective-permute-start(bf16[512,512]{1,0:T(8,128)(2,1)} %get-tuple-element.48), channel_id=1, source_target_pairs={{0,1},{1,0},{2,3},{3,2},{4,5},{5,4},{6,7},{7,6},{8,9},{9,8},{10,11... | collective-permute-start | bytes 1572872 | tf_op jit(solution)/shard_map/ppermute | solution.py:74
  4.5 47.9 %collective-permute-start.3 = (bf16[512,512]{1,0:T(8,128)(2,1)}, bf16[512,512]{1,0:T(8,128)(2,1)}, u32[]{:S(2)}, u32[]{:S(2)}) collective-permute-start(bf16[512,512]{1,0:T(8,128)(2,1)} %get-tuple-element.48), channel_id=1, source_target_pairs={{12,0},{5,1},{14,2},{7,3},{0,4},{9,5},{2,6},{11,7},{4,8},{13,9},{6... | collective-permute-start | bytes 1572872 | tf_op jit(solution)/shard_map/ppermute | solution.py:73
  7.1 37.4 %collective-permute-start.2 = (bf16[512,512]{1,0:T(8,128)(2,1)}, bf16[512,512]{1,0:T(8,128)(2,1)}, u32[]{:S(2)}, u32[]{:S(2)}) collective-permute-start(bf16[512,512]{1,0:T(8,128)(2,1)} %get-tuple-element.48), channel_id=1, source_target_pairs={{13,0},{4,1},{15,2},{6,3},{1,4},{8,5},{3,6},{10,7},{5,8},{12,9},{7... | collective-permute-start | bytes 1572872 | tf_op jit(solution)/shard_map/ppermute | solution.py:73
  8.2 38.5 %collective-permute-start.1 = (bf16[512,512]{1,0:T(8,128)(2,1)}, bf16[512,512]{1,0:T(8,128)(2,1)}, u32[]{:S(2)}, u32[]{:S(2)}) collective-permute-start(bf16[512,512]{1,0:T(8,128)(2,1)} %get-tuple-element.48), channel_id=1, source_target_pairs={{14,0},{3,1},{0,2},{5,3},{2,4},{7,5},{4,6},{9,7},{6,8},{11,9},{8,1... | collective-permute-start | bytes 1572872 | tf_op jit(solution)/shard_map/ppermute | solution.py:73
  14.6 9.1 %copy-start.14 = (bf16[2,256,2,256]{3,2,1,0:T(2,128)(2,1)}, bf16[2,256,2,256]{3,2,1,0:T(2,128)(2,1)S(1)}, u32[]{:S(2)}) copy-start(bf16[2,256,2,256]{3,2,1,0:T(2,128)(2,1)S(1)} %mul.397) | copy-start | bytes 1572868
  26.6 3.5 slice-start.4
  29.1 2.2 slice-start.5
  36.1 6.7 %copy-start = (bf16[3,512,512]{2,1,0:T(8,128)(2,1)S(1)}, bf16[3,512,512]{2,1,0:T(8,128)(2,1)}, u32[]{:S(2)}) copy-start(bf16[3,512,512]{2,1,0:T(8,128)(2,1)} %param.9) | copy-start | bytes 4718596
  41.4 9.4 %slice-start = ((s8[4718592]{0:T(1024)(128)(4,1)}), s8[524288]{0:T(1024)(128)(4,1)S(1)}, s32[]{:S(2)}) async-start(s8[4718592]{0:T(1024)(128)(4,1)} %bitcast.98), calls=%async_computation | async-start | bytes 1048576
  42.8 6.4 %copy-start.5 = (bf16[64,8,2,256]{3,1,2,0:T(8,128)(2,1)S(1)}, bf16[64,8,2,256]{3,1,2,0:T(8,128)(2,1)}, u32[]{:S(2)}) copy-start(bf16[64,8,2,256]{3,1,2,0:T(8,128)(2,1)} %copy.57) | copy-start | bytes 1572868
  42.8 8.1 %copy-start.3 = (bf16[64,8,2,256]{3,1,2,0:T(8,128)(2,1)S(1)}, bf16[64,8,2,256]{3,1,2,0:T(8,128)(2,1)}, u32[]{:S(2)}) copy-start(bf16[64,8,2,256]{3,1,2,0:T(8,128)(2,1)} %copy.52) | copy-start | bytes 1572868
  42.8 8.1 %slice-start.1 = ((s8[4718592]{0:T(1024)(128)(4,1)}), s8[4194304]{0:T(1024)(128)(4,1)S(1)}, s32[]{:S(2)}) async-start(s8[4718592]{0:T(1024)(128)(4,1)} %bitcast.98), calls=%async_computation.1 | async-start | bytes 8388608
  44.4 8.0 %copy-start.9 = (bf16[64,8,2,256]{3,1,2,0:T(8,128)(2,1)S(1)}, bf16[64,8,2,256]{3,1,2,0:T(8,128)(2,1)}, u32[]{:S(2)}) copy-start(bf16[64,8,2,256]{3,1,2,0:T(8,128)(2,1)} %copy.56) | copy-start | bytes 1572868
  44.4 11.1 %collective-permute-start.7 = (bf16[512,512]{1,0:T(8,128)(2,1)}, bf16[512,512]{1,0:T(8,128)(2,1)S(1)}, u32[]{:S(2)}, u32[]{:S(2)}) collective-permute-start(bf16[512,512]{1,0:T(8,128)(2,1)} %collective-permute-done.2), channel_id=1, source_target_pairs={{0,1},{1,0},{2,3},{3,2},{4,5},{5,4},{6,7},{7,6},{8,9},{9,8},{10,11... | collective-permute-start | bytes 1572872 | tf_op jit(solution)/shard_map/ppermute | solution.py:75
  46.7 9.4 %collective-permute-start.6 = (bf16[512,512]{1,0:T(8,128)(2,1)}, bf16[512,512]{1,0:T(8,128)(2,1)S(1)}, u32[]{:S(2)}, u32[]{:S(2)}) collective-permute-start(bf16[512,512]{1,0:T(8,128)(2,1)} %collective-permute-done.1), channel_id=1, source_target_pairs={{0,1},{1,0},{2,3},{3,2},{4,5},{5,4},{6,7},{7,6},{8,9},{9,8},{10,11... | collective-permute-start | bytes 1572872 | tf_op jit(solution)/shard_map/ppermute | solution.py:75
  46.7 9.8 %collective-permute-start.5 = (bf16[512,512]{1,0:T(8,128)(2,1)}, bf16[512,512]{1,0:T(8,128)(2,1)S(1)}, u32[]{:S(2)}, u32[]{:S(2)}) collective-permute-start(bf16[512,512]{1,0:T(8,128)(2,1)} %collective-permute-done), channel_id=1, source_target_pairs={{0,1},{1,0},{2,3},{3,2},{4,5},{5,4},{6,7},{7,6},{8,9},{9,8},{10,11... | collective-permute-start | bytes 1572872 | tf_op jit(solution)/shard_map/ppermute | solution.py:75
  49.1 4.8 %copy-start.12 = (bf16[64,8,2,256]{3,1,2,0:T(8,128)(2,1)S(1)}, bf16[64,8,2,256]{3,1,2,0:T(8,128)(2,1)}, u32[]{:S(2)}) copy-start(bf16[64,8,2,256]{3,1,2,0:T(8,128)(2,1)} %copy.54) | copy-start | bytes 1572868
  52.4 3.2 copy-start.1
  53.9 2.1 copy-start.7
  58.0 20.8 %collective-permute-start.9 = (bf16[512,512]{1,0:T(8,128)(2,1)}, bf16[512,512]{1,0:T(8,128)(2,1)}, u32[]{:S(2)}, u32[]{:S(2)}) collective-permute-start(bf16[512,512]{1,0:T(8,128)(2,1)} %get-tuple-element.25), channel_id=1, source_target_pairs={{15,0},{2,1},{1,2},{4,3},{3,4},{6,5},{5,6},{8,7},{7,8},{10,9},{9,1... | collective-permute-start | bytes 1572872 | tf_op jit(solution)/shard_map/ppermute | solution.py:73
  58.0 27.7 %collective-permute-start.10 = (bf16[512,512]{1,0:T(8,128)(2,1)}, bf16[512,512]{1,0:T(8,128)(2,1)}, u32[]{:S(2)}, u32[]{:S(2)}) collective-permute-start(bf16[512,512]{1,0:T(8,128)(2,1)} %get-tuple-element.25), channel_id=1, source_target_pairs={{14,0},{3,1},{0,2},{5,3},{2,4},{7,5},{4,6},{9,7},{6,8},{11,9},{8,1... | collective-permute-start | bytes 1572872 | tf_op jit(solution)/shard_map/ppermute | solution.py:73
  63.2 35.4 %collective-permute-start.11 = (bf16[512,512]{1,0:T(8,128)(2,1)}, bf16[512,512]{1,0:T(8,128)(2,1)S(1)}, u32[]{:S(2)}, u32[]{:S(2)}) collective-permute-start(bf16[512,512]{1,0:T(8,128)(2,1)} %get-tuple-element.25), channel_id=1, source_target_pairs={{13,0},{4,1},{15,2},{6,3},{1,4},{8,5},{3,6},{10,7},{5,8},{12,9},{7... | collective-permute-start | bytes 1572872 | tf_op jit(solution)/shard_map/ppermute | solution.py:73
  63.2 37.9 %collective-permute-start.12 = (bf16[512,512]{1,0:T(8,128)(2,1)}, bf16[512,512]{1,0:T(8,128)(2,1)}, u32[]{:S(2)}, u32[]{:S(2)}) collective-permute-start(bf16[512,512]{1,0:T(8,128)(2,1)} %get-tuple-element.25), channel_id=1, source_target_pairs={{12,0},{5,1},{14,2},{7,3},{0,4},{9,5},{2,6},{11,7},{4,8},{13,9},{6... | collective-permute-start | bytes 1572872 | tf_op jit(solution)/shard_map/ppermute | solution.py:73
  67.2 111.8 %collective-permute-start.8 = (f32[512,512]{1,0:T(8,128)}, f32[512,512]{1,0:T(8,128)}, u32[]{:S(2)}, u32[]{:S(2)}) collective-permute-start(f32[512,512]{1,0:T(8,128)} %fusion.12), channel_id=1, source_target_pairs={{0,0},{1,16},{2,32},{3,48},{4,64},{5,80},{6,96},{7,112},{8,128},{9... | collective-permute-start | bytes 3145736 | tf_op jit(solution)/shard_map/ppermute | solution.py:84
  73.9 29.5 %copy-start.22 = (s32[3]{0:T(128)S(1)}, s32[3]{0:T(128)}, u32[]{:S(2)}) copy-start(s32[3]{0:T(128)} %param.5) | copy-start | bytes 40
  73.9 31.5 %copy-start.11 = (bf16[64,8,2,256]{3,1,2,0:T(8,128)(2,1)S(1)}, bf16[64,8,2,256]{3,1,2,0:T(8,128)(2,1)}, u32[]{:S(2)}) copy-start(bf16[64,8,2,256]{3,1,2,0:T(8,128)(2,1)} %copy.55) | copy-start | bytes 1572868
  78.7 30.5 %collective-permute-start.13 = (bf16[512,512]{1,0:T(8,128)(2,1)}, bf16[512,512]{1,0:T(8,128)(2,1)S(1)}, u32[]{:S(2)}, u32[]{:S(2)}) collective-permute-start(bf16[512,512]{1,0:T(8,128)(2,1)} %get-tuple-element.25), channel_id=1, source_target_pairs={{0,1},{1,0},{2,3},{3,2},{4,5},{5,4},{6,7},{7,6},{8,9},{9,8},{10,11... | collective-permute-start | bytes 1572872 | tf_op jit(solution)/shard_map/ppermute | solution.py:74
  85.6 23.8 %collective-permute-start.14 = (bf16[512,512]{1,0:T(8,128)(2,1)}, bf16[512,512]{1,0:T(8,128)(2,1)S(1)}, u32[]{:S(2)}, u32[]{:S(2)}) collective-permute-start(bf16[512,512]{1,0:T(8,128)(2,1)} %collective-permute-done.9), channel_id=1, source_target_pairs={{0,1},{1,0},{2,3},{3,2},{4,5},{5,4},{6,7},{7,6},{8,9},{9,8},{10,11... | collective-permute-start | bytes 1572872 | tf_op jit(solution)/shard_map/ppermute | solution.py:75
  98.6 10.9 %collective-permute-start.15 = (bf16[512,512]{1,0:T(8,128)(2,1)}, bf16[512,512]{1,0:T(8,128)(2,1)S(1)}, u32[]{:S(2)}, u32[]{:S(2)}) collective-permute-start(bf16[512,512]{1,0:T(8,128)(2,1)} %collective-permute-done.10), channel_id=1, source_target_pairs={{0,1},{1,0},{2,3},{3,2},{4,5},{5,4},{6,7},{7,6},{8,9},{9,8},{10,11... | collective-permute-start | bytes 1572872 | tf_op jit(solution)/shard_map/ppermute | solution.py:75
  101.1 8.6 %collective-permute-start.16 = (bf16[512,512]{1,0:T(8,128)(2,1)S(1)}, bf16[512,512]{1,0:T(8,128)(2,1)S(1)}, u32[]{:S(2)}, u32[]{:S(2)}) collective-permute-start(bf16[512,512]{1,0:T(8,128)(2,1)S(1)} %collective-permute-done.11), channel_id=1, source_target_pairs={{0,1},{1,0},{2,3},{3,2},{4,5},{5,4},{6,7},{7,6},{8,9},{9,8},{10,11... | collective-permute-start | bytes 1572872 | tf_op jit(solution)/shard_map/ppermute | solution.py:75
  102.5 3.0 copy-start.13
  102.5 4.3 %copy-start.4 = (bf16[64,8,2,256]{3,1,2,0:T(8,128)(2,1)S(1)}, bf16[64,8,2,256]{3,1,2,0:T(8,128)(2,1)}, u32[]{:S(2)}) copy-start(bf16[64,8,2,256]{3,1,2,0:T(8,128)(2,1)} %copy.52) | copy-start | bytes 1572868
  103.3 4.6 %copy-start.10 = (bf16[64,8,2,256]{3,1,2,0:T(8,128)(2,1)S(1)}, bf16[64,8,2,256]{3,1,2,0:T(8,128)(2,1)}, u32[]{:S(2)}) copy-start(bf16[64,8,2,256]{3,1,2,0:T(8,128)(2,1)} %copy.56) | copy-start | bytes 1572868
  103.3 5.9 %copy-start.6 = (bf16[64,8,2,256]{3,1,2,0:T(8,128)(2,1)S(1)}, bf16[64,8,2,256]{3,1,2,0:T(8,128)(2,1)}, u32[]{:S(2)}) copy-start(bf16[64,8,2,256]{3,1,2,0:T(8,128)(2,1)} %copy.57) | copy-start | bytes 1572868
  104.0 75.0 %slice-start.2 = ((s8[4718592]{0:T(1024)(128)(4,1)}), s8[4194304]{0:T(1024)(128)(4,1)S(1)}, s32[]{:S(2)}) async-start(s8[4718592]{0:T(1024)(128)(4,1)} %bitcast.100), calls=%async_computation.2 | async-start | bytes 8388608
  105.4 4.2 %copy-start.8 = (bf16[64,8,2,256]{3,1,2,0:T(8,128)(2,1)S(1)}, bf16[64,8,2,256]{3,1,2,0:T(8,128)(2,1)}, u32[]{:S(2)}) copy-start(bf16[64,8,2,256]{3,1,2,0:T(8,128)(2,1)} %copy.59) | copy-start | bytes 1572868
  105.5 4.2 %copy-start.2 = (bf16[64,8,2,256]{3,1,2,0:T(8,128)(2,1)S(1)}, bf16[64,8,2,256]{3,1,2,0:T(8,128)(2,1)}, u32[]{:S(2)}) copy-start(bf16[64,8,2,256]{3,1,2,0:T(8,128)(2,1)} %copy.60) | copy-start | bytes 1572868
  108.0 71.0 %slice-start.3 = ((s8[4718592]{0:T(1024)(128)(4,1)}), s8[524288]{0:T(1024)(128)(4,1)S(1)}, s32[]{:S(2)}) async-start(s8[4718592]{0:T(1024)(128)(4,1)} %bitcast.100), calls=%async_computation.3 | async-start | bytes 1048576
  182.5 1.5 copy-start.18
  184.0 21.4 %collective-permute-start.18 = (bf16[512,512]{1,0:T(8,128)(2,1)S(1)}, bf16[512,512]{1,0:T(8,128)(2,1)S(1)}, u32[]{:S(2)}, u32[]{:S(2)}) collective-permute-start(bf16[512,512]{1,0:T(8,128)(2,1)S(1)} %copy-done.18), channel_id=1, source_target_pairs={{15,0},{2,1},{1,2},{4,3},{3,4},{6,5},{5,6},{8,7},{7,8},{10,9},{9,1... | collective-permute-start | bytes 1572872 | tf_op jit(solution)/shard_map/ppermute | solution.py:73
  184.1 21.9 %collective-permute-start.19 = (bf16[512,512]{1,0:T(8,128)(2,1)S(1)}, bf16[512,512]{1,0:T(8,128)(2,1)S(1)}, u32[]{:S(2)}, u32[]{:S(2)}) collective-permute-start(bf16[512,512]{1,0:T(8,128)(2,1)S(1)} %copy-done.18), channel_id=1, source_target_pairs={{14,0},{3,1},{0,2},{5,3},{2,4},{7,5},{4,6},{9,7},{6,8},{11,9},{8,1... | collective-permute-start | bytes 1572872 | tf_op jit(solution)/shard_map/ppermute | solution.py:73
  184.2 55.2 %collective-permute-start.20 = (bf16[512,512]{1,0:T(8,128)(2,1)S(1)}, bf16[512,512]{1,0:T(8,128)(2,1)S(1)}, u32[]{:S(2)}, u32[]{:S(2)}) collective-permute-start(bf16[512,512]{1,0:T(8,128)(2,1)S(1)} %copy-done.18), channel_id=1, source_target_pairs={{13,0},{4,1},{15,2},{6,3},{1,4},{8,5},{3,6},{10,7},{5,8},{12,9},{7... | collective-permute-start | bytes 1572872 | tf_op jit(solution)/shard_map/ppermute | solution.py:73
  184.3 55.1 %collective-permute-start.21 = (bf16[512,512]{1,0:T(8,128)(2,1)S(1)}, bf16[512,512]{1,0:T(8,128)(2,1)S(1)}, u32[]{:S(2)}, u32[]{:S(2)}) collective-permute-start(bf16[512,512]{1,0:T(8,128)(2,1)S(1)} %copy-done.18), channel_id=1, source_target_pairs={{12,0},{5,1},{14,2},{7,3},{0,4},{9,5},{2,6},{11,7},{4,8},{13,9},{6... | collective-permute-start | bytes 1572872 | tf_op jit(solution)/shard_map/ppermute | solution.py:73
  191.5 152.7 %collective-permute-start.17 = (f32[512,512]{1,0:T(8,128)S(1)}, f32[512,512]{1,0:T(8,128)S(1)}, u32[]{:S(2)}, u32[]{:S(2)}) collective-permute-start(f32[512,512]{1,0:T(8,128)S(1)} %get-tuple-element.68), channel_id=1, source_target_pairs={{0,0},{1,16},{2,32},{3,48},{4,64},{5,80},{6,96},{7,112},{8,128},{9... | collective-permute-start | bytes 3145736 | tf_op jit(solution)/shard_map/ppermute | solution.py:84
  205.4 42.5 %collective-permute-start.22 = (bf16[512,512]{1,0:T(8,128)(2,1)S(1)}, bf16[512,512]{1,0:T(8,128)(2,1)S(1)}, u32[]{:S(2)}, u32[]{:S(2)}) collective-permute-start(bf16[512,512]{1,0:T(8,128)(2,1)S(1)} %copy-done.18), channel_id=1, source_target_pairs={{0,1},{1,0},{2,3},{3,2},{4,5},{5,4},{6,7},{7,6},{8,9},{9,8},{10,11... | collective-permute-start | bytes 1572872 | tf_op jit(solution)/shard_map/ppermute | solution.py:74
  206.0 42.1 %collective-permute-start.23 = (bf16[512,512]{1,0:T(8,128)(2,1)S(1)}, bf16[512,512]{1,0:T(8,128)(2,1)S(1)}, u32[]{:S(2)}, u32[]{:S(2)}) collective-permute-start(bf16[512,512]{1,0:T(8,128)(2,1)S(1)} %collective-permute-done.18), channel_id=1, source_target_pairs={{0,1},{1,0},{2,3},{3,2},{4,5},{5,4},{6,7},{7,6},{8,9},{9,8},{10,11... | collective-permute-start | bytes 1572872 | tf_op jit(solution)/shard_map/ppermute | solution.py:75
  239.4 8.8 %collective-permute-start.24 = (bf16[512,512]{1,0:T(8,128)(2,1)S(1)}, bf16[512,512]{1,0:T(8,128)(2,1)S(1)}, u32[]{:S(2)}, u32[]{:S(2)}) collective-permute-start(bf16[512,512]{1,0:T(8,128)(2,1)S(1)} %collective-permute-done.19), channel_id=1, source_target_pairs={{0,1},{1,0},{2,3},{3,2},{4,5},{5,4},{6,7},{7,6},{8,9},{9,8},{10,11... | collective-permute-start | bytes 1572872 | tf_op jit(solution)/shard_map/ppermute | solution.py:75
  239.4 9.0 %collective-permute-start.25 = (bf16[512,512]{1,0:T(8,128)(2,1)S(1)}, bf16[512,512]{1,0:T(8,128)(2,1)S(1)}, u32[]{:S(2)}, u32[]{:S(2)}) collective-permute-start(bf16[512,512]{1,0:T(8,128)(2,1)S(1)} %collective-permute-done.20), channel_id=1, source_target_pairs={{0,1},{1,0},{2,3},{3,2},{4,5},{5,4},{6,7},{7,6},{8,9},{9,8},{10,11... | collective-permute-start | bytes 1572872 | tf_op jit(solution)/shard_map/ppermute | solution.py:75
  344.2 2.2 copy-start.19
  350.5 50.4 %collective-permute-start.26 = (f32[512,512]{1,0:T(8,128)}, f32[512,512]{1,0:T(8,128)}, u32[]{:S(2)}, u32[]{:S(2)}) collective-permute-start(f32[512,512]{1,0:T(8,128)} %get-tuple-element.66), channel_id=1, source_target_pairs={{0,0},{1,16},{2,32},{3,48},{4,64},{5,80},{6,96},{7,112},{8,128},{9... | collective-permute-start | bytes 3145736 | tf_op jit(solution)/shard_map/ppermute | solution.py:84
  361.0 6.2 %copy-start.15 = (f32[512,512]{1,0:T(8,128)S(1)}, f32[512,512]{1,0:T(8,128)}, u32[]{:S(2)}) copy-start(f32[512,512]{1,0:T(8,128)} %get-tuple-element.65) | copy-start | bytes 3145732
  362.3 3.7 copy-start.17
  362.3 3.7 copy-start.20
  366.0 36.3 %copy-start.16 = (f32[1,512,512]{1,2,0:T(8,128)S(1)}, f32[1,512,512]{1,2,0:T(8,128)}, u32[]{:S(2)}) copy-start(f32[1,512,512]{1,2,0:T(8,128)} %fusion.21) | copy-start | bytes 3145732

commit v10 on v4

--- a/solution.py
+++ b/solution.py
@@ -61,19 +61,17 @@
     outs = []
     products = []
     mirrors = []
+    band_cols = (col_at + jnp.arange(-col_span, col_span + 1)) % col_count
     for d in range(p1_tiles.shape[0]):
         own = p1_local[d]
         if d >= 1:
             own = lax.optimization_barrier((own, products[d - 1]))[0]
-        fetched = [lax.ppermute(own, "col", fp) for fp in fetch_pairs]
-        partner_own = lax.ppermute(own, "col", swap)
-        partner_fetched = [lax.ppermute(fetched[j], "col", swap) for j in range(col_span - 1)]
-        tiles = [own] + fetched + [partner_own] + partner_fetched
+        everyone = lax.all_gather(own, "col", axis=0)
         if d >= 1:
-            tiles, mirrors[d - 1] = lax.optimization_barrier((tiles, mirrors[d - 1]))
-        summed = jnp.zeros((row_height, col_width), jnp.float32)
-        for tile, factor in zip(tiles, factors):
-            summed = summed + jnp.dot(tile, factor, preferred_element_type=jnp.float32)
+            everyone, mirrors[d - 1] = lax.optimization_barrier((everyone, mirrors[d - 1]))
+        band = jnp.take(everyone, band_cols, axis=0)
+        band = jnp.transpose(band, (1, 0, 2)).reshape(row_height, -1)
+        summed = jnp.dot(band, strip_local, preferred_element_type=jnp.float32)
         products.append(summed)
         mirrored = lax.ppermute(summed, ("row", "col"), pairs)
         mirrors.append(mirrored)

time: 411 us -> 523 us (1.27)
  waiting for transfers between devices: 287 us -> 386 us
  starting transfers between devices: 46.8 us -> 5.99 us
  local copies, waits for them, and re-layouts: 26.9 us -> 58.7 us
  between operations: 0.96 us -> 13.3 us
  other arithmetic: 19.5 us -> 30.5 us
    ppermute x3, waiting for transfers between devices: 198 us -> 321 us  [body(): mirrored = lax.ppermute(summed, ('row', 'col'), pairs)]
    ppermute x24 -> x0, waiting for transfers between devices: 89.3 us -> none  [the longest x12 89.3 us: body(): fetched = [lax.ppermute(own, 'col', fp) for fp in fetch_pairs]]
    all_gather x0 -> x3, waiting for transfers between devices: none -> 65.2 us  [body(): everyone = lax.all_gather(own, 'col', axis=0)]
    ppermute x24 -> x0, starting transfers between devices: 38.4 us -> none  [the longest x12 28.7 us: body(): fetched = [lax.ppermute(own, 'col', fp) for fp in fetch_pairs]]
    gather x0 -> x3, local copies, waits for them, and re-layouts: none -> 21.1 us  [body(): band = jnp.take(everyone, band_cols, axis=0)]
    transpose x0 -> x3, local copies, waits for them, and re-layouts: none -> 20 us  [body(): band = jnp.transpose(band, (1, 0, 2)).reshape(row_height, -1)]
    transpose x0 -> x3, other arithmetic: none -> 14.9 us  [body(): band = jnp.transpose(band, (1, 0, 2)).reshape(row_height, -1)]
    reshape x2 -> x1, local copies, waits for them, and re-layouts: 10.1 us -> 2.36 us  [mask_blocks(): shaped = values.reshape(leading + (row_blocks, BLK, col_blocks, BLK))]
  transfers between devices with their start and end apart: 27 -> 6, of which waited for: 11 -> 4; matrix products, arithmetic and copies ran while one was open for 10% -> 4% of each run, Pallas kernels for 0% -> 0%
where the time goes in v10:
time: 523 us; the launch traced here: 516 us
  waiting for transfers between devices  386 us (74%)
  local copies, waits for them, and re-layouts  58.7 us (11%)
  other arithmetic  30.5 us (6%)
  matrix products  20.7 us (4%)
  between operations  13.3 us (3%)
  starting transfers between devices  5.99 us (1%)
    ppermute x3, waiting for transfers between devices, body(): mirrored = lax.ppermute(summed, ('row', 'col'), pairs)  321 us
    all_gather x3, waiting for transfers between devices, body(): everyone = lax.all_gather(own, 'col', axis=0)  65.2 us
    gather x3, local copies, waits for them, and re-layouts, body(): band = jnp.take(everyone, band_cols, axis=0)  21.1 us
    dot_general x3, matrix products, body(): summed = jnp.dot(band, strip_local, preferred_element_type=jnp.float32)  20.7 us
    transpose x3, local copies, waits for them, and re-layouts, body(): band = jnp.transpose(band, (1, 0, 2)).reshape(row_height, -1)  20 us
    transpose x3, other arithmetic, body(): band = jnp.transpose(band, (1, 0, 2)).reshape(row_height, -1)  14.9 us
  transfers between devices with their start and end apart: 6, of which 4 were waited for; matrix products, arithmetic and copies ran while one was open for 4% of the time, Pallas kernels for 0%

profile of v10, /device:TPU:218, one launch (start us, length us, event | category | flops | bytes accessed | tf_op | source)
XLA Modules:
  0.0 515.6 jit_solution(3935705716835689231)
XLA Ops:
  6.5 0.0 all-gather.6.cloned.1.call-start
  6.5 2.4 reshape.48
  8.9 0.0 copy-start.4
  8.9 0.8 dynamic-slice_convert_fusion
  9.7 1.4 broadcast_multiply_fusion
  11.1 1.1 fusion.8
  12.2 1.1 slice.25
  13.3 0.0 all-gather.6.cloned.1.call-update
  13.3 0.0 all-gather.8.cloned.1.call-start
  13.4 0.0 copy-done.4
  13.4 0.1 copy.19
  13.5 0.1 fusion.6
  13.6 0.1 copy.22
  13.7 2.5 mul.56
  16.2 1.0 copy.28
  17.2 0.9 copy.30
  18.1 5.9 %mul.58 = bf16[4608,512]{1,0:T(8,128)(2,1)} multiply(bf16[4608,512]{1,0:T(8,128)(2,1)} %param.10, bf16[4608,512]{1,0:T(8,128)(2,1)S(1)} %bitcast.53) | non-fusion elementwise | flops 2359296 | bytes 14155776 | tf_op jit(solution)/shard_map/mul | solution.py:15
  24.0 65.2 %all-gather.6.cloned.1.call-done = bf16[16,512,512]{2,1,0:T(8,128)(2,1)} async-done(((bf16[1,512,512]{2,1,0:T(8,128)(2,1)}), bf16[16,512,512]{2,1,0:T(8,128)(2,1)}) %all-gather.6.cloned.1.call-update) | async-done | bytes 8388624 | tf_op jit(solution)/shard_map/all_gather | solution.py:69
  89.2 7.0 %gather_fusion = bf16[9,512,512]{2,1,0:T(8,128)(2,1)} fusion(bf16[16,512,512]{2,1,0:T(8,128)(2,1)} %all-gather.6.cloned.1.call-done, s32[1024]{0:T(1024)S(1)} %pad_clamp_fusion), kind=kCustom, calls=%fused_computation.clone | custom fusion | bytes 9437220 | tf_op jit(solution)/shard_map/jit(_take)/gather | solution.py:72
  96.2 5.0 select_bitcast_fusion.2
  101.2 6.7 %copy.18 = bf16[512,9,512]{0,2,1:T(8,128)(2,1)} copy(bf16[512,9,512]{2,0,1:T(8,128)(2,1)} %select_bitcast_fusion.2) | data formatting | bytes 9437184 | tf_op jit(solution)/shard_map/transpose | solution.py:73
  107.9 6.0 %fusion.10 = f32[512,512]{1,0:T(8,128)S(1)} fusion(bf16[512,4608]{0,1:T(8,128)(2,1)} %bitcast.56, bf16[4608,512]{1,0:T(8,128)(2,1)} %mul.58), kind=kOutput, calls=%fused_computation.37 | convolution fusion | flops 2415919104 | bytes 10485760 | tf_op jit(solution)/shard_map/dot_general | solution.py:74
  113.9 0.0 all-gather.8.cloned.1.call-update
  113.9 0.0 all-gather.10.cloned.1.call-start
  114.0 1.3 copy.23
  115.3 2.1 collective-permute-start
  117.4 0.9 copy.31
  118.2 120.7 %collective-permute-done = f32[512,512]{0,1:T(8,128)} collective-permute-done((f32[512,512]{0,1:T(8,128)}, f32[512,512]{0,1:T(8,128)}, u32[]{:S(2)}, u32[]{:S(2)}) %collective-permute-start) | collective-permute-done | bytes 1048608 | tf_op jit(solution)/shard_map/ppermute | solution.py:76
  239.0 0.0 all-gather.8.cloned.1.call-done
  239.0 7.0 %gather_fusion.1 = bf16[9,512,512]{2,1,0:T(8,128)(2,1)} fusion(bf16[16,512,512]{2,1,0:T(8,128)(2,1)} %bitcast.66, s32[1024]{0:T(1024)S(1)} %pad_clamp_fusion), kind=kCustom, calls=%fused_computation.1.clone | custom fusion | bytes 9437220 | tf_op jit(solution)/shard_map/jit(_take)/gather | solution.py:72
  246.0 5.0 select_bitcast_fusion.1
  251.0 6.7 %copy.24 = bf16[512,9,512]{0,2,1:T(8,128)(2,1)} copy(bf16[512,9,512]{2,0,1:T(8,128)(2,1)} %select_bitcast_fusion.1) | data formatting | bytes 9437184 | tf_op jit(solution)/shard_map/transpose | solution.py:73
  257.7 7.4 %fusion.11 = f32[512,512]{1,0:T(8,128)} fusion(bf16[512,4608]{0,1:T(8,128)(2,1)} %bitcast.57, bf16[4608,512]{1,0:T(8,128)(2,1)} %mul.58), kind=kOutput, calls=%fused_computation.38 | convolution fusion | flops 2415919104 | bytes 10485760 | tf_op jit(solution)/shard_map/dot_general | solution.py:74
  265.0 0.0 all-gather.10.cloned.1.call-update
  265.1 2.5 copy.25
  267.6 1.9 collective-permute-start.1
  269.5 117.6 %collective-permute-done.1 = f32[512,512]{0,1:T(8,128)} collective-permute-done((f32[512,512]{0,1:T(8,128)}, f32[512,512]{0,1:T(8,128)}, u32[]{:S(2)}, u32[]{:S(2)}) %collective-permute-start.1) | collective-permute-done | bytes 1048608 | tf_op jit(solution)/shard_map/ppermute | solution.py:76
  387.2 0.0 all-gather.10.cloned.1.call-done
  387.2 7.0 %gather_fusion.2 = bf16[9,512,512]{2,1,0:T(8,128)(2,1)} fusion(bf16[16,512,512]{2,1,0:T(8,128)(2,1)} %bitcast.67, s32[1024]{0:T(1024)S(1)} %pad_clamp_fusion), kind=kCustom, calls=%fused_computation.2.clone | custom fusion | bytes 9437220 | tf_op jit(solution)/shard_map/jit(_take)/gather | solution.py:72
  394.2 5.0 select_bitcast_fusion
  399.2 6.7 %copy.26 = bf16[512,9,512]{0,2,1:T(8,128)(2,1)} copy(bf16[512,9,512]{2,0,1:T(8,128)(2,1)} %select_bitcast_fusion) | data formatting | bytes 9437184 | tf_op jit(solution)/shard_map/transpose | solution.py:73
  405.8 7.4 %fusion.12 = f32[512,512]{1,0:T(8,128)} fusion(bf16[512,4608]{0,1:T(8,128)(2,1)} %bitcast.55, bf16[4608,512]{1,0:T(8,128)(2,1)} %mul.58), kind=kOutput, calls=%fused_computation.39 | convolution fusion | flops 2415919104 | bytes 10485760 | tf_op jit(solution)/shard_map/dot_general | solution.py:74
  413.2 0.0 copy-start.5
  413.2 2.6 copy.27
  415.8 1.9 collective-permute-start.2
  417.7 0.5 convert_multiply_fusion
  418.1 0.0 copy-start
  418.2 0.0 copy-start.2
  418.2 0.1 copy.29
  418.2 0.3 mul.63
  418.6 0.0 copy-start.1
  418.6 0.0 copy-start.3
  418.6 0.1 copy.32
  418.7 0.0 copy-done.5
  418.7 0.7 fusion.9
  419.4 2.3 fusion.1
  421.6 0.0 copy-done
  421.6 0.0 copy-done.2
  421.7 2.1 fusion.2
  423.7 82.7 %collective-permute-done.2 = f32[512,512]{0,1:T(8,128)S(1)} collective-permute-done((f32[512,512]{0,1:T(8,128)}, f32[512,512]{0,1:T(8,128)S(1)}, u32[]{:S(2)}, u32[]{:S(2)}) %collective-permute-start.2) | collective-permute-done | bytes 1048608 | tf_op jit(solution)/shard_map/ppermute | solution.py:76
  506.4 0.0 copy-done.1
  506.4 0.0 copy-done.3
  506.4 0.9 fusion.3
  507.3 1.7 fusion
  (4 shorter events, 0.0 us)
Async XLA Ops:
  6.5 82.7 %all-gather.6.cloned.1.call-start = ((), (), s32[]{:S(2)}) async-start(), calls=%async_computation | async-start | bytes 8912896 | tf_op jit(solution)/shard_map/all_gather | solution.py:69
  8.9 4.5 copy-start.4
  13.3 225.7 %all-gather.8.cloned.1.call-start = ((), (), s32[]{:S(2)}) async-start(), calls=%async_computation.1 | async-start | bytes 8912896 | tf_op jit(solution)/shard_map/all_gather | solution.py:69
  113.9 273.3 %all-gather.10.cloned.1.call-start = ((), (), s32[]{:S(2)}) async-start(), calls=%async_computation.2 | async-start | bytes 8912896 | tf_op jit(solution)/shard_map/all_gather | solution.py:69
  115.3 123.7 %collective-permute-start = (f32[512,512]{0,1:T(8,128)}, f32[512,512]{0,1:T(8,128)}, u32[]{:S(2)}, u32[]{:S(2)}) collective-permute-start(f32[512,512]{0,1:T(8,128)} %copy.23), channel_id=1, source_target_pairs={{0,0},{1,16},{2,32},{3,48},{4,64},{5,80},{6,96},{7,112},{8,128},{9... | collective-permute-start | bytes 3145736 | tf_op jit(solution)/shard_map/ppermute | solution.py:76
  267.6 119.6 %collective-permute-start.1 = (f32[512,512]{0,1:T(8,128)}, f32[512,512]{0,1:T(8,128)}, u32[]{:S(2)}, u32[]{:S(2)}) collective-permute-start(f32[512,512]{0,1:T(8,128)} %copy.25), channel_id=1, source_target_pairs={{0,0},{1,16},{2,32},{3,48},{4,64},{5,80},{6,96},{7,112},{8,128},{9... | collective-permute-start | bytes 3145736 | tf_op jit(solution)/shard_map/ppermute | solution.py:76
  413.2 5.5 %copy-start.5 = (s32[3]{0:T(128)S(1)}, s32[3]{0:T(128)}, u32[]{:S(2)}) copy-start(s32[3]{0:T(128)} %param.7) | copy-start | bytes 40
  415.8 90.6 %collective-permute-start.2 = (f32[512,512]{0,1:T(8,128)}, f32[512,512]{0,1:T(8,128)S(1)}, u32[]{:S(2)}, u32[]{:S(2)}) collective-permute-start(f32[512,512]{0,1:T(8,128)} %copy.27), channel_id=1, source_target_pairs={{0,0},{1,16},{2,32},{3,48},{4,64},{5,80},{6,96},{7,112},{8,128},{9... | collective-permute-start | bytes 3145736 | tf_op jit(solution)/shard_map/ppermute | solution.py:76
  418.1 3.5 copy-start
  418.2 3.5 copy-start.2
  418.6 87.8 %copy-start.1 = (bf16[64,8,2,256]{3,1,2,0:T(8,128)(2,1)S(1)}, bf16[64,8,2,256]{3,1,2,0:T(8,128)(2,1)}, u32[]{:S(2)}) copy-start(bf16[64,8,2,256]{3,1,2,0:T(8,128)(2,1)} %copy.31) | copy-start | bytes 1572868
  418.6 87.8 %copy-start.3 = (f32[512,512]{1,0:T(8,128)S(1)}, f32[512,512]{1,0:T(8,128)}, u32[]{:S(2)}) copy-start(f32[512,512]{1,0:T(8,128)} %fusion.12) | copy-start | bytes 3145732
Sparse Core Ops, SparseCore 0:
  13.5 75.6 all-gather.5
  114.0 120.8 all-gather.7
  265.2 117.1 all-gather.9

commit v11 on v4

--- a/solution.py
+++ b/solution.py
@@ -65,7 +65,10 @@
         own = p1_local[d]
         if d >= 1:
             own = lax.optimization_barrier((own, products[d - 1]))[0]
-        fetched = [lax.ppermute(own, "col", fp) for fp in fetch_pairs]
+        near = [lax.ppermute(own, "col", fp) for fp in fetch_pairs[:2]]
+        relay = [(c, (c + 2) % col_count) if c % 2 == 0 else (c, (c - 2) % col_count) for c in range(col_count)]
+        far = lax.ppermute(jnp.stack(near, axis=0), "col", relay)
+        fetched = near + [far[0], far[1]]
         partner_own = lax.ppermute(own, "col", swap)
         partner_fetched = [lax.ppermute(fetched[j], "col", swap) for j in range(col_span - 1)]
         tiles = [own] + fetched + [partner_own] + partner_fetched

time: 411 us -> 411 us (level); the launches traced: 405 us -> 409 us
  waiting for transfers between devices: 287 us -> 293 us
    ppermute x3, waiting for transfers between devices: 198 us -> 247 us  [body(): mirrored = lax.ppermute(summed, ('row', 'col'), pairs)]
    ppermute x12 -> x9, waiting for transfers between devices: 89.3 us -> 46.4 us  [the longest x6 23.4 us: body(): near = [lax.ppermute(own, 'col', fp) for fp in fetch_pairs[:2]]]
    ppermute x12 -> x9, starting transfers between devices: 28.7 us -> 19.6 us  [the longest x6 11 us: body(): near = [lax.ppermute(own, 'col', fp) for fp in fetch_pairs[:2]]]
    ppermute x9, starting transfers between devices: 7.95 us -> 15.7 us  [body(): lax.ppermute(fetched[j], 'col', swap)]
  transfers between devices with their start and end apart: 27 -> 24, of which waited for: 11 -> 11; matrix products, arithmetic and copies ran while one was open for 10% -> 9% of each run, Pallas kernels for 0% -> 0%
where the time goes in v11:
time: 411 us; the launch traced here: 409 us
  waiting for transfers between devices  293 us (71%)
  starting transfers between devices  49 us (12%)
  local copies, waits for them, and re-layouts  26.1 us (6%)
  other arithmetic  20.3 us (5%)
  matrix products  20 us (5%)
    ppermute x3, waiting for transfers between devices, body(): mirrored = lax.ppermute(summed, ('row', 'col'), pairs)  247 us
    ppermute x6, waiting for transfers between devices, body(): near = [lax.ppermute(own, 'col', fp) for fp in fetch_pairs[:2]]  23.4 us
    ppermute x3, waiting for transfers between devices, body(): far = lax.ppermute(jnp.stack(near, axis=0), 'col', relay)  22.9 us
    dot_general x27, matrix products, body(): summed = summed + jnp.dot(tile, factor, preferred_element_type=jnp.float32)  20 us
    ppermute x9, starting transfers between devices, body(): lax.ppermute(fetched[j], 'col', swap)  15.7 us
    ppermute x6, starting transfers between devices, body(): near = [lax.ppermute(own, 'col', fp) for fp in fetch_pairs[:2]]  11 us
    reshape x2, local copies, waits for them, and re-layouts, mask_blocks(): shaped = values.reshape(leading + (row_blocks, BLK, col_blocks, BLK))  10.1 us
    ppermute x3, starting transfers between devices, body(): mirrored = lax.ppermute(summed, ('row', 'col'), pairs)  8.66 us
  transfers between devices with their start and end apart: 24, of which 11 were waited for; matrix products, arithmetic and copies ran while one was open for 9% of the time, Pallas kernels for 0%

profile of v11, /device:TPU:218, one launch (start us, length us, event | category | flops | bytes accessed | tf_op | source)
XLA Modules:
  0.0 409.2 jit_solution(16278800207887928108)
XLA Ops:
  0.0 2.4 reshape.34
  2.4 0.8 dynamic-slice_convert_fusion
  3.2 1.4 broadcast_multiply_fusion
  4.6 1.9 fusion.95
  6.9 4.9 %collective-permute-start.1 = (bf16[512,512]{1,0:T(8,128)(2,1)S(1)}, bf16[512,512]{1,0:T(8,128)(2,1)S(1)}, u32[]{:S(2)}, u32[]{:S(2)}) collective-permute-start(bf16[512,512]{1,0:T(8,128)(2,1)S(1)} %bitcast.107), channel_id=1, source_target_pairs={{14,0},{3,1},{0,2},{5,3},{2,4},{7,5},{4,6},{9,7},{6,8},{11,9},{8,1... | collective-permute-start | bytes 1572872 | tf_op jit(solution)/shard_map/ppermute | solution.py:68
  12.0 7.7 %reshape.35 = bf16[18,256,2,256]{3,2,1,0:T(2,128)(2,1)} reshape(bf16[4608,512]{1,0:T(8,128)(2,1)} %param.8) | data formatting | bytes 9437184 | tf_op jit(solution)/shard_map/reshape | solution.py:13
  19.7 1.6 slice_multiply_fusion
  21.4 2.5 mul.97
  23.9 1.0 copy.72
  24.9 1.2 slice-done.3
  26.1 3.6 mul.100
  29.9 2.3 collective-permute-start.2
  32.9 0.5 collective-permute-start.4
  33.4 1.6 fusion.45
  35.1 1.5 convolution_add_fusion.4
  37.0 7.8 %collective-permute-done.2 = bf16[2,512,512]{2,1,0:T(8,128)(2,1)S(1)} collective-permute-done((bf16[2,512,512]{2,1,0:T(8,128)(2,1)S(1)}, bf16[2,512,512]{2,1,0:T(8,128)(2,1)S(1)}, u32[]{:S(2)}, u32[]{:S(2)}) %collective-permute-start.2) | collective-permute-done | bytes 1048608 | tf_op jit(solution)/shard_map/ppermute | solution.py:70
  44.9 3.1 collective-permute-start.6
  48.8 0.5 fusion.15
  49.9 0.5 fusion.12
  50.5 5.6 %collective-permute-start.9 = (bf16[512,512]{1,0:T(8,128)(2,1)S(1)}, bf16[512,512]{1,0:T(8,128)(2,1)}, u32[]{:S(2)}, u32[]{:S(2)}) collective-permute-start(bf16[512,512]{1,0:T(8,128)(2,1)S(1)} %bitcast.97), channel_id=1, source_target_pairs={{14,0},{3,1},{0,2},{5,3},{2,4},{7,5},{4,6},{9,7},{6,8},{11,9},{8,1... | collective-permute-start | bytes 1572872 | tf_op jit(solution)/shard_map/ppermute | solution.py:68
  56.1 8.1 %collective-permute-done.8 = bf16[512,512]{1,0:T(8,128)(2,1)} collective-permute-done((bf16[512,512]{1,0:T(8,128)(2,1)S(1)}, bf16[512,512]{1,0:T(8,128)(2,1)}, u32[]{:S(2)}, u32[]{:S(2)}) %collective-permute-start.8) | collective-permute-done | bytes 524320 | tf_op jit(solution)/shard_map/ppermute | solution.py:68
  64.2 1.2 collective-permute-done.9
  65.4 2.3 pad_maximum_fusion.1
  67.7 6.2 %collective-permute-start.10 = (bf16[2,512,512]{2,1,0:T(8,128)(2,1)}, bf16[2,512,512]{2,1,0:T(8,128)(2,1)}, u32[]{:S(2)}, u32[]{:S(2)}) collective-permute-start(bf16[2,512,512]{2,1,0:T(8,128)(2,1)} %pad_maximum_fusion.1), channel_id=1, source_target_pairs={{0,2},{1,15},{2,4},{3,1},{4,6},{5,3},{6,8},{7,5},{8,10},{9,7},{10,... | collective-permute-start | bytes 3145736 | tf_op jit(solution)/shard_map/ppermute | solution.py:70
  73.9 1.3 copy.31
  75.3 2.2 collective-permute-start.7
  77.4 0.5 collective-permute-start.11
  78.5 8.8 %collective-permute-done.10 = bf16[2,512,512]{2,1,0:T(8,128)(2,1)} collective-permute-done((bf16[2,512,512]{2,1,0:T(8,128)(2,1)}, bf16[2,512,512]{2,1,0:T(8,128)(2,1)}, u32[]{:S(2)}, u32[]{:S(2)}) %collective-permute-start.10) | collective-permute-done | bytes 1048608 | tf_op jit(solution)/shard_map/ppermute | solution.py:70
  87.3 1.3 slice_bitcast_fusion.2
  88.5 1.7 collective-permute-start.14
  90.3 1.1 copy.74
  91.4 86.8 %collective-permute-done.7 = f32[512,512]{0,1:T(8,128)S(1)} collective-permute-done((f32[512,512]{0,1:T(8,128)}, f32[512,512]{0,1:T(8,128)S(1)}, u32[]{:S(2)}, u32[]{:S(2)}) %collective-permute-start.7) | collective-permute-done | bytes 1048608 | tf_op jit(solution)/shard_map/ppermute | solution.py:81
  178.2 1.7 fusion.65
  179.9 1.7 fusion.60
  181.6 1.5 fusion.54
  183.2 0.5 fusion.49
  184.1 0.5 fusion.38
  184.6 0.5 fusion.32
  185.6 0.8 fusion.17
  186.6 13.5 %collective-permute-done.16 = bf16[512,512]{1,0:T(8,128)(2,1)S(1)} collective-permute-done((bf16[512,512]{1,0:T(8,128)(2,1)S(1)}, bf16[512,512]{1,0:T(8,128)(2,1)S(1)}, u32[]{:S(2)}, u32[]{:S(2)}) %collective-permute-start.16) | collective-permute-done | bytes 524320 | tf_op jit(solution)/shard_map/ppermute | solution.py:68
  200.1 0.6 collective-permute-done.17
  200.9 3.4 collective-permute-start.15
  204.3 4.6 %collective-permute-start.19 = (bf16[512,512]{1,0:T(8,128)(2,1)S(1)}, bf16[512,512]{1,0:T(8,128)(2,1)S(1)}, u32[]{:S(2)}, u32[]{:S(2)}) collective-permute-start(bf16[512,512]{1,0:T(8,128)(2,1)S(1)} %bitcast.103), channel_id=1, source_target_pairs={{0,1},{1,0},{2,3},{3,2},{4,5},{5,4},{6,7},{7,6},{8,9},{9,8},{10,11... | collective-permute-start | bytes 1572872 | tf_op jit(solution)/shard_map/ppermute | solution.py:72
  209.4 6.3 %collective-permute-done.18 = bf16[2,512,512]{2,1,0:T(8,128)(2,1)S(1)} collective-permute-done((bf16[2,512,512]{2,1,0:T(8,128)(2,1)S(1)}, bf16[2,512,512]{2,1,0:T(8,128)(2,1)S(1)}, u32[]{:S(2)}, u32[]{:S(2)}) %collective-permute-start.18) | collective-permute-done | bytes 1048608 | tf_op jit(solution)/shard_map/ppermute | solution.py:70
  215.7 9.1 %collective-permute-start.22 = (bf16[512,512]{1,0:T(8,128)(2,1)S(1)}, bf16[512,512]{1,0:T(8,128)(2,1)S(1)}, u32[]{:S(2)}, u32[]{:S(2)}) collective-permute-start(bf16[512,512]{1,0:T(8,128)(2,1)S(1)} %get-tuple-element.39), channel_id=1, source_target_pairs={{0,1},{1,0},{2,3},{3,2},{4,5},{5,4},{6,7},{7,6},{8,9},{9,8},{10,11... | collective-permute-start | bytes 1572872 | tf_op jit(solution)/shard_map/ppermute | solution.py:73
  224.9 124.0 %collective-permute-done.15 = f32[512,512]{0,1:T(8,128)S(1)} collective-permute-done((f32[512,512]{0,1:T(8,128)S(1)}, f32[512,512]{0,1:T(8,128)S(1)}, u32[]{:S(2)}, u32[]{:S(2)}) %collective-permute-start.15) | collective-permute-done | bytes 1048608 | tf_op jit(solution)/shard_map/ppermute | solution.py:81
  348.9 0.5 fusion.63
  349.4 0.5 fusion.58
  349.9 0.5 fusion.52
  350.4 0.5 fusion.47
  350.9 0.5 fusion.41
  351.9 0.5 fusion.30
  352.4 0.5 fusion.24
  353.0 1.7 fusion.19
  354.7 3.1 collective-permute-start.23
  358.1 1.1 copy.75
  359.2 0.6 fusion.96
  359.8 1.9 fusion.20
  361.7 1.6 copy.41
  363.3 3.2 fusion.21
  366.5 1.6 copy.51
  368.0 35.8 %collective-permute-done.23 = f32[512,512]{0,1:T(8,128)} collective-permute-done((f32[512,512]{0,1:T(8,128)}, f32[512,512]{0,1:T(8,128)}, u32[]{:S(2)}, u32[]{:S(2)}) %collective-permute-start.23) | collective-permute-done | bytes 1048608 | tf_op jit(solution)/shard_map/ppermute | solution.py:81
  403.8 2.1 fusion.22
  406.0 3.3 fusion
  (73 shorter events, 7.0 us)
Async XLA Ops:
  0.0 11.8 %copy-start.7 = (s32[32,32]{1,0:T(8,128)S(1)}, s32[32,32]{1,0:T(8,128)}, u32[]{:S(2)}) copy-start(s32[32,32]{1,0:T(8,128)} %param.6) | copy-start | bytes 12292
  6.6 25.6 %copy-start.1 = (bf16[64,8,2,256]{3,1,2,0:T(8,128)(2,1)}, bf16[64,8,2,256]{3,1,2,0:T(8,128)(2,1)S(1)}, u32[]{:S(2)}) copy-start(bf16[64,8,2,256]{3,1,2,0:T(8,128)(2,1)S(1)} %copy.70) | copy-start | bytes 1572868
  6.6 23.2 %collective-permute-start = (bf16[512,512]{1,0:T(8,128)(2,1)S(1)}, bf16[512,512]{1,0:T(8,128)(2,1)S(1)}, u32[]{:S(2)}, u32[]{:S(2)}) collective-permute-start(bf16[512,512]{1,0:T(8,128)(2,1)S(1)} %bitcast.106), channel_id=1, source_target_pairs={{15,0},{2,1},{1,2},{4,3},{3,4},{6,5},{5,6},{8,7},{7,8},{10,9},{9,1... | collective-permute-start | bytes 1572872 | tf_op jit(solution)/shard_map/ppermute | solution.py:68
  6.9 23.0 %collective-permute-start.1 = (bf16[512,512]{1,0:T(8,128)(2,1)S(1)}, bf16[512,512]{1,0:T(8,128)(2,1)S(1)}, u32[]{:S(2)}, u32[]{:S(2)}) collective-permute-start(bf16[512,512]{1,0:T(8,128)(2,1)S(1)} %bitcast.107), channel_id=1, source_target_pairs={{14,0},{3,1},{0,2},{5,3},{2,4},{7,5},{4,6},{9,7},{6,8},{11,9},{8,1... | collective-permute-start | bytes 1572872 | tf_op jit(solution)/shard_map/ppermute | solution.py:68
  11.7 21.7 %collective-permute-start.3 = (bf16[512,512]{1,0:T(8,128)(2,1)S(1)}, bf16[512,512]{1,0:T(8,128)(2,1)}, u32[]{:S(2)}, u32[]{:S(2)}) collective-permute-start(bf16[512,512]{1,0:T(8,128)(2,1)S(1)} %bitcast.108), channel_id=1, source_target_pairs={{0,1},{1,0},{2,3},{3,2},{4,5},{5,4},{6,7},{7,6},{8,9},{9,8},{10,11... | collective-permute-start | bytes 1572872 | tf_op jit(solution)/shard_map/ppermute | solution.py:72
  21.4 3.5 slice-start.2
  23.9 2.2 slice-start.3
  29.8 5.3 %copy-start = (bf16[4608,512]{1,0:T(8,128)(2,1)S(1)}, bf16[4608,512]{1,0:T(8,128)(2,1)}, u32[]{:S(2)}) copy-start(bf16[4608,512]{1,0:T(8,128)(2,1)} %mul.100) | copy-start | bytes 14155780
  29.8 2.4 copy-start.5
  29.9 14.9 %collective-permute-start.2 = (bf16[2,512,512]{2,1,0:T(8,128)(2,1)S(1)}, bf16[2,512,512]{2,1,0:T(8,128)(2,1)S(1)}, u32[]{:S(2)}, u32[]{:S(2)}) collective-permute-start(bf16[2,512,512]{2,1,0:T(8,128)(2,1)S(1)} %pad_maximum_fusion), channel_id=1, source_target_pairs={{0,2},{1,15},{2,4},{3,1},{4,6},{5,3},{6,8},{7,5},{8,10},{9,7},{10,... | collective-permute-start | bytes 3145736 | tf_op jit(solution)/shard_map/ppermute | solution.py:70
  32.6 3.9 collective-permute-start.5
  32.9 17.0 %collective-permute-start.4 = (bf16[512,512]{1,0:T(8,128)(2,1)}, bf16[512,512]{1,0:T(8,128)(2,1)S(1)}, u32[]{:S(2)}, u32[]{:S(2)}) collective-permute-start(bf16[512,512]{1,0:T(8,128)(2,1)} %copy-done.5), channel_id=1, source_target_pairs={{0,1},{1,0},{2,3},{3,2},{4,5},{5,4},{6,7},{7,6},{8,9},{9,8},{10,11... | collective-permute-start | bytes 1572872 | tf_op jit(solution)/shard_map/ppermute | solution.py:73
  44.9 4.6 %collective-permute-start.6 = (bf16[512,512]{1,0:T(8,128)(2,1)S(1)}, bf16[512,512]{1,0:T(8,128)(2,1)S(1)}, u32[]{:S(2)}, u32[]{:S(2)}) collective-permute-start(bf16[512,512]{1,0:T(8,128)(2,1)S(1)} %slice_bitcast_fusion.6), channel_id=1, source_target_pairs={{0,1},{1,0},{2,3},{3,2},{4,5},{5,4},{6,7},{7,6},{8,9},{9,8},{10,11... | collective-permute-start | bytes 1572872 | tf_op jit(solution)/shard_map/ppermute | solution.py:73
  49.9 133.2 %slice-start = ((s8[4718592]{0:T(1024)(128)(4,1)}), s8[524288]{0:T(1024)(128)(4,1)S(1)}, s32[]{:S(2)}) async-start(s8[4718592]{0:T(1024)(128)(4,1)} %bitcast.87), calls=%async_computation | async-start | bytes 1048576
  50.4 13.8 %collective-permute-start.8 = (bf16[512,512]{1,0:T(8,128)(2,1)S(1)}, bf16[512,512]{1,0:T(8,128)(2,1)}, u32[]{:S(2)}, u32[]{:S(2)}) collective-permute-start(bf16[512,512]{1,0:T(8,128)(2,1)S(1)} %bitcast.96), channel_id=1, source_target_pairs={{15,0},{2,1},{1,2},{4,3},{3,4},{6,5},{5,6},{8,7},{7,8},{10,9},{9,1... | collective-permute-start | bytes 1572872 | tf_op jit(solution)/shard_map/ppermute | solution.py:68
  50.5 14.9 %collective-permute-start.9 = (bf16[512,512]{1,0:T(8,128)(2,1)S(1)}, bf16[512,512]{1,0:T(8,128)(2,1)}, u32[]{:S(2)}, u32[]{:S(2)}) collective-permute-start(bf16[512,512]{1,0:T(8,128)(2,1)S(1)} %bitcast.97), channel_id=1, source_target_pairs={{14,0},{3,1},{0,2},{5,3},{2,4},{7,5},{4,6},{9,7},{6,8},{11,9},{8,1... | collective-permute-start | bytes 1572872 | tf_op jit(solution)/shard_map/ppermute | solution.py:68
  67.7 19.6 %collective-permute-start.10 = (bf16[2,512,512]{2,1,0:T(8,128)(2,1)}, bf16[2,512,512]{2,1,0:T(8,128)(2,1)}, u32[]{:S(2)}, u32[]{:S(2)}) collective-permute-start(bf16[2,512,512]{2,1,0:T(8,128)(2,1)} %pad_maximum_fusion.1), channel_id=1, source_target_pairs={{0,2},{1,15},{2,4},{3,1},{4,6},{5,3},{6,8},{7,5},{8,10},{9,7},{10,... | collective-permute-start | bytes 3145736 | tf_op jit(solution)/shard_map/ppermute | solution.py:70
  75.3 107.9 %slice-start.1 = ((s8[4718592]{0:T(1024)(128)(4,1)}), s8[4194304]{0:T(1024)(128)(4,1)S(1)}, s32[]{:S(2)}) async-start(s8[4718592]{0:T(1024)(128)(4,1)} %bitcast.87), calls=%async_computation.1 | async-start | bytes 8388608
  75.3 102.9 %collective-permute-start.7 = (f32[512,512]{0,1:T(8,128)}, f32[512,512]{0,1:T(8,128)S(1)}, u32[]{:S(2)}, u32[]{:S(2)}) collective-permute-start(f32[512,512]{0,1:T(8,128)} %copy.31), channel_id=1, source_target_pairs={{0,0},{1,16},{2,32},{3,48},{4,64},{5,80},{6,96},{7,112},{8,128},{9... | collective-permute-start | bytes 3145736 | tf_op jit(solution)/shard_map/ppermute | solution.py:81
  77.4 14.0 %collective-permute-start.11 = (bf16[512,512]{1,0:T(8,128)(2,1)S(1)}, bf16[512,512]{1,0:T(8,128)(2,1)S(1)}, u32[]{:S(2)}, u32[]{:S(2)}) collective-permute-start(bf16[512,512]{1,0:T(8,128)(2,1)S(1)} %bitcast.98), channel_id=1, source_target_pairs={{0,1},{1,0},{2,3},{3,2},{4,5},{5,4},{6,7},{7,6},{8,9},{9,8},{10,11... | collective-permute-start | bytes 1572872 | tf_op jit(solution)/shard_map/ppermute | solution.py:72
  78.0 100.2 %collective-permute-start.12 = (bf16[512,512]{1,0:T(8,128)(2,1)}, bf16[512,512]{1,0:T(8,128)(2,1)S(1)}, u32[]{:S(2)}, u32[]{:S(2)}) collective-permute-start(bf16[512,512]{1,0:T(8,128)(2,1)} %collective-permute-done.8), channel_id=1, source_target_pairs={{0,1},{1,0},{2,3},{3,2},{4,5},{5,4},{6,7},{7,6},{8,9},{9,8},{10,11... | collective-permute-start | bytes 1572872 | tf_op jit(solution)/shard_map/ppermute | solution.py:73
  78.1 100.1 %collective-permute-start.13 = (bf16[512,512]{1,0:T(8,128)(2,1)}, bf16[512,512]{1,0:T(8,128)(2,1)S(1)}, u32[]{:S(2)}, u32[]{:S(2)}) collective-permute-start(bf16[512,512]{1,0:T(8,128)(2,1)} %collective-permute-done.9), channel_id=1, source_target_pairs={{0,1},{1,0},{2,3},{3,2},{4,5},{5,4},{6,7},{7,6},{8,9},{9,8},{10,11... | collective-permute-start | bytes 1572872 | tf_op jit(solution)/shard_map/ppermute | solution.py:73
  88.5 89.7 %collective-permute-start.14 = (bf16[512,512]{1,0:T(8,128)(2,1)S(1)}, bf16[512,512]{1,0:T(8,128)(2,1)S(1)}, u32[]{:S(2)}, u32[]{:S(2)}) collective-permute-start(bf16[512,512]{1,0:T(8,128)(2,1)S(1)} %get-tuple-element.29), channel_id=1, source_target_pairs={{0,1},{1,0},{2,3},{3,2},{4,5},{5,4},{6,7},{7,6},{8,9},{9,8},{10,11... | collective-permute-start | bytes 1572872 | tf_op jit(solution)/shard_map/ppermute | solution.py:73
  186.4 165.6 %copy-start.3 = (f32[512,512]{0,1:T(8,128)}, f32[512,512]{0,1:T(8,128)S(1)}, u32[]{:S(2)}) copy-start(f32[512,512]{0,1:T(8,128)S(1)} %fusion.17) | copy-start | bytes 3145732
  186.4 13.7 %collective-permute-start.16 = (bf16[512,512]{1,0:T(8,128)(2,1)S(1)}, bf16[512,512]{1,0:T(8,128)(2,1)S(1)}, u32[]{:S(2)}, u32[]{:S(2)}) collective-permute-start(bf16[512,512]{1,0:T(8,128)(2,1)S(1)} %bitcast.101), channel_id=1, source_target_pairs={{15,0},{2,1},{1,2},{4,3},{3,4},{6,5},{5,6},{8,7},{7,8},{10,9},{9,1... | collective-permute-start | bytes 1572872 | tf_op jit(solution)/shard_map/ppermute | solution.py:68
  186.5 14.2 %collective-permute-start.17 = (bf16[512,512]{1,0:T(8,128)(2,1)S(1)}, bf16[512,512]{1,0:T(8,128)(2,1)S(1)}, u32[]{:S(2)}, u32[]{:S(2)}) collective-permute-start(bf16[512,512]{1,0:T(8,128)(2,1)S(1)} %bitcast.102), channel_id=1, source_target_pairs={{14,0},{3,1},{0,2},{5,3},{2,4},{7,5},{4,6},{9,7},{6,8},{11,9},{8,1... | collective-permute-start | bytes 1572872 | tf_op jit(solution)/shard_map/ppermute | solution.py:68
  200.8 14.9 %collective-permute-start.18 = (bf16[2,512,512]{2,1,0:T(8,128)(2,1)S(1)}, bf16[2,512,512]{2,1,0:T(8,128)(2,1)S(1)}, u32[]{:S(2)}, u32[]{:S(2)}) collective-permute-start(bf16[2,512,512]{2,1,0:T(8,128)(2,1)S(1)} %pad_maximum_fusion.2), channel_id=1, source_target_pairs={{0,2},{1,15},{2,4},{3,1},{4,6},{5,3},{6,8},{7,5},{8,10},{9,7},{10,... | collective-permute-start | bytes 3145736 | tf_op jit(solution)/shard_map/ppermute | solution.py:70
  200.9 148.0 %collective-permute-start.15 = (f32[512,512]{0,1:T(8,128)S(1)}, f32[512,512]{0,1:T(8,128)S(1)}, u32[]{:S(2)}, u32[]{:S(2)}) collective-permute-start(f32[512,512]{0,1:T(8,128)S(1)} %fusion.17), channel_id=1, source_target_pairs={{0,0},{1,16},{2,32},{3,48},{4,64},{5,80},{6,96},{7,112},{8,128},{9... | collective-permute-start | bytes 3145736 | tf_op jit(solution)/shard_map/ppermute | solution.py:81
  204.3 20.6 %collective-permute-start.19 = (bf16[512,512]{1,0:T(8,128)(2,1)S(1)}, bf16[512,512]{1,0:T(8,128)(2,1)S(1)}, u32[]{:S(2)}, u32[]{:S(2)}) collective-permute-start(bf16[512,512]{1,0:T(8,128)(2,1)S(1)} %bitcast.103), channel_id=1, source_target_pairs={{0,1},{1,0},{2,3},{3,2},{4,5},{5,4},{6,7},{7,6},{8,9},{9,8},{10,11... | collective-permute-start | bytes 1572872 | tf_op jit(solution)/shard_map/ppermute | solution.py:72
  208.9 16.0 %collective-permute-start.20 = (bf16[512,512]{1,0:T(8,128)(2,1)S(1)}, bf16[512,512]{1,0:T(8,128)(2,1)S(1)}, u32[]{:S(2)}, u32[]{:S(2)}) collective-permute-start(bf16[512,512]{1,0:T(8,128)(2,1)S(1)} %collective-permute-done.16), channel_id=1, source_target_pairs={{0,1},{1,0},{2,3},{3,2},{4,5},{5,4},{6,7},{7,6},{8,9},{9,8},{10,11... | collective-permute-start | bytes 1572872 | tf_op jit(solution)/shard_map/ppermute | solution.py:73
  209.0 15.9 %collective-permute-start.21 = (bf16[512,512]{1,0:T(8,128)(2,1)S(1)}, bf16[512,512]{1,0:T(8,128)(2,1)S(1)}, u32[]{:S(2)}, u32[]{:S(2)}) collective-permute-start(bf16[512,512]{1,0:T(8,128)(2,1)S(1)} %collective-permute-done.17), channel_id=1, source_target_pairs={{0,1},{1,0},{2,3},{3,2},{4,5},{5,4},{6,7},{7,6},{8,9},{9,8},{10,11... | collective-permute-start | bytes 1572872 | tf_op jit(solution)/shard_map/ppermute | solution.py:73
  215.7 133.2 %collective-permute-start.22 = (bf16[512,512]{1,0:T(8,128)(2,1)S(1)}, bf16[512,512]{1,0:T(8,128)(2,1)S(1)}, u32[]{:S(2)}, u32[]{:S(2)}) collective-permute-start(bf16[512,512]{1,0:T(8,128)(2,1)S(1)} %get-tuple-element.39), channel_id=1, source_target_pairs={{0,1},{1,0},{2,3},{3,2},{4,5},{5,4},{6,7},{7,6},{8,9},{9,8},{10,11... | collective-permute-start | bytes 1572872 | tf_op jit(solution)/shard_map/ppermute | solution.py:73
  348.9 2.0 copy-start.6
  352.9 6.3 %copy-start.8 = (s32[3]{0:T(128)S(1)}, s32[3]{0:T(128)}, u32[]{:S(2)}) copy-start(s32[3]{0:T(128)} %param.5) | copy-start | bytes 40
  352.9 6.9 %copy-start.2 = (bf16[64,8,2,256]{3,1,2,0:T(8,128)(2,1)S(1)}, bf16[64,8,2,256]{3,1,2,0:T(8,128)(2,1)}, u32[]{:S(2)}) copy-start(bf16[64,8,2,256]{3,1,2,0:T(8,128)(2,1)} %copy-done.1) | copy-start | bytes 1572868
  354.7 49.1 %collective-permute-start.23 = (f32[512,512]{0,1:T(8,128)}, f32[512,512]{0,1:T(8,128)}, u32[]{:S(2)}, u32[]{:S(2)}) collective-permute-start(f32[512,512]{0,1:T(8,128)} %fusion.19), channel_id=1, source_target_pairs={{0,0},{1,16},{2,32},{3,48},{4,64},{5,80},{6,96},{7,112},{8,128},{9... | collective-permute-start | bytes 3145736 | tf_op jit(solution)/shard_map/ppermute | solution.py:81
  363.3 42.7 %copy-start.4 = (f32[64,8,2,256]{3,1,2,0:T(8,128)S(1)}, f32[64,8,2,256]{3,1,2,0:T(8,128)}, u32[]{:S(2)}) copy-start(f32[64,8,2,256]{3,1,2,0:T(8,128)} %copy.75) | copy-start | bytes 3145732
